TPU v7x, 256 devices: a whole 4x4x8 slice. The times are simulated.
256 devices in a mesh: gx: 32 (over z, x), gy: 8 (over y, core).
Axes of the slice: x: 4, y: 4, z: 8, core: 2. Of those that a mesh axis runs over, the one named last changes fastest.
Arguments:
- hidden_in: bfloat16 [64, 5120], P(None, 'gx'), may hold values from -60 to 60
- norm1_gain: float32 [5120], P('gx'), may hold values from 0.1 to 1.9
- norm1_bias: float32 [5120], P('gx'), may hold values from -4 to 4
- norm2_gain: float32 [5120], P('gx'), may hold values from 0.1 to 1.9
- norm2_bias: float32 [5120], P('gx'), may hold values from -4 to 4
- w_qkv: bfloat16 [5120, 15360], P('gx', 'gy'), may hold values from -0.078125 to 0.078125
- b_qkv: float32 [15360], P('gy'), may hold values from -4 to 4
- w_out: bfloat16 [5120, 5120], P('gy', 'gx'), may hold values from -0.078125 to 0.078125
- b_out: float32 [5120], P('gx'), may hold values from -4 to 4
- w_up: bfloat16 [5120, 20480], P('gx', 'gy'), may hold values from -0.078125 to 0.078125
- b_up: float32 [20480], P('gy'), may hold values from -4 to 4
- w_down: bfloat16 [20480, 5120], P('gy', 'gx'), may hold values from -0.0390625 to 0.0390625
- b_down: float32 [5120], P('gx'), may hold values from -4 to 4
- key_cache: bfloat16 [64, 40, 1024, 128], P('gx', 'gy'), may hold values from -70 to 70
- value_cache: bfloat16 [64, 40, 1024, 128], P('gx', 'gy'), may hold values from -6 to 6
- lengths: int32 [64], replicated, may hold values from 1 to 1024, 32768 in all
- assignment: int32 [64], replicated, may hold values from 0 to 63, each once
Outputs:
- hidden_out: bfloat16 [64, 5120], P(None, 'gx')
- new_keys: bfloat16 [64, 40, 1024, 128], P('gx', 'gy')
- new_values: bfloat16 [64, 40, 1024, 128], P('gx', 'gy')
Inputs may be any that keep to these rules, and one draw needn't show every extreme that they name: `lengths`: each request's length, the largest exactly 1024. `assignment`: a permutation: every slot holds exactly one request.
All inputs are finite; a program needn't handle non-finite values.
Results may differ from a plain program's by a relative error of at most 0.0068.
Values may be sent and summed in bfloat16 or wider, within the bound.
No kernel may reach another device: no remote copies, remote signals or barrier semaphores. Data moves between devices by JAX's collectives and lax.ppermute only.
A program may use at most 64 MiB of HBM per device.

v0:
```python
import jax
import jax.numpy as jnp
from jax import lax
from jax.sharding import PartitionSpec as P

D = 5120
HD = 128
ROT = 32


def rotate(tensor, position):
    half_rot = ROT // 2
    frequency = 10000.0 ** (-2.0 * jnp.arange(half_rot, dtype=jnp.float32) / ROT)
    angle = position.astype(jnp.float32)[:, None, None] * frequency
    cosine = jnp.cos(angle)
    sine = jnp.sin(angle)
    first_half = tensor[..., :half_rot]
    second_half = tensor[..., half_rot:ROT]
    return jnp.concatenate(
        [
            first_half * cosine - second_half * sine,
            second_half * cosine + first_half * sine,
            tensor[..., ROT:],
        ],
        axis=-1,
    )


def block_scores(query, keys, my_len):
    span_len = keys.shape[2]
    scores = jnp.einsum("shd,shpd->shp", query, keys, preferred_element_type=jnp.float32) * HD ** (
        -0.5
    )
    places = lax.iota(jnp.int32, span_len)
    valid = places[None, None, :] < my_len[:, None, None]
    return (jnp.where(valid, scores, -1e30), valid)


def on_device(
    hidden_in,
    norm1_gain,
    norm1_bias,
    norm2_gain,
    norm2_bias,
    w_qkv,
    b_qkv,
    w_out,
    b_out,
    w_up,
    b_up,
    w_down,
    b_down,
    key_cache,
    value_cache,
    lengths,
    assignment,
):
    requests = hidden_in.shape[0]
    rows_dev = key_cache.shape[0]
    heads_dev = key_cache.shape[1]
    wide_in = hidden_in.astype(jnp.float32)
    sum_rows, sum_squares = lax.psum(
        (jnp.sum(wide_in, axis=1), jnp.sum(wide_in * wide_in, axis=1)), "gx"
    )
    row_mean = sum_rows / D
    row_var = sum_squares / D - row_mean * row_mean
    normed = (wide_in - row_mean[:, None]) * lax.rsqrt(row_var + 1e-05)[:, None]
    attn_in = (normed * norm1_gain + norm1_bias).astype(jnp.bfloat16)
    mlp_in = (normed * norm2_gain + norm2_bias).astype(jnp.bfloat16)
    slot_ids = lax.iota(jnp.int32, requests)
    matches = assignment[:, None] == slot_ids[None, :]
    to_request = matches.astype(jnp.float32)
    attn_slot = jnp.dot(
        matches.T.astype(jnp.bfloat16), attn_in, preferred_element_type=jnp.float32
    ).astype(jnp.bfloat16)
    slot_len = jnp.sum(jnp.where(matches, lengths[:, None], 0), axis=0)
    my_len = lax.dynamic_slice_in_dim(slot_len, lax.axis_index("gx") * rows_dev, rows_dev, 0)
    qkv = (
        lax.psum_scatter(
            jnp.dot(attn_slot, w_qkv, preferred_element_type=jnp.float32),
            "gx",
            scatter_dimension=0,
            tiled=True,
        )
        + b_qkv
    )
    qkv = qkv.reshape(rows_dev, heads_dev, 3, HD)
    position = my_len - 1
    query = rotate(qkv[:, :, 0], position).astype(jnp.bfloat16)
    new_key = rotate(qkv[:, :, 1], position).astype(jnp.bfloat16)
    new_value = qkv[:, :, 2].astype(jnp.bfloat16)
    new_keys = key_cache
    new_values = value_cache
    zero_index = jnp.int32(0)
    for local_slot in range(rows_dev):
        slot_index = jnp.int32(local_slot)
        new_keys = lax.dynamic_update_slice(
            new_keys,
            new_key[local_slot][None, :, None, :],
            (slot_index, zero_index, position[local_slot], zero_index),
        )
        new_values = lax.dynamic_update_slice(
            new_values,
            new_value[local_slot][None, :, None, :],
            (slot_index, zero_index, position[local_slot], zero_index),
        )
    scores, valid = block_scores(query, new_keys, my_len)
    top_score = jnp.max(scores, axis=2)
    weights = jnp.where(valid, jnp.exp(scores - top_score[:, :, None]), 0.0)
    total = jnp.sum(weights, axis=2)
    weights_low = weights.astype(jnp.bfloat16)
    weighted = jnp.einsum(
        "shp,shpd->shd", weights_low, new_values, preferred_element_type=jnp.float32
    )
    attended = (weighted / total[:, :, None]).astype(jnp.bfloat16).reshape(rows_dev, heads_dev * HD)
    slot_part = jnp.dot(
        lax.all_gather(attended, "gx", axis=0, tiled=True),
        w_out,
        preferred_element_type=jnp.float32,
    )
    attn_part = jnp.dot(to_request, slot_part, precision=lax.Precision.HIGHEST)
    up_partial = jnp.dot(mlp_in, w_up, preferred_element_type=jnp.float32)
    up = lax.psum(up_partial, "gx") + b_up
    hidden = jax.nn.gelu(up, approximate=False).astype(jnp.bfloat16)
    mlp_part = jnp.dot(hidden, w_down, preferred_element_type=jnp.float32)
    branches = lax.psum(attn_part + mlp_part, "gy")
    hidden_out = (wide_in + branches + b_out + b_down).astype(jnp.bfloat16)
    return (hidden_out, new_keys, new_values)


def solution(mesh):
    return jax.shard_map(
        on_device,
        mesh=mesh,
        in_specs=(
            P(None, "gx"),
            P("gx"),
            P("gx"),
            P("gx"),
            P("gx"),
            P("gx", "gy"),
            P("gy"),
            P("gy", "gx"),
            P("gx"),
            P("gx", "gy"),
            P("gy"),
            P("gy", "gx"),
            P("gx"),
            P("gx", "gy", None, None),
            P("gx", "gy", None, None),
            P(),
            P(),
        ),
        out_specs=(P(None, "gx"), P("gx", "gy", None, None), P("gx", "gy", None, None)),
        check_vma=False,
    )
```

profile of v0, /device:TPU:16, one launch (start us, length us, event | category | flops | bytes accessed | tf_op | source)
XLA Modules:
  0.0 321.2 jit_solution(3638242814341928627)
XLA Ops:
  7.2 1.8 copy-done.3
  9.0 1.5 copy.66
  10.5 0.1 convert_reduce_fusion
  10.7 77.7 %all-reduce.1 = (f32[64]{0:T(128)S(1)}, f32[64]{0:T(128)S(1)}) all-reduce(f32[64]{0:T(128)S(1)} %get-tuple-element.4, f32[64]{0:T(128)S(1)} %get-tuple-element.3), channel_id=1, replica_groups=mesh['gx'=32,'gy'=8] {'gx'}, use_global_device_ids=true, to_apply=%region_4.5 | all-reduce | flops 128 | bytes 1024 | tf_op jit(solution)/shard_map/psum | solution.py:62
  88.4 1.2 fusion.61
  89.5 2.5 fusion.4
  92.1 0.1 select_reduce_fusion
  92.2 0.1 fusion.118
  92.3 0.6 fusion.122
  95.5 0.6 dynamic-slice
  98.1 0.1 multiply_cosine_fusion
  98.3 139.3 %all-reduce.5.cloned.1.call-done = (f32[64,1920]{1,0:T(8,128)}, f32[64,2560]{1,0:T(8,128)}) async-done(((f32[64,1920]{1,0:T(8,128)}, f32[64,2560]{1,0:T(8,128)}), (f32[64,1920]{1,0:T(8,128)}, f32[64,2560]{1,0:T(8,128)})) %all-reduce.5.cloned.1.call-update) | async-done | bytes 1146896
  237.6 0.8 dynamic-slice_add_fusion
  238.7 0.1 subtract_convert_fusion.1
  238.8 0.1 pad_maximum_fusion
  238.9 1.3 dynamic_update_slice.12
  240.2 0.1 maximum_bitcast_fusion
  240.3 1.3 dynamic_update_slice.13
  241.6 2.5 fusion.84
  244.1 0.1 fusion.3
  244.2 0.1 fusion.119
  244.3 0.1 copy.42
  244.5 0.4 fusion.59
  244.9 0.1 fusion.83
  245.0 0.9 reshape.113
  245.9 41.6 %all-gather = bf16[32,2,640]{2,1,0:T(2,128)(2,1)S(1)} all-gather(bf16[1,2,640]{2,1,0:T(2,128)(2,1)} %reshape.113), channel_id=1, replica_groups=mesh['gx'=32,'gy'=8] {'gx'}, dimensions={0}, use_global_device_ids=true | all-gather | bytes 84480 | tf_op jit(solution)/shard_map/all_gather | solution.py:117
  287.6 0.7 reshape.114
  288.2 1.1 fusion.123
  289.4 0.9 fusion.77
  290.3 3.5 %convolution_add_fusion = f32[64,160]{1,0:T(8,128)} fusion(f32[64,160]{1,0:T(8,128)S(1)} %fusion.77, bf16[2560,160]{0,1:T(8,128)(2,1)} %param.28, f32[64,2560]{1,0:T(8,128)} %get-tuple-element.8, f32[2560]{0:T(1024)} %param.27), kind=kOutput, calls=%fused_computation.1 | convolution fusion | flops 63252480 | bytes 1566720 | tf_op jit(solution)/shard_map/dot_general | solution.py:125
  293.9 19.9 %psum.31 = f32[64,160]{1,0:T(8,128)S(1)} all-reduce(f32[64,160]{1,0:T(8,128)} %convolution_add_fusion), channel_id=1, replica_groups=mesh['gx'=32,'gy'=8] {'gy'}, use_global_device_ids=true, to_apply=%region_9.10 | all-reduce | flops 10240 | bytes 81920 | tf_op jit(solution)/shard_map/psum | solution.py:126
  313.7 0.6 fusion.57
  (45 shorter events, 0.5 us)
Async XLA Ops:
  7.2 81.2 %copy-start = (bf16[160,2560]{1,0:T(8,128)(2,1)S(1)}, bf16[160,2560]{1,0:T(8,128)(2,1)}, u32[]{:S(2)}) copy-start(bf16[160,2560]{1,0:T(8,128)(2,1)} %param.26) | copy-start | bytes 2457604
  7.2 1.8 copy-start.3
  7.2 230.4 %all-reduce.5.cloned.1.call-start = ((), (), s32[]{:S(2)}) async-start(), calls=%async_computation | async-start | bytes 2293760
  9.0 1.5 copy-start.4
  9.0 79.3 %copy-start.7 = (f32[160]{0:T(256)S(1)}, f32[160]{0:T(256)}, u32[]{:S(2)}) copy-start(f32[160]{0:T(256)} %param.21) | copy-start | bytes 1924
  9.0 79.3 %copy-start.8 = (f32[160]{0:T(256)S(1)}, f32[160]{0:T(256)}, u32[]{:S(2)}) copy-start(f32[160]{0:T(256)} %param.20) | copy-start | bytes 1924
  9.0 80.5 %copy-start.6 = (s32[64]{0:T(128)S(1)}, s32[64]{0:T(128)}, u32[]{:S(2)}) copy-start(s32[64]{0:T(128)} %param.33) | copy-start | bytes 772
  9.0 80.5 %copy-start.9 = (f32[160]{0:T(256)S(1)}, f32[160]{0:T(256)}, u32[]{:S(2)}) copy-start(f32[160]{0:T(256)} %param.19) | copy-start | bytes 1924
  9.0 80.5 %copy-start.10 = (f32[160]{0:T(256)S(1)}, f32[160]{0:T(256)}, u32[]{:S(2)}) copy-start(f32[160]{0:T(256)} %param.18) | copy-start | bytes 1924
  10.5 81.6 %copy-start.13 = (s32[64]{0:T(128)S(1)}, s32[64]{0:T(128)}, u32[]{:S(2)}) copy-start(s32[64]{0:T(128)} %param.32) | copy-start | bytes 772
  10.5 85.0 %copy-start.14 = (u32[256]{0:T(256)S(1)}, u32[256]{0:T(256)}, u32[]{:S(2)}) copy-start(u32[256]{0:T(256)} %constant.103) | copy-start | bytes 3076
  10.5 227.1 %copy-start.5 = (f32[1920]{0:T(1024)S(1)}, f32[1920]{0:T(1024)}, u32[]{:S(2)}) copy-start(f32[1920]{0:T(1024)} %param.23) | copy-start | bytes 23044
  89.5 154.9 %copy-start.2 = (bf16[2,5,1024,128]{3,2,1,0:T(8,128)(2,1)S(1)}, bf16[2,5,1024,128]{3,2,1,0:T(8,128)(2,1)}, u32[]{:S(2)}) copy-start(bf16[2,5,1024,128]{3,2,1,0:T(8,128)(2,1)} %param.31) | copy-start | bytes 7864324
  244.5 49.4 %copy-start.1 = (bf16[2,5,1024,128]{3,2,1,0:T(8,128)(2,1)}, bf16[2,5,1024,128]{3,2,1,0:T(8,128)(2,1)S(1)}, u32[]{:S(2)}) copy-start(bf16[2,5,1024,128]{3,2,1,0:T(8,128)(2,1)S(1)} %dynamic_update_slice.15) | copy-start | bytes 7864324
  290.3 23.4 %copy-start.11 = (f32[160]{0:T(256)S(1)}, f32[160]{0:T(256)}, u32[]{:S(2)}) copy-start(f32[160]{0:T(256)} %param.29) | copy-start | bytes 1924
  290.3 23.4 %copy-start.12 = (f32[160]{0:T(256)S(1)}, f32[160]{0:T(256)}, u32[]{:S(2)}) copy-start(f32[160]{0:T(256)} %param.25) | copy-start | bytes 1924
Sparse Core Ops, SparseCore 0:
  92.2 145.3 all-reduce.4
where the time goes:
time: 325 us; the launch traced here: 321 us
  blocking collectives  139 us (43%)
  waiting for transfers between devices  139 us (43%)
  between operations  18.9 us (6%)
  matrix products  12.2 us (4%)
  local copies, waits for them, and re-layouts  9.11 us (3%)
    unnamed x2, waiting for transfers between devices  139 us
    psum x1, blocking collectives, on_device(): lax.psum((jnp.sum(wide_in, axis=1), jnp.sum(wide_in * wide_in, axis=1)),...  77.7 us
    all_gather x1, blocking collectives, on_device(): lax.all_gather(attended, 'gx', axis=0, tiled=True)  41.6 us
    psum x1, blocking collectives, on_device(): branches = lax.psum(attn_part + mlp_part, 'gy')  19.9 us
  transfers between devices with their start and end apart: 1, of which 1 were waited for; matrix products, arithmetic and copies ran while one was open for 0% of the time, Pallas kernels for 0%

commit v1 on v0

--- a/solution.py
+++ b/solution.py
@@ -1,3 +1,5 @@
+import functools
+
 import jax
 import jax.numpy as jnp
 from jax import lax
@@ -34,6 +36,50 @@
     places = lax.iota(jnp.int32, span_len)
     valid = places[None, None, :] < my_len[:, None, None]
     return (jnp.where(valid, scores, -1e30), valid)
+
+
+def xor_pairs(size, bit):
+    return [(i, i ^ (1 << bit)) for i in range(size)]
+
+
+def tree_sum(x, axis, size, bits):
+    for bit in bits:
+        x = x + lax.ppermute(x, axis, xor_pairs(size, bit))
+    return x
+
+
+def tree_scatter_sum(x, axis, size, bits):
+    rows = x.shape[0]
+    me = lax.axis_index(axis)
+    x = x.reshape((2,) * len(bits) + (rows // size,) + x.shape[1:])
+    left = list(range(len(bits) - 1, -1, -1))
+    for bit in bits:
+        at = left.index(bit)
+        mine = (me >> bit) & 1
+        keep = lax.dynamic_index_in_dim(x, mine, at, keepdims=False)
+        send = lax.dynamic_index_in_dim(x, 1 - mine, at, keepdims=False)
+        x = keep + lax.ppermute(send, axis, xor_pairs(size, bit))
+        left.pop(at)
+    return x.reshape((rows // size,) + x.shape[-1:])
+
+
+def tree_gather(x, axis, size, bits):
+    me = lax.axis_index(axis)
+    held = []
+    for bit in bits:
+        other = lax.ppermute(x, axis, xor_pairs(size, bit))
+        low = (me >> bit) & 1 == 0
+        x = jnp.stack([jnp.where(low, x, other), jnp.where(low, other, x)], 0)
+        held.insert(0, bit)
+    count = len(bits)
+    order = [held.index(bit) for bit in range(count - 1, -1, -1)]
+    x = jnp.transpose(x, order + list(range(count, x.ndim)))
+    return x.reshape((size * x.shape[count],) + x.shape[count + 1 :])
+
+
+def bit_order(size, first):
+    bits = [b for b in first if (1 << b) < size]
+    return bits + [b for b in range(size.bit_length() - 1) if b not in bits]
 
 
 def on_device(
@@ -54,14 +100,22 @@
     value_cache,
     lengths,
     assignment,
+    gx_size,
+    gy_size,
 ):
     requests = hidden_in.shape[0]
     rows_dev = key_cache.shape[0]
     heads_dev = key_cache.shape[1]
+    gx_bits = bit_order(gx_size, (0, 2, 1, 3, 4))
+    gy_bits = bit_order(gy_size, (0, 1, 2))
     wide_in = hidden_in.astype(jnp.float32)
-    sum_rows, sum_squares = lax.psum(
-        (jnp.sum(wide_in, axis=1), jnp.sum(wide_in * wide_in, axis=1)), "gx"
-    )
+    stats = tree_sum(
+        jnp.stack([jnp.sum(wide_in, axis=1), jnp.sum(wide_in * wide_in, axis=1)]),
+        "gx",
+        gx_size,
+        gx_bits,
+    )
+    sum_rows, sum_squares = stats[0], stats[1]
     row_mean = sum_rows / D
     row_var = sum_squares / D - row_mean * row_mean
     normed = (wide_in - row_mean[:, None]) * lax.rsqrt(row_var + 1e-05)[:, None]
@@ -70,20 +124,22 @@
     slot_ids = lax.iota(jnp.int32, requests)
     matches = assignment[:, None] == slot_ids[None, :]
     to_request = matches.astype(jnp.float32)
-    attn_slot = jnp.dot(
-        matches.T.astype(jnp.bfloat16), attn_in, preferred_element_type=jnp.float32
-    ).astype(jnp.bfloat16)
+    to_slot = matches.T.astype(jnp.bfloat16)
+    attn_slot = jnp.dot(to_slot, attn_in, preferred_element_type=jnp.float32).astype(jnp.bfloat16)
+    mlp_slot = jnp.dot(to_slot, mlp_in, preferred_element_type=jnp.float32).astype(jnp.bfloat16)
     slot_len = jnp.sum(jnp.where(matches, lengths[:, None], 0), axis=0)
     my_len = lax.dynamic_slice_in_dim(slot_len, lax.axis_index("gx") * rows_dev, rows_dev, 0)
-    qkv = (
-        lax.psum_scatter(
+    qkv_cols = w_qkv.shape[1]
+    partial = jnp.concatenate(
+        [
             jnp.dot(attn_slot, w_qkv, preferred_element_type=jnp.float32),
-            "gx",
-            scatter_dimension=0,
-            tiled=True,
-        )
-        + b_qkv
-    )
+            jnp.dot(mlp_slot, w_up, preferred_element_type=jnp.float32),
+        ],
+        axis=1,
+    )
+    reduced = tree_scatter_sum(partial, "gx", gx_size, gx_bits)
+    qkv = reduced[:, :qkv_cols] + b_qkv
+    up = reduced[:, qkv_cols:] + b_up
     qkv = qkv.reshape(rows_dev, heads_dev, 3, HD)
     position = my_len - 1
     query = rotate(qkv[:, :, 0], position).astype(jnp.bfloat16)
@@ -113,24 +169,24 @@
         "shp,shpd->shd", weights_low, new_values, preferred_element_type=jnp.float32
     )
     attended = (weighted / total[:, :, None]).astype(jnp.bfloat16).reshape(rows_dev, heads_dev * HD)
+    hidden = jax.nn.gelu(up, approximate=False).astype(jnp.bfloat16)
+    gathered = tree_gather(
+        jnp.concatenate([attended, hidden], axis=1), "gx", gx_size, gx_bits[::-1]
+    )
+    attn_cols = attended.shape[1]
     slot_part = jnp.dot(
-        lax.all_gather(attended, "gx", axis=0, tiled=True),
-        w_out,
-        preferred_element_type=jnp.float32,
-    )
-    attn_part = jnp.dot(to_request, slot_part, precision=lax.Precision.HIGHEST)
-    up_partial = jnp.dot(mlp_in, w_up, preferred_element_type=jnp.float32)
-    up = lax.psum(up_partial, "gx") + b_up
-    hidden = jax.nn.gelu(up, approximate=False).astype(jnp.bfloat16)
-    mlp_part = jnp.dot(hidden, w_down, preferred_element_type=jnp.float32)
-    branches = lax.psum(attn_part + mlp_part, "gy")
+        gathered[:, :attn_cols], w_out, preferred_element_type=jnp.float32
+    ) + jnp.dot(gathered[:, attn_cols:], w_down, preferred_element_type=jnp.float32)
+    branches = tree_sum(slot_part, "gy", gy_size, gy_bits)
+    branches = jnp.dot(to_request, branches, precision=lax.Precision.HIGHEST)
     hidden_out = (wide_in + branches + b_out + b_down).astype(jnp.bfloat16)
     return (hidden_out, new_keys, new_values)
 
 
 def solution(mesh):
+    body = functools.partial(on_device, gx_size=mesh.shape["gx"], gy_size=mesh.shape["gy"])
     return jax.shard_map(
-        on_device,
+        body,
         mesh=mesh,
         in_specs=(
             P(None, "gx"),

time: 325 us -> 144 us (0.44)
  blocking collectives: 139 us -> 0 us
  waiting for transfers between devices: 139 us -> 60.1 us
  starting transfers between devices: 0.04 us -> 40.7 us
  between operations: 18.9 us -> 4.94 us
  other arithmetic: 2.53 us -> 15.2 us
  local copies, waits for them, and re-layouts: 9.11 us -> 14.6 us
  matrix products: 12.2 us -> 7.55 us
    unnamed x2 -> x0, waiting for transfers between devices: 139 us -> none
    psum x2 -> x0, blocking collectives: 97.5 us -> none  [the longest x1 77.7 us: on_device(): lax.psum((jnp.sum(wide_in, axis=1), jnp.sum(wide_in * wide_in, axis=1)),...]
    ppermute x0 -> x18, waiting for transfers between devices: none -> 60.1 us  [the longest x5 21.5 us: tree_gather(): other = lax.ppermute(x, axis, xor_pairs(size, bit))]
    all_gather x1 -> x0, blocking collectives: 41.6 us -> none  [on_device(): lax.all_gather(attended, 'gx', axis=0, tiled=True)]
    ppermute x0 -> x18, starting transfers between devices: none -> 40.7 us  [the longest x8 18.7 us: tree_sum(): x = x + lax.ppermute(x, axis, xor_pairs(size, bit))]
    another operation x2 -> x12, other arithmetic: 0.09 us -> 6.15 us  [the longest x9 5.38 us: tree_gather(): x = jnp.stack([jnp.where(low, x, other), jnp.where(low, other, x)], 0)]
    unnamed x34 -> x42, local copies, waits for them, and re-layouts: 5.48 us -> 6.9 us
  transfers between devices with their start and end apart: 1 -> 18, of which waited for: 1 -> 17; matrix products, arithmetic and copies ran while one was open for 0% -> 2% of each run, Pallas kernels for 0% -> 0%
where the time goes in v1:
time: 144 us; the launch traced here: 143 us
  waiting for transfers between devices  60.1 us (42%)
  starting transfers between devices  40.7 us (28%)
  other arithmetic  15.2 us (11%)
  local copies, waits for them, and re-layouts  14.6 us (10%)
  matrix products  7.55 us (5%)
  between operations  4.94 us (3%)
    ppermute x5, waiting for transfers between devices, tree_gather(): other = lax.ppermute(x, axis, xor_pairs(size, bit))  21.5 us
    ppermute x5, waiting for transfers between devices, tree_scatter_sum(): x = keep + lax.ppermute(send, axis, xor_pairs(size, bit))  20.1 us
    ppermute x8, starting transfers between devices, tree_sum(): x = x + lax.ppermute(x, axis, xor_pairs(size, bit))  18.7 us
    ppermute x8, waiting for transfers between devices, tree_sum(): x = x + lax.ppermute(x, axis, xor_pairs(size, bit))  18.5 us
    ppermute x5, starting transfers between devices, tree_scatter_sum(): x = keep + lax.ppermute(send, axis, xor_pairs(size, bit))  13.3 us
    ppermute x5, starting transfers between devices, tree_gather(): other = lax.ppermute(x, axis, xor_pairs(size, bit))  8.64 us
    unnamed x42, local copies, waits for them, and re-layouts  6.9 us
    another operation x9, other arithmetic, tree_gather(): x = jnp.stack([jnp.where(low, x, other), jnp.where(low, other, x)], 0)  5.38 us
  transfers between devices with their start and end apart: 18, of which 17 were waited for; matrix products, arithmetic and copies ran while one was open for 2% of the time, Pallas kernels for 0%

profile of v1, /device:TPU:16, one launch (start us, length us, event | category | flops | bytes accessed | tf_op | source)
XLA Modules:
  0.0 143.1 jit_solution(16426811336521270966)
XLA Ops:
  0.6 3.5 %copy.93 = bf16[2,5,1024,128]{3,2,1,0:T(8,128)(2,1)} copy(bf16[2,5,1024,128]{3,2,1,0:T(8,128)(2,1)} %param.30) | data formatting | bytes 5242880
  5.0 1.6 %collective-permute-start = (f32[2,64]{1,0:T(2,128)S(1)}, f32[2,64]{1,0:T(2,128)S(1)}, u32[]{:S(2)}, u32[]{:S(2)}) collective-permute-start(f32[2,64]{1,0:T(2,128)S(1)} %pad_maximum_fusion.7), channel_id=1, source_target_pairs={{0,8},{8,0},{16,24},{24,16},{32,40},{40,32},{48,56},{56,48},{64,72... | collective-permute-start | bytes 1544 | tf_op jit(solution)/shard_map/ppermute | solution.py:47
  6.6 2.1 %collective-permute-done = f32[2,64]{1,0:T(2,128)S(1)} collective-permute-done((f32[2,64]{1,0:T(2,128)S(1)}, f32[2,64]{1,0:T(2,128)S(1)}, u32[]{:S(2)}, u32[]{:S(2)}) %collective-permute-start) | collective-permute-done | bytes 544 | tf_op jit(solution)/shard_map/ppermute | solution.py:47
  8.7 2.0 %collective-permute-start.1 = (f32[2,64]{1,0:T(2,128)S(1)}, f32[2,64]{1,0:T(2,128)S(1)}, u32[]{:S(2)}, u32[]{:S(2)}) collective-permute-start(f32[2,64]{1,0:T(2,128)S(1)} %fusion.75), channel_id=1, source_target_pairs={{0,32},{8,40},{16,48},{24,56},{32,0},{40,8},{48,16},{56,24},{64,96... | collective-permute-start | bytes 1544 | tf_op jit(solution)/shard_map/ppermute | solution.py:47
  10.7 1.7 %collective-permute-done.1 = f32[2,64]{1,0:T(2,128)S(1)} collective-permute-done((f32[2,64]{1,0:T(2,128)S(1)}, f32[2,64]{1,0:T(2,128)S(1)}, u32[]{:S(2)}, u32[]{:S(2)}) %collective-permute-start.1) | collective-permute-done | bytes 544 | tf_op jit(solution)/shard_map/ppermute | solution.py:47
  12.4 3.1 %collective-permute-start.2 = (f32[2,64]{1,0:T(2,128)S(1)}, f32[2,64]{1,0:T(2,128)S(1)}, u32[]{:S(2)}, u32[]{:S(2)}) collective-permute-start(f32[2,64]{1,0:T(2,128)S(1)} %fusion.85), channel_id=1, source_target_pairs={{0,16},{8,24},{16,0},{24,8},{32,48},{40,56},{48,32},{56,40},{64,80... | collective-permute-start | bytes 1544 | tf_op jit(solution)/shard_map/ppermute | solution.py:47
  15.5 2.1 %collective-permute-done.2 = f32[2,64]{1,0:T(2,128)S(1)} collective-permute-done((f32[2,64]{1,0:T(2,128)S(1)}, f32[2,64]{1,0:T(2,128)S(1)}, u32[]{:S(2)}, u32[]{:S(2)}) %collective-permute-start.2) | collective-permute-done | bytes 544 | tf_op jit(solution)/shard_map/ppermute | solution.py:47
  17.6 3.3 %collective-permute-start.3 = (f32[2,64]{1,0:T(2,128)S(1)}, f32[2,64]{1,0:T(2,128)S(1)}, u32[]{:S(2)}, u32[]{:S(2)}) collective-permute-start(f32[2,64]{1,0:T(2,128)S(1)} %add.164), channel_id=1, source_target_pairs={{0,64},{8,72},{16,80},{24,88},{32,96},{40,104},{48,112},{56,120},{... | collective-permute-start | bytes 1544 | tf_op jit(solution)/shard_map/ppermute | solution.py:47
  20.8 1.6 %collective-permute-done.3 = f32[2,64]{1,0:T(2,128)S(1)} collective-permute-done((f32[2,64]{1,0:T(2,128)S(1)}, f32[2,64]{1,0:T(2,128)S(1)}, u32[]{:S(2)}, u32[]{:S(2)}) %collective-permute-start.3) | collective-permute-done | bytes 544 | tf_op jit(solution)/shard_map/ppermute | solution.py:47
  22.4 6.8 %collective-permute-start.4 = (f32[2,64]{1,0:T(2,128)S(1)}, f32[2,64]{1,0:T(2,128)S(1)}, u32[]{:S(2)}, u32[]{:S(2)}) collective-permute-start(f32[2,64]{1,0:T(2,128)S(1)} %add.165), channel_id=1, source_target_pairs={{0,128},{8,136},{16,144},{24,152},{32,160},{40,168},{48,176},{56,1... | collective-permute-start | bytes 1544 | tf_op jit(solution)/shard_map/ppermute | solution.py:47
  29.2 1.6 %collective-permute-done.4 = f32[2,64]{1,0:T(2,128)S(1)} collective-permute-done((f32[2,64]{1,0:T(2,128)S(1)}, f32[2,64]{1,0:T(2,128)S(1)}, u32[]{:S(2)}, u32[]{:S(2)}) %collective-permute-start.4) | collective-permute-done | bytes 544 | tf_op jit(solution)/shard_map/ppermute | solution.py:47
  32.7 1.6 %collective-permute-start.5 = (f32[2,2,2,2,2,4480]{5,4,3,2,1,0:T(2,128)S(1)}, f32[2,2,2,2,2,4480]{5,4,3,2,1,0:T(2,128)S(1)}, u32[]{:S(2)}, u32[]{:S(2)}) collective-permute-start(f32[2,2,2,2,2,4480]{5,4,3,2,1,0:T(2,128)S(1)} %dynamic-slice_bitcast_fusion), channel_id=1, source_target_pairs={{0,8},{8,0},{16,24},{24,16},{32,40},{40,32},{48,56},{56,48},{64,72... | collective-permute-start | bytes 1720328 | tf_op jit(solution)/shard_map/ppermute | solution.py:61
  34.4 8.1 %collective-permute-done.5 = f32[2,2,2,2,2,4480]{5,4,3,2,1,0:T(2,128)S(1)} collective-permute-done((f32[2,2,2,2,2,4480]{5,4,3,2,1,0:T(2,128)S(1)}, f32[2,2,2,2,2,4480]{5,4,3,2,1,0:T(2,128)S(1)}, u32[]{:S(2)}, u32[]{:S(2)}) %collective-permute-start.5) | collective-permute-done | bytes 573472 | tf_op jit(solution)/shard_map/ppermute | solution.py:61
  45.3 4.3 %collective-permute-done.6 = f32[2,2,2,2,4480]{4,3,2,1,0:T(2,128)S(1)} collective-permute-done((f32[2,2,2,2,4480]{4,3,2,1,0:T(2,128)S(1)}, f32[2,2,2,2,4480]{4,3,2,1,0:T(2,128)S(1)}, u32[]{:S(2)}, u32[]{:S(2)}) %collective-permute-start.6) | collective-permute-done | bytes 286752 | tf_op jit(solution)/shard_map/ppermute | solution.py:61
  51.1 3.0 %collective-permute-start.7 = (f32[2,2,2,4480]{3,2,1,0:T(2,128)}, f32[2,2,2,4480]{3,2,1,0:T(2,128)}, u32[]{:S(2)}, u32[]{:S(2)}) collective-permute-start(f32[2,2,2,4480]{3,2,1,0:T(2,128)} %dynamic-slice_bitcast_fusion.2), channel_id=1, source_target_pairs={{0,16},{8,24},{16,0},{24,8},{32,48},{40,56},{48,32},{56,40},{64,80... | collective-permute-start | bytes 430088 | tf_op jit(solution)/shard_map/ppermute | solution.py:61
  54.1 3.9 %collective-permute-done.7 = f32[2,2,2,4480]{3,2,1,0:T(2,128)} collective-permute-done((f32[2,2,2,4480]{3,2,1,0:T(2,128)}, f32[2,2,2,4480]{3,2,1,0:T(2,128)}, u32[]{:S(2)}, u32[]{:S(2)}) %collective-permute-start.7) | collective-permute-done | bytes 143392 | tf_op jit(solution)/shard_map/ppermute | solution.py:61
  59.7 2.0 %collective-permute-start.8 = (f32[2,2,4480]{2,1,0:T(2,128)S(1)}, f32[2,2,4480]{2,1,0:T(2,128)}, u32[]{:S(2)}, u32[]{:S(2)}) collective-permute-start(f32[2,2,4480]{2,1,0:T(2,128)S(1)} %dynamic-slice_bitcast_fusion.3), channel_id=1, source_target_pairs={{0,64},{8,72},{16,80},{24,88},{32,96},{40,104},{48,112},{56,120},{... | collective-permute-start | bytes 215048 | tf_op jit(solution)/shard_map/ppermute | solution.py:61
  62.5 3.8 %collective-permute-done.8 = f32[2,2,4480]{2,1,0:T(2,128)} collective-permute-done((f32[2,2,4480]{2,1,0:T(2,128)S(1)}, f32[2,2,4480]{2,1,0:T(2,128)}, u32[]{:S(2)}, u32[]{:S(2)}) %collective-permute-start.8) | collective-permute-done | bytes 71712 | tf_op jit(solution)/shard_map/ppermute | solution.py:61
  67.2 5.6 %collective-permute-start.9 = (f32[2,4480]{1,0:T(2,128)S(1)}, f32[2,4480]{1,0:T(2,128)}, u32[]{:S(2)}, u32[]{:S(2)}) collective-permute-start(f32[2,4480]{1,0:T(2,128)S(1)} %dynamic-slice_bitcast_fusion.4), channel_id=1, source_target_pairs={{0,128},{8,136},{16,144},{24,152},{32,160},{40,168},{48,176},{56,1... | collective-permute-start | bytes 107528 | tf_op jit(solution)/shard_map/ppermute | solution.py:61
  84.3 2.5 %fusion.67 = f32[2,5,1,1024]{3,2,1,0:T(1,128)S(1)} fusion(bf16[2,5,1024,128]{3,2,1,0:T(8,128)(2,1)} %dynamic_update_slice.13, bf16[2,5,128,1]{2,0,1,3:T(2,128)(2,1)S(1)} %maximum_bitcast_fusion.1), kind=kOutput, calls=%fused_computation.103 | convolution fusion | flops 2621440 | bytes 2664960 | tf_op jit(solution)/shard_map/shd,shpd->shp/dot_general | solution.py:33
  87.8 2.9 %collective-permute-start.10 = (bf16[2,3200]{1,0:T(2,128)(2,1)S(1)}, bf16[2,3200]{1,0:T(2,128)(2,1)S(1)}, u32[]{:S(2)}, u32[]{:S(2)}) collective-permute-start(bf16[2,3200]{1,0:T(2,128)(2,1)S(1)} %pad_maximum_fusion.5), channel_id=1, source_target_pairs={{0,128},{8,136},{16,144},{24,152},{32,160},{40,168},{48,176},{56,1... | collective-permute-start | bytes 38408 | tf_op jit(solution)/shard_map/ppermute | solution.py:70
  90.6 4.8 %collective-permute-done.10 = bf16[2,3200]{1,0:T(2,128)(2,1)S(1)} collective-permute-done((bf16[2,3200]{1,0:T(2,128)(2,1)S(1)}, bf16[2,3200]{1,0:T(2,128)(2,1)S(1)}, u32[]{:S(2)}, u32[]{:S(2)}) %collective-permute-start.10) | collective-permute-done | bytes 12832 | tf_op jit(solution)/shard_map/ppermute | solution.py:70
  96.4 4.1 %collective-permute-done.11 = bf16[2,2,3200]{2,1,0:T(2,128)(2,1)} collective-permute-done((bf16[2,2,3200]{2,1,0:T(2,128)(2,1)S(1)}, bf16[2,2,3200]{2,1,0:T(2,128)(2,1)}, u32[]{:S(2)}, u32[]{:S(2)}) %collective-permute-start.11) | collective-permute-done | bytes 25632 | tf_op jit(solution)/shard_map/ppermute | solution.py:70
  102.0 3.0 %collective-permute-start.12 = (bf16[2,2,2,3200]{3,2,0,1:T(2,128)(2,1)}, bf16[2,2,2,3200]{3,2,0,1:T(2,128)(2,1)S(1)}, u32[]{:S(2)}, u32[]{:S(2)}) collective-permute-start(bf16[2,2,2,3200]{3,2,0,1:T(2,128)(2,1)} %pad_maximum_fusion.3), channel_id=1, source_target_pairs={{0,16},{8,24},{16,0},{24,8},{32,48},{40,56},{48,32},{56,40},{64,80... | collective-permute-start | bytes 153608 | tf_op jit(solution)/shard_map/ppermute | solution.py:70
  105.0 3.3 %collective-permute-done.12 = bf16[2,2,2,3200]{3,2,0,1:T(2,128)(2,1)S(1)} collective-permute-done((bf16[2,2,2,3200]{3,2,0,1:T(2,128)(2,1)}, bf16[2,2,2,3200]{3,2,0,1:T(2,128)(2,1)S(1)}, u32[]{:S(2)}, u32[]{:S(2)}) %collective-permute-start.12) | collective-permute-done | bytes 51232 | tf_op jit(solution)/shard_map/ppermute | solution.py:70
  109.8 4.5 %collective-permute-done.13 = bf16[2,2,2,2,3200]{4,3,0,1,2:T(2,128)(2,1)} collective-permute-done((bf16[2,2,2,2,3200]{4,3,0,1,2:T(2,128)(2,1)S(1)}, bf16[2,2,2,2,3200]{4,3,0,1,2:T(2,128)(2,1)}, u32[]{:S(2)}, u32[]{:S(2)}) %collective-permute-start.13) | collective-permute-done | bytes 102432 | tf_op jit(solution)/shard_map/ppermute | solution.py:70
  118.4 4.8 %collective-permute-done.14 = bf16[2,2,2,2,2,3200]{5,4,1,0,2,3:T(2,128)(2,1)} collective-permute-done((bf16[2,2,2,2,2,3200]{5,4,1,0,2,3:T(2,128)(2,1)}, bf16[2,2,2,2,2,3200]{5,4,1,0,2,3:T(2,128)(2,1)}, u32[]{:S(2)}, u32[]{:S(2)}) %collective-permute-start.14) | collective-permute-done | bytes 204832 | tf_op jit(solution)/shard_map/ppermute | solution.py:70
  123.1 1.5 %fusion.10 = (bf16[1,2,2,2,2,2,3200]{6,5,0,2,1,3,4:T(2,128)(2,1)S(1)}, bf16[1,2,2,2,2,2,3200]{6,5,0,2,1,3,4:T(2,128)(2,1)S(1)}) fusion(bf16[2,2,2,2,2,3200]{5,4,1,0,2,3:T(2,128)(2,1)} %collective-permute-done.14, pred[]{:T(512)S(6)} %eq.31, bf16[1,2,2,2,2,3200]{5,4,1,0,2,3:T(2,128)(2,1)} %copy-done.4, bf16[1,2,2,2,2,3200]{5,4,1,0,2,3:T(2,128)(2,1)S(1)} %get-tuple-element.9), kind=kLoop, calls=%fused_computation.22 | loop fusion | flops 307200 | bytes 819201 | tf_op jit(solution)/shard_map/stack | solution.py:72
  125.9 1.9 %reshape.139 = bf16[64,3200]{1,0:T(8,128)(2,1)} reshape(bf16[2,2,2,2,2,2,3200]{6,5,4,3,2,1,0:T(2,128)(2,1)} %maximum_bitcast_fusion) | data formatting | bytes 819200 | tf_op jit(solution)/shard_map/reshape | solution.py:77
  129.0 1.6 %convolution_add_fusion.1 = f32[64,160]{1,0:T(8,128)S(1)} fusion(f32[64,160]{1,0:T(8,128)S(1)} %fusion.14, bf16[2560,160]{0,1:T(8,128)(2,1)} %param.28, bf16[64,3200]{1,0:T(8,128)(2,1)} %reshape.139), kind=kOutput, calls=%fused_computation.5 | convolution fusion | flops 52439040 | bytes 1228800 | tf_op jit(solution)/shard_map/dot_general | solution.py:179
  133.4 3.0 %collective-permute-done.16 = f32[64,160]{1,0:T(8,128)S(1)} collective-permute-done((f32[64,160]{1,0:T(8,128)S(1)}, f32[64,160]{1,0:T(8,128)S(1)}, u32[]{:S(2)}, u32[]{:S(2)}) %collective-permute-start.16) | collective-permute-done | bytes 40992 | tf_op jit(solution)/shard_map/ppermute | solution.py:47
  136.8 5.4 %collective-permute-done.17 = f32[64,160]{1,0:T(8,128)S(1)} collective-permute-done((f32[64,160]{1,0:T(8,128)S(1)}, f32[64,160]{1,0:T(8,128)S(1)}, u32[]{:S(2)}, u32[]{:S(2)}) %collective-permute-start.17) | collective-permute-done | bytes 40992 | tf_op jit(solution)/shard_map/ppermute | solution.py:47
  (116 shorter events, 33.3 us)
Async XLA Ops:
  0.6 30.7 %copy-start = (bf16[160,2560]{1,0:T(8,128)(2,1)S(1)}, bf16[160,2560]{1,0:T(8,128)(2,1)}, u32[]{:S(2)}) copy-start(bf16[160,2560]{1,0:T(8,128)(2,1)} %param.26) | copy-start | bytes 2457604
  4.2 26.7 %copy-start.5 = (bf16[160,1920]{1,0:T(8,128)(2,1)S(1)}, bf16[160,1920]{1,0:T(8,128)(2,1)}, u32[]{:S(2)}) copy-start(bf16[160,1920]{1,0:T(8,128)(2,1)} %param.22) | copy-start | bytes 1843204
  4.2 26.7 %copy-start.11 = (s32[64]{0:T(128)S(1)}, s32[64]{0:T(128)}, u32[]{:S(2)}) copy-start(s32[64]{0:T(128)} %param.33) | copy-start | bytes 772
  4.2 26.7 %copy-start.13 = (f32[160]{0:T(256)S(1)}, f32[160]{0:T(256)}, u32[]{:S(2)}) copy-start(f32[160]{0:T(256)} %param.19) | copy-start | bytes 1924
  4.2 26.7 %copy-start.14 = (f32[160]{0:T(256)S(1)}, f32[160]{0:T(256)}, u32[]{:S(2)}) copy-start(f32[160]{0:T(256)} %param.18) | copy-start | bytes 1924
  4.2 27.2 %copy-start.15 = (f32[160]{0:T(256)S(1)}, f32[160]{0:T(256)}, u32[]{:S(2)}) copy-start(f32[160]{0:T(256)} %param.21) | copy-start | bytes 1924
  4.2 27.2 %copy-start.16 = (f32[160]{0:T(256)S(1)}, f32[160]{0:T(256)}, u32[]{:S(2)}) copy-start(f32[160]{0:T(256)} %param.20) | copy-start | bytes 1924
  5.0 3.7 %collective-permute-start = (f32[2,64]{1,0:T(2,128)S(1)}, f32[2,64]{1,0:T(2,128)S(1)}, u32[]{:S(2)}, u32[]{:S(2)}) collective-permute-start(f32[2,64]{1,0:T(2,128)S(1)} %pad_maximum_fusion.7), channel_id=1, source_target_pairs={{0,8},{8,0},{16,24},{24,16},{32,40},{40,32},{48,56},{56,48},{64,72... | collective-permute-start | bytes 1544 | tf_op jit(solution)/shard_map/ppermute | solution.py:47
  8.7 3.7 %collective-permute-start.1 = (f32[2,64]{1,0:T(2,128)S(1)}, f32[2,64]{1,0:T(2,128)S(1)}, u32[]{:S(2)}, u32[]{:S(2)}) collective-permute-start(f32[2,64]{1,0:T(2,128)S(1)} %fusion.75), channel_id=1, source_target_pairs={{0,32},{8,40},{16,48},{24,56},{32,0},{40,8},{48,16},{56,24},{64,96... | collective-permute-start | bytes 1544 | tf_op jit(solution)/shard_map/ppermute | solution.py:47
  12.4 5.2 %collective-permute-start.2 = (f32[2,64]{1,0:T(2,128)S(1)}, f32[2,64]{1,0:T(2,128)S(1)}, u32[]{:S(2)}, u32[]{:S(2)}) collective-permute-start(f32[2,64]{1,0:T(2,128)S(1)} %fusion.85), channel_id=1, source_target_pairs={{0,16},{8,24},{16,0},{24,8},{32,48},{40,56},{48,32},{56,40},{64,80... | collective-permute-start | bytes 1544 | tf_op jit(solution)/shard_map/ppermute | solution.py:47
  17.6 4.8 %collective-permute-start.3 = (f32[2,64]{1,0:T(2,128)S(1)}, f32[2,64]{1,0:T(2,128)S(1)}, u32[]{:S(2)}, u32[]{:S(2)}) collective-permute-start(f32[2,64]{1,0:T(2,128)S(1)} %add.164), channel_id=1, source_target_pairs={{0,64},{8,72},{16,80},{24,88},{32,96},{40,104},{48,112},{56,120},{... | collective-permute-start | bytes 1544 | tf_op jit(solution)/shard_map/ppermute | solution.py:47
  22.4 8.4 %collective-permute-start.4 = (f32[2,64]{1,0:T(2,128)S(1)}, f32[2,64]{1,0:T(2,128)S(1)}, u32[]{:S(2)}, u32[]{:S(2)}) collective-permute-start(f32[2,64]{1,0:T(2,128)S(1)} %add.165), channel_id=1, source_target_pairs={{0,128},{8,136},{16,144},{24,152},{32,160},{40,168},{48,176},{56,1... | collective-permute-start | bytes 1544 | tf_op jit(solution)/shard_map/ppermute | solution.py:47
  31.9 2.4 %copy-start.19 = (s32[64]{0:T(128)S(1)}, s32[64]{0:T(128)}, u32[]{:S(2)}) copy-start(s32[64]{0:T(128)} %param.32) | copy-start | bytes 772
  32.7 9.8 %collective-permute-start.5 = (f32[2,2,2,2,2,4480]{5,4,3,2,1,0:T(2,128)S(1)}, f32[2,2,2,2,2,4480]{5,4,3,2,1,0:T(2,128)S(1)}, u32[]{:S(2)}, u32[]{:S(2)}) collective-permute-start(f32[2,2,2,2,2,4480]{5,4,3,2,1,0:T(2,128)S(1)} %dynamic-slice_bitcast_fusion), channel_id=1, source_target_pairs={{0,8},{8,0},{16,24},{24,16},{32,40},{40,32},{48,56},{56,48},{64,72... | collective-permute-start | bytes 1720328 | tf_op jit(solution)/shard_map/ppermute | solution.py:61
  42.8 6.7 %collective-permute-start.6 = (f32[2,2,2,2,4480]{4,3,2,1,0:T(2,128)S(1)}, f32[2,2,2,2,4480]{4,3,2,1,0:T(2,128)S(1)}, u32[]{:S(2)}, u32[]{:S(2)}) collective-permute-start(f32[2,2,2,2,4480]{4,3,2,1,0:T(2,128)S(1)} %dynamic-slice_bitcast_fusion.1), channel_id=1, source_target_pairs={{0,32},{8,40},{16,48},{24,56},{32,0},{40,8},{48,16},{56,24},{64,96... | collective-permute-start | bytes 860168 | tf_op jit(solution)/shard_map/ppermute | solution.py:61
  45.3 41.9 %copy-start.2 = (bf16[2,5,1024,128]{3,2,1,0:T(8,128)(2,1)S(1)}, bf16[2,5,1024,128]{3,2,1,0:T(8,128)(2,1)}, u32[]{:S(2)}) copy-start(bf16[2,5,1024,128]{3,2,1,0:T(8,128)(2,1)} %param.31) | copy-start | bytes 7864324
  51.1 6.9 %collective-permute-start.7 = (f32[2,2,2,4480]{3,2,1,0:T(2,128)}, f32[2,2,2,4480]{3,2,1,0:T(2,128)}, u32[]{:S(2)}, u32[]{:S(2)}) collective-permute-start(f32[2,2,2,4480]{3,2,1,0:T(2,128)} %dynamic-slice_bitcast_fusion.2), channel_id=1, source_target_pairs={{0,16},{8,24},{16,0},{24,8},{32,48},{40,56},{48,32},{56,40},{64,80... | collective-permute-start | bytes 430088 | tf_op jit(solution)/shard_map/ppermute | solution.py:61
  59.7 6.5 %collective-permute-start.8 = (f32[2,2,4480]{2,1,0:T(2,128)S(1)}, f32[2,2,4480]{2,1,0:T(2,128)}, u32[]{:S(2)}, u32[]{:S(2)}) collective-permute-start(f32[2,2,4480]{2,1,0:T(2,128)S(1)} %dynamic-slice_bitcast_fusion.3), channel_id=1, source_target_pairs={{0,64},{8,72},{16,80},{24,88},{32,96},{40,104},{48,112},{56,120},{... | collective-permute-start | bytes 215048 | tf_op jit(solution)/shard_map/ppermute | solution.py:61
  67.2 10.8 %collective-permute-start.9 = (f32[2,4480]{1,0:T(2,128)S(1)}, f32[2,4480]{1,0:T(2,128)}, u32[]{:S(2)}, u32[]{:S(2)}) collective-permute-start(f32[2,4480]{1,0:T(2,128)S(1)} %dynamic-slice_bitcast_fusion.4), channel_id=1, source_target_pairs={{0,128},{8,136},{16,144},{24,152},{32,160},{40,168},{48,176},{56,1... | collective-permute-start | bytes 107528 | tf_op jit(solution)/shard_map/ppermute | solution.py:61
  78.8 8.0 %copy-start.12 = (pred[2,1024]{1,0:T(4,128)(4,1)S(1)}, pred[2,1024]{1,0:T(4,128)(4,1)}, u32[]{:S(2)}) copy-start(pred[2,1024]{1,0:T(4,128)(4,1)} %iota_compare_fusion.6) | copy-start | bytes 6148
  87.2 38.7 %copy-start.1 = (bf16[2,5,1024,128]{3,2,1,0:T(8,128)(2,1)}, bf16[2,5,1024,128]{3,2,1,0:T(8,128)(2,1)S(1)}, u32[]{:S(2)}) copy-start(bf16[2,5,1024,128]{3,2,1,0:T(8,128)(2,1)S(1)} %dynamic_update_slice.15) | copy-start | bytes 7864324
  87.8 7.7 %collective-permute-start.10 = (bf16[2,3200]{1,0:T(2,128)(2,1)S(1)}, bf16[2,3200]{1,0:T(2,128)(2,1)S(1)}, u32[]{:S(2)}, u32[]{:S(2)}) collective-permute-start(bf16[2,3200]{1,0:T(2,128)(2,1)S(1)} %pad_maximum_fusion.5), channel_id=1, source_target_pairs={{0,128},{8,136},{16,144},{24,152},{32,160},{40,168},{48,176},{56,1... | collective-permute-start | bytes 38408 | tf_op jit(solution)/shard_map/ppermute | solution.py:70
  95.5 5.0 %collective-permute-start.11 = (bf16[2,2,3200]{2,1,0:T(2,128)(2,1)S(1)}, bf16[2,2,3200]{2,1,0:T(2,128)(2,1)}, u32[]{:S(2)}, u32[]{:S(2)}) collective-permute-start(bf16[2,2,3200]{2,1,0:T(2,128)(2,1)S(1)} %pad_maximum_fusion.4), channel_id=1, source_target_pairs={{0,64},{8,72},{16,80},{24,88},{32,96},{40,104},{48,112},{56,120},{... | collective-permute-start | bytes 76808 | tf_op jit(solution)/shard_map/ppermute | solution.py:70
  102.0 6.4 %collective-permute-start.12 = (bf16[2,2,2,3200]{3,2,0,1:T(2,128)(2,1)}, bf16[2,2,2,3200]{3,2,0,1:T(2,128)(2,1)S(1)}, u32[]{:S(2)}, u32[]{:S(2)}) collective-permute-start(bf16[2,2,2,3200]{3,2,0,1:T(2,128)(2,1)} %pad_maximum_fusion.3), channel_id=1, source_target_pairs={{0,16},{8,24},{16,0},{24,8},{32,48},{40,56},{48,32},{56,40},{64,80... | collective-permute-start | bytes 153608 | tf_op jit(solution)/shard_map/ppermute | solution.py:70
  109.3 5.0 %collective-permute-start.13 = (bf16[2,2,2,2,3200]{4,3,0,1,2:T(2,128)(2,1)S(1)}, bf16[2,2,2,2,3200]{4,3,0,1,2:T(2,128)(2,1)}, u32[]{:S(2)}, u32[]{:S(2)}) collective-permute-start(bf16[2,2,2,2,3200]{4,3,0,1,2:T(2,128)(2,1)S(1)} %pad_maximum_fusion.2), channel_id=1, source_target_pairs={{0,32},{8,40},{16,48},{24,56},{32,0},{40,8},{48,16},{56,24},{64,96... | collective-permute-start | bytes 307208 | tf_op jit(solution)/shard_map/ppermute | solution.py:70
  109.8 32.4 %copy-start.17 = (f32[160]{0:T(256)S(1)}, f32[160]{0:T(256)}, u32[]{:S(2)}) copy-start(f32[160]{0:T(256)} %param.29) | copy-start | bytes 1924
  109.8 32.4 %copy-start.18 = (f32[160]{0:T(256)S(1)}, f32[160]{0:T(256)}, u32[]{:S(2)}) copy-start(f32[160]{0:T(256)} %param.25) | copy-start | bytes 1924
  117.1 6.1 %collective-permute-start.14 = (bf16[2,2,2,2,2,3200]{5,4,1,0,2,3:T(2,128)(2,1)}, bf16[2,2,2,2,2,3200]{5,4,1,0,2,3:T(2,128)(2,1)}, u32[]{:S(2)}, u32[]{:S(2)}) collective-permute-start(bf16[2,2,2,2,2,3200]{5,4,1,0,2,3:T(2,128)(2,1)} %pad_maximum_fusion.1), channel_id=1, source_target_pairs={{0,8},{8,0},{16,24},{24,16},{32,40},{40,32},{48,56},{56,48},{64,72... | collective-permute-start | bytes 614408 | tf_op jit(solution)/shard_map/ppermute | solution.py:70
  124.6 17.6 %copy-start.8 = (bf16[64,160]{1,0:T(8,128)(2,1)S(1)}, bf16[64,160]{1,0:T(8,128)(2,1)}, u32[]{:S(2)}) copy-start(bf16[64,160]{1,0:T(8,128)(2,1)} %param.17) | copy-start | bytes 61444
  130.7 1.3 collective-permute-start.15
  132.0 4.4 %collective-permute-start.16 = (f32[64,160]{1,0:T(8,128)S(1)}, f32[64,160]{1,0:T(8,128)S(1)}, u32[]{:S(2)}, u32[]{:S(2)}) collective-permute-start(f32[64,160]{1,0:T(8,128)S(1)} %add.197), channel_id=1, source_target_pairs={{0,2},{1,3},{2,0},{3,1},{4,6},{5,7},{6,4},{7,5},{8,10},{9,11},{10,... | collective-permute-start | bytes 122888 | tf_op jit(solution)/shard_map/ppermute | solution.py:47
  136.4 5.9 %collective-permute-start.17 = (f32[64,160]{1,0:T(8,128)S(1)}, f32[64,160]{1,0:T(8,128)S(1)}, u32[]{:S(2)}, u32[]{:S(2)}) collective-permute-start(f32[64,160]{1,0:T(8,128)S(1)} %add.198), channel_id=1, source_target_pairs={{0,4},{1,5},{2,6},{3,7},{4,0},{5,1},{6,2},{7,3},{8,12},{9,13},{10,... | collective-permute-start | bytes 122888 | tf_op jit(solution)/shard_map/ppermute | solution.py:47
  (6 other events, 4.1 us)

commit v2 on v1

--- a/solution.py
+++ b/solution.py
@@ -75,6 +75,22 @@
     order = [held.index(bit) for bit in range(count - 1, -1, -1)]
     x = jnp.transpose(x, order + list(range(count, x.ndim)))
     return x.reshape((size * x.shape[count],) + x.shape[count + 1 :])
+
+
+def exchange_sum(x, axis, size):
+    spread = jnp.broadcast_to(x[None], (size,) + x.shape)
+    return jnp.sum(lax.all_to_all(spread, axis, 0, 0, tiled=False), axis=0)
+
+
+def exchange_scatter_sum(x, axis, size):
+    blocks = x.reshape((size, x.shape[0] // size) + x.shape[1:])
+    return jnp.sum(lax.all_to_all(blocks, axis, 0, 0, tiled=False), axis=0)
+
+
+def exchange_gather(x, axis, size):
+    spread = jnp.broadcast_to(x[None], (size,) + x.shape)
+    out = lax.all_to_all(spread, axis, 0, 0, tiled=False)
+    return out.reshape((size * x.shape[0],) + x.shape[1:])
 
 
 def bit_order(size, first):
@@ -109,11 +125,10 @@
     gx_bits = bit_order(gx_size, (0, 2, 1, 3, 4))
     gy_bits = bit_order(gy_size, (0, 1, 2))
     wide_in = hidden_in.astype(jnp.float32)
-    stats = tree_sum(
+    stats = exchange_sum(
         jnp.stack([jnp.sum(wide_in, axis=1), jnp.sum(wide_in * wide_in, axis=1)]),
         "gx",
         gx_size,
-        gx_bits,
     )
     sum_rows, sum_squares = stats[0], stats[1]
     row_mean = sum_rows / D
@@ -137,7 +152,7 @@
         ],
         axis=1,
     )
-    reduced = tree_scatter_sum(partial, "gx", gx_size, gx_bits)
+    reduced = exchange_scatter_sum(partial, "gx", gx_size)
     qkv = reduced[:, :qkv_cols] + b_qkv
     up = reduced[:, qkv_cols:] + b_up
     qkv = qkv.reshape(rows_dev, heads_dev, 3, HD)
@@ -170,9 +185,7 @@
     )
     attended = (weighted / total[:, :, None]).astype(jnp.bfloat16).reshape(rows_dev, heads_dev * HD)
     hidden = jax.nn.gelu(up, approximate=False).astype(jnp.bfloat16)
-    gathered = tree_gather(
-        jnp.concatenate([attended, hidden], axis=1), "gx", gx_size, gx_bits[::-1]
-    )
+    gathered = exchange_gather(jnp.concatenate([attended, hidden], axis=1), "gx", gx_size)
     attn_cols = attended.shape[1]
     slot_part = jnp.dot(
         gathered[:, :attn_cols], w_out, preferred_element_type=jnp.float32

time: 144 us -> 111 us (0.77)
  blocking collectives: 0 us -> 40 us
  starting transfers between devices: 40.7 us -> 6.55 us
  waiting for transfers between devices: 60.1 us -> 32.8 us
  other arithmetic: 15.2 us -> 6.27 us
  local copies, waits for them, and re-layouts: 14.6 us -> 12.4 us
    ppermute x10 -> x0, waiting for transfers between devices: 41.6 us -> none  [the longest x5 21.5 us: tree_gather(): other = lax.ppermute(x, axis, xor_pairs(size, bit))]
    all_to_all x0 -> x2, blocking collectives: none -> 40 us  [the longest x1 20.9 us: exchange_sum(): return jnp.sum(lax.all_to_all(spread, axis, 0, 0, tiled=False), axis=0)]
    all_to_all x0 -> x1, waiting for transfers between devices: none -> 23.1 us  [exchange_scatter_sum(): return jnp.sum(lax.all_to_all(blocks, axis, 0, 0, tiled=False), axis=0)]
    ppermute x10 -> x0, starting transfers between devices: 22 us -> none  [the longest x5 13.3 us: tree_scatter_sum(): x = keep + lax.ppermute(send, axis, xor_pairs(size, bit))]
    ppermute x8 -> x3, starting transfers between devices: 18.7 us -> 1.88 us  [tree_sum(): x = x + lax.ppermute(x, axis, xor_pairs(size, bit))]
    ppermute x8 -> x3, waiting for transfers between devices: 18.5 us -> 9.66 us  [tree_sum(): x = x + lax.ppermute(x, axis, xor_pairs(size, bit))]
    another operation x11 -> x2, other arithmetic: 6.14 us -> 0.76 us  [the longest x9 5.38 us: tree_gather(): x = jnp.stack([jnp.where(low, x, other), jnp.where(low, other, x)], 0)]
    all_to_all x0 -> x1, starting transfers between devices: none -> 4.66 us  [exchange_scatter_sum(): return jnp.sum(lax.all_to_all(blocks, axis, 0, 0, tiled=False), axis=0)]
  transfers between devices with their start and end apart: 18 -> 4, of which waited for: 17 -> 4; matrix products, arithmetic and copies ran while one was open for 2% -> 2% of each run, Pallas kernels for 0% -> 0%
where the time goes in v2:
time: 111 us
  blocking collectives  40 us (36%)
  waiting for transfers between devices  32.8 us (30%)
  local copies, waits for them, and re-layouts  12.4 us (11%)
  matrix products  7.55 us (7%)
  starting transfers between devices  6.55 us (6%)
  other arithmetic  6.27 us (6%)
  between operations  5.04 us (5%)
    all_to_all x1, waiting for transfers between devices, exchange_scatter_sum(): return jnp.sum(lax.all_to_all(blocks, axis, 0, 0, tiled=False), axis=0)  23.1 us
    all_to_all x1, blocking collectives, exchange_sum(): return jnp.sum(lax.all_to_all(spread, axis, 0, 0, tiled=False), axis=0)  20.9 us
    all_to_all x1, blocking collectives, exchange_gather(): out = lax.all_to_all(spread, axis, 0, 0, tiled=False)  19.1 us
    ppermute x3, waiting for transfers between devices, tree_sum(): x = x + lax.ppermute(x, axis, xor_pairs(size, bit))  9.66 us
    all_to_all x1, starting transfers between devices, exchange_scatter_sum(): return jnp.sum(lax.all_to_all(blocks, axis, 0, 0, tiled=False), axis=0)  4.66 us
    unnamed x34, local copies, waits for them, and re-layouts  4.49 us
    dynamic_update_slice x2, local copies, waits for them, and re-layouts, on_device(): lax.dynamic_update_slice(new_keys, new_key[local_slot][None, :, None, :],...  2.64 us
    dot_general x1, matrix products, block_scores(): jnp.einsum('shd,shpd->shp', query, keys, preferred_element_type=jnp.float32)  2.51 us
  transfers between devices with their start and end apart: 4, of which 4 were waited for; matrix products, arithmetic and copies ran while one was open for 2% of the time, Pallas kernels for 0%

profile of v2, /device:TPU:16, one launch (start us, length us, event | category | flops | bytes accessed | tf_op | source)
XLA Modules:
  0.0 110.6 jit_solution(5436536648649414252)
XLA Ops:
  0.6 3.5 %copy.74 = bf16[2,5,1024,128]{3,2,1,0:T(8,128)(2,1)} copy(bf16[2,5,1024,128]{3,2,1,0:T(8,128)(2,1)} %param.30) | data formatting | bytes 5242880
  4.2 0.7 copy-done.4
  5.2 20.9 %all_to_all.15 = f32[32,1,128]{2,1,0:T(1,128)S(1)} all-to-all(f32[32,1,128]{2,1,0:T(1,128)S(1)} %reshape.146), channel_id=1, replica_groups=mesh['gx'=32,'gy'=8] {'gx'}, dimensions={0} | all-to-all | bytes 32768 | tf_op jit(solution)/shard_map/all_to_all | solution.py:82
  26.0 0.5 broadcast.116
  26.6 0.7 reduce
  27.4 0.5 fusion.8
  27.9 0.5 fusion.7
  28.6 1.7 %reshape.138 = f32[32,2,4480]{2,1,0:T(2,128)} reshape(f32[64,4480]{1,0:T(8,128)S(1)} %pad_maximum_fusion) | data formatting | bytes 2293760 | tf_op jit(solution)/shard_map/reshape | solution.py:86
  30.2 4.7 %all-to-all-start.1 = ((f32[32,2,4480]{2,1,0:T(2,128)}), f32[32,2,4480]{2,1,0:T(2,128)}, u32[]{:S(2)}, u32[]{:S(2)}) async-start(f32[32,2,4480]{2,1,0:T(2,128)} %reshape.138), calls=%async_computation.1 | async-start | bytes 2293760 | tf_op jit(solution)/shard_map/all_to_all | solution.py:87
  35.1 0.6 fusion.67
  39.7 0.7 multiply_cosine_fusion
  40.4 0.7 iota_compare_fusion.6
  41.1 23.1 %all-to-all-done.1 = f32[32,2,4480]{2,1,0:T(2,128)} async-done(((f32[32,2,4480]{2,1,0:T(2,128)}), f32[32,2,4480]{2,1,0:T(2,128)}, u32[]{:S(2)}, u32[]{:S(2)}) %all-to-all-start.1) | async-done | bytes 1146912 | tf_op jit(solution)/shard_map/all_to_all | solution.py:87
  64.2 1.6 %reduce_sum.58 = f32[2,4480]{1,0:T(2,128)S(1)} reduce(f32[32,2,4480]{2,1,0:T(2,128)} %all-to-all-done.1, f32[]{:T(128)} %constant.10.clone.1), dimensions={0}, to_apply=%region_4.5 | reduce | flops 277760 | bytes 1182724 | tf_op jit(solution)/shard_map/reduce_sum | solution.py:87
  65.9 0.9 fusion.46
  67.0 0.8 subtract_convert_fusion.1
  67.9 1.3 %dynamic_update_slice.12 = bf16[2,5,1024,128]{3,2,1,0:T(8,128)(2,1)} dynamic-update-slice(bf16[2,5,1024,128]{3,2,1,0:T(8,128)(2,1)} %copy.74, bf16[1,5,1,128]{3,2,1,0:T(2,128)(2,1)S(1)} %get-tuple-element.18, s32[]{:T(128)} %constant.45.clone.1, s32[]{:T(128)} %constant.45.clone.1, s32[]{:T(128)S(6)} %select_n.24, s32[]{:T(128)} %constant.45.clone.1) | dynamic-update-slice | bytes 2564 | tf_op jit(solution)/shard_map/dynamic_update_slice | solution.py:168
  69.3 1.3 %dynamic_update_slice.13 = bf16[2,5,1024,128]{3,2,1,0:T(8,128)(2,1)} dynamic-update-slice(bf16[2,5,1024,128]{3,2,1,0:T(8,128)(2,1)} %dynamic_update_slice.12, bf16[1,5,1,128]{3,2,1,0:T(2,128)(2,1)S(1)} %get-tuple-element.17, s32[]{:T(128)} %constant.17.clone.1, s32[]{:T(128)} %constant.45.clone.1, s32[]{:T(128)S(6)} %select_n.25, s32[]{:T(128)} %constant.45.clone.1) | dynamic-update-slice | bytes 2564 | tf_op jit(solution)/shard_map/dynamic_update_slice | solution.py:168
  70.6 2.5 %fusion.57 = f32[2,5,1,1024]{3,2,1,0:T(1,128)S(1)} fusion(bf16[2,5,1024,128]{3,2,1,0:T(8,128)(2,1)} %dynamic_update_slice.13, bf16[2,5,128,1]{2,0,1,3:T(2,128)(2,1)S(1)} %maximum_bitcast_fusion), kind=kOutput, calls=%fused_computation.68 | convolution fusion | flops 2621440 | bytes 2664960 | tf_op jit(solution)/shard_map/shd,shpd->shp/dot_general | solution.py:33
  73.1 0.1 fusion.6
  73.5 0.4 fusion.22
  74.1 0.2 broadcast_in_dim.40
  74.3 19.1 %all_to_all.16 = bf16[32,2,3200]{2,1,0:T(2,128)(2,1)} all-to-all(bf16[32,2,3200]{2,1,0:T(2,128)(2,1)S(1)} %broadcast_in_dim.40), channel_id=1, replica_groups=mesh['gx'=32,'gy'=8] {'gx'}, dimensions={0} | all-to-all | bytes 819200 | tf_op jit(solution)/shard_map/all_to_all | solution.py:92
  93.4 1.9 %reshape.141 = bf16[64,3200]{1,0:T(8,128)(2,1)} reshape(bf16[32,2,3200]{2,1,0:T(2,128)(2,1)} %all_to_all.16) | data formatting | bytes 819200 | tf_op jit(solution)/shard_map/reshape | solution.py:93
  95.3 1.1 %fusion.10 = f32[64,160]{1,0:T(8,128)S(1)} fusion(bf16[640,160]{0,1:T(8,128)(2,1)} %param.24, bf16[64,3200]{1,0:T(8,128)(2,1)} %reshape.141), kind=kOutput, calls=%fused_computation.18 | convolution fusion | flops 13107200 | bytes 327680 | tf_op jit(solution)/shard_map/dot_general | solution.py:190
  96.5 1.6 %convolution_add_fusion.1 = f32[64,160]{1,0:T(8,128)S(1)} fusion(f32[64,160]{1,0:T(8,128)S(1)} %fusion.10, bf16[2560,160]{0,1:T(8,128)(2,1)} %param.28, bf16[64,3200]{1,0:T(8,128)(2,1)} %reshape.141), kind=kOutput, calls=%fused_computation.5 | convolution fusion | flops 52439040 | bytes 1228800 | tf_op jit(solution)/shard_map/dot_general | solution.py:192
  98.3 1.2 %collective-permute-done = f32[64,160]{1,0:T(8,128)S(1)} collective-permute-done((f32[64,160]{1,0:T(8,128)S(1)}, f32[64,160]{1,0:T(8,128)S(1)}, u32[]{:S(2)}, u32[]{:S(2)}) %collective-permute-start) | collective-permute-done | bytes 40992 | tf_op jit(solution)/shard_map/ppermute | solution.py:47
  99.5 1.4 %collective-permute-start.1 = (f32[64,160]{1,0:T(8,128)S(1)}, f32[64,160]{1,0:T(8,128)S(1)}, u32[]{:S(2)}, u32[]{:S(2)}) collective-permute-start(f32[64,160]{1,0:T(8,128)S(1)} %add.107), channel_id=1, source_target_pairs={{0,2},{1,3},{2,0},{3,1},{4,6},{5,7},{6,4},{7,5},{8,10},{9,11},{10,... | collective-permute-start | bytes 122888 | tf_op jit(solution)/shard_map/ppermute | solution.py:47
  100.9 3.0 %collective-permute-done.1 = f32[64,160]{1,0:T(8,128)S(1)} collective-permute-done((f32[64,160]{1,0:T(8,128)S(1)}, f32[64,160]{1,0:T(8,128)S(1)}, u32[]{:S(2)}, u32[]{:S(2)}) %collective-permute-start.1) | collective-permute-done | bytes 40992 | tf_op jit(solution)/shard_map/ppermute | solution.py:47
  103.9 0.4 collective-permute-start.2
  104.3 5.4 %collective-permute-done.2 = f32[64,160]{1,0:T(8,128)S(1)} collective-permute-done((f32[64,160]{1,0:T(8,128)S(1)}, f32[64,160]{1,0:T(8,128)S(1)}, u32[]{:S(2)}, u32[]{:S(2)}) %collective-permute-start.2) | collective-permute-done | bytes 40992 | tf_op jit(solution)/shard_map/ppermute | solution.py:47
  109.8 0.8 fusion.4
  (63 shorter events, 1.6 us)
Async XLA Ops:
  0.6 27.3 %copy-start = (bf16[160,2560]{1,0:T(8,128)(2,1)S(1)}, bf16[160,2560]{1,0:T(8,128)(2,1)}, u32[]{:S(2)}) copy-start(bf16[160,2560]{1,0:T(8,128)(2,1)} %param.26) | copy-start | bytes 2457604
  4.2 0.8 copy-start.4
  4.2 23.2 %copy-start.3 = (bf16[160,1920]{1,0:T(8,128)(2,1)S(1)}, bf16[160,1920]{1,0:T(8,128)(2,1)}, u32[]{:S(2)}) copy-start(bf16[160,1920]{1,0:T(8,128)(2,1)} %param.22) | copy-start | bytes 1843204
  4.2 23.3 %copy-start.6 = (s32[64]{0:T(128)S(1)}, s32[64]{0:T(128)}, u32[]{:S(2)}) copy-start(s32[64]{0:T(128)} %param.33) | copy-start | bytes 772
  4.2 23.3 %copy-start.8 = (f32[160]{0:T(256)S(1)}, f32[160]{0:T(256)}, u32[]{:S(2)}) copy-start(f32[160]{0:T(256)} %param.19) | copy-start | bytes 1924
  4.2 23.3 %copy-start.9 = (f32[160]{0:T(256)S(1)}, f32[160]{0:T(256)}, u32[]{:S(2)}) copy-start(f32[160]{0:T(256)} %param.18) | copy-start | bytes 1924
  4.2 23.8 %copy-start.10 = (f32[160]{0:T(256)S(1)}, f32[160]{0:T(256)}, u32[]{:S(2)}) copy-start(f32[160]{0:T(256)} %param.21) | copy-start | bytes 1924
  4.2 23.7 %copy-start.11 = (f32[160]{0:T(256)S(1)}, f32[160]{0:T(256)}, u32[]{:S(2)}) copy-start(f32[160]{0:T(256)} %param.20) | copy-start | bytes 1924
  28.5 6.4 %copy-start.14 = (s32[64]{0:T(128)S(1)}, s32[64]{0:T(128)}, u32[]{:S(2)}) copy-start(s32[64]{0:T(128)} %param.32) | copy-start | bytes 772
  28.5 37.3 %copy-start.5 = (f32[1920]{0:T(1024)S(1)}, f32[1920]{0:T(1024)}, u32[]{:S(2)}) copy-start(f32[1920]{0:T(1024)} %param.23) | copy-start | bytes 23044
  30.2 34.0 %all-to-all-start.1 = ((f32[32,2,4480]{2,1,0:T(2,128)}), f32[32,2,4480]{2,1,0:T(2,128)}, u32[]{:S(2)}, u32[]{:S(2)}) async-start(f32[32,2,4480]{2,1,0:T(2,128)} %reshape.138), calls=%async_computation.1 | async-start | bytes 2293760 | tf_op jit(solution)/shard_map/all_to_all | solution.py:87
  34.9 38.5 %copy-start.2 = (bf16[2,5,1024,128]{3,2,1,0:T(8,128)(2,1)S(1)}, bf16[2,5,1024,128]{3,2,1,0:T(8,128)(2,1)}, u32[]{:S(2)}) copy-start(bf16[2,5,1024,128]{3,2,1,0:T(8,128)(2,1)} %param.31) | copy-start | bytes 7864324
  65.9 7.2 %copy-start.7 = (pred[2,1024]{1,0:T(4,128)(4,1)S(1)}, pred[2,1024]{1,0:T(4,128)(4,1)}, u32[]{:S(2)}) copy-start(pred[2,1024]{1,0:T(4,128)(4,1)} %iota_compare_fusion.6) | copy-start | bytes 6148
  73.5 24.7 %copy-start.1 = (bf16[2,5,1024,128]{3,2,1,0:T(8,128)(2,1)}, bf16[2,5,1024,128]{3,2,1,0:T(8,128)(2,1)S(1)}, u32[]{:S(2)}) copy-start(bf16[2,5,1024,128]{3,2,1,0:T(8,128)(2,1)S(1)} %dynamic_update_slice.15) | copy-start | bytes 7864324
  73.9 35.8 %copy-start.12 = (f32[160]{0:T(256)S(1)}, f32[160]{0:T(256)}, u32[]{:S(2)}) copy-start(f32[160]{0:T(256)} %param.29) | copy-start | bytes 1924
  73.9 35.8 %copy-start.13 = (f32[160]{0:T(256)S(1)}, f32[160]{0:T(256)}, u32[]{:S(2)}) copy-start(f32[160]{0:T(256)} %param.25) | copy-start | bytes 1924
  98.2 1.3 %collective-permute-start = (f32[64,160]{1,0:T(8,128)S(1)}, f32[64,160]{1,0:T(8,128)S(1)}, u32[]{:S(2)}, u32[]{:S(2)}) collective-permute-start(f32[64,160]{1,0:T(8,128)S(1)} %convolution_add_fusion.1), channel_id=1, source_target_pairs={{0,1},{1,0},{2,3},{3,2},{4,5},{5,4},{6,7},{7,6},{8,9},{9,8},{10,11... | collective-permute-start | bytes 122888 | tf_op jit(solution)/shard_map/ppermute | solution.py:47
  99.5 4.4 %collective-permute-start.1 = (f32[64,160]{1,0:T(8,128)S(1)}, f32[64,160]{1,0:T(8,128)S(1)}, u32[]{:S(2)}, u32[]{:S(2)}) collective-permute-start(f32[64,160]{1,0:T(8,128)S(1)} %add.107), channel_id=1, source_target_pairs={{0,2},{1,3},{2,0},{3,1},{4,6},{5,7},{6,4},{7,5},{8,10},{9,11},{10,... | collective-permute-start | bytes 122888 | tf_op jit(solution)/shard_map/ppermute | solution.py:47
  103.9 5.9 %collective-permute-start.2 = (f32[64,160]{1,0:T(8,128)S(1)}, f32[64,160]{1,0:T(8,128)S(1)}, u32[]{:S(2)}, u32[]{:S(2)}) collective-permute-start(f32[64,160]{1,0:T(8,128)S(1)} %add.108), channel_id=1, source_target_pairs={{0,4},{1,5},{2,6},{3,7},{4,0},{5,1},{6,2},{7,3},{8,12},{9,13},{10,... | collective-permute-start | bytes 122888 | tf_op jit(solution)/shard_map/ppermute | solution.py:47

commit v3 on v2

--- a/solution.py
+++ b/solution.py
@@ -4,6 +4,7 @@
 import jax.numpy as jnp
 from jax import lax
 from jax.sharding import PartitionSpec as P
+
 
 D = 5120
 HD = 128
@@ -48,35 +49,6 @@
     return x
 
 
-def tree_scatter_sum(x, axis, size, bits):
-    rows = x.shape[0]
-    me = lax.axis_index(axis)
-    x = x.reshape((2,) * len(bits) + (rows // size,) + x.shape[1:])
-    left = list(range(len(bits) - 1, -1, -1))
-    for bit in bits:
-        at = left.index(bit)
-        mine = (me >> bit) & 1
-        keep = lax.dynamic_index_in_dim(x, mine, at, keepdims=False)
-        send = lax.dynamic_index_in_dim(x, 1 - mine, at, keepdims=False)
-        x = keep + lax.ppermute(send, axis, xor_pairs(size, bit))
-        left.pop(at)
-    return x.reshape((rows // size,) + x.shape[-1:])
-
-
-def tree_gather(x, axis, size, bits):
-    me = lax.axis_index(axis)
-    held = []
-    for bit in bits:
-        other = lax.ppermute(x, axis, xor_pairs(size, bit))
-        low = (me >> bit) & 1 == 0
-        x = jnp.stack([jnp.where(low, x, other), jnp.where(low, other, x)], 0)
-        held.insert(0, bit)
-    count = len(bits)
-    order = [held.index(bit) for bit in range(count - 1, -1, -1)]
-    x = jnp.transpose(x, order + list(range(count, x.ndim)))
-    return x.reshape((size * x.shape[count],) + x.shape[count + 1 :])
-
-
 def exchange_sum(x, axis, size):
     spread = jnp.broadcast_to(x[None], (size,) + x.shape)
     return jnp.sum(lax.all_to_all(spread, axis, 0, 0, tiled=False), axis=0)
@@ -98,7 +70,7 @@
     return bits + [b for b in range(size.bit_length() - 1) if b not in bits]
 
 
-def on_device(
+def layer(
     hidden_in,
     norm1_gain,
     norm1_bias,
@@ -122,7 +94,6 @@
     requests = hidden_in.shape[0]
     rows_dev = key_cache.shape[0]
     heads_dev = key_cache.shape[1]
-    gx_bits = bit_order(gx_size, (0, 2, 1, 3, 4))
     gy_bits = bit_order(gy_size, (0, 1, 2))
     wide_in = hidden_in.astype(jnp.float32)
     stats = exchange_sum(
@@ -155,6 +126,8 @@
     reduced = exchange_scatter_sum(partial, "gx", gx_size)
     qkv = reduced[:, :qkv_cols] + b_qkv
     up = reduced[:, qkv_cols:] + b_up
+    hidden = jax.nn.gelu(up, approximate=False).astype(jnp.bfloat16)
+    hidden_all = exchange_gather(hidden, "gx", gx_size)
     qkv = qkv.reshape(rows_dev, heads_dev, 3, HD)
     position = my_len - 1
     query = rotate(qkv[:, :, 0], position).astype(jnp.bfloat16)
@@ -184,12 +157,11 @@
         "shp,shpd->shd", weights_low, new_values, preferred_element_type=jnp.float32
     )
     attended = (weighted / total[:, :, None]).astype(jnp.bfloat16).reshape(rows_dev, heads_dev * HD)
-    hidden = jax.nn.gelu(up, approximate=False).astype(jnp.bfloat16)
-    gathered = exchange_gather(jnp.concatenate([attended, hidden], axis=1), "gx", gx_size)
-    attn_cols = attended.shape[1]
-    slot_part = jnp.dot(
-        gathered[:, :attn_cols], w_out, preferred_element_type=jnp.float32
-    ) + jnp.dot(gathered[:, attn_cols:], w_down, preferred_element_type=jnp.float32)
+    attended_all = exchange_gather(attended, "gx", gx_size)
+    mlp_part = lax.optimization_barrier(
+        jnp.dot(hidden_all, w_down, preferred_element_type=jnp.float32)
+    )
+    slot_part = jnp.dot(attended_all, w_out, preferred_element_type=jnp.float32) + mlp_part
     branches = tree_sum(slot_part, "gy", gy_size, gy_bits)
     branches = jnp.dot(to_request, branches, precision=lax.Precision.HIGHEST)
     hidden_out = (wide_in + branches + b_out + b_down).astype(jnp.bfloat16)
@@ -197,7 +169,7 @@
 
 
 def solution(mesh):
-    body = functools.partial(on_device, gx_size=mesh.shape["gx"], gy_size=mesh.shape["gy"])
+    body = functools.partial(layer, gx_size=mesh.shape["gx"], gy_size=mesh.shape["gy"])
     return jax.shard_map(
         body,
         mesh=mesh,

time: 111 us -> 126 us (1.14)
  waiting for transfers between devices: 32.8 us -> 53.3 us
  blocking collectives: 40 us -> 20.9 us
  starting transfers between devices: 6.55 us -> 16.4 us
  local copies, waits for them, and re-layouts: 12.4 us -> 15.6 us
    all_to_all x0 -> x2, waiting for transfers between devices: none -> 19.8 us  [exchange_gather(): out = lax.all_to_all(spread, axis, 0, 0, tiled=False)]
    all_to_all x1 -> x0, blocking collectives: 19.1 us -> none  [exchange_gather(): out = lax.all_to_all(spread, axis, 0, 0, tiled=False)]
    all_to_all x0 -> x2, starting transfers between devices: none -> 9.83 us  [exchange_gather(): out = lax.all_to_all(spread, axis, 0, 0, tiled=False)]
    broadcast_in_dim x1 -> x2, local copies, waits for them, and re-layouts: 0.21 us -> 2.54 us  [exchange_gather(): spread = jnp.broadcast_to(x[None], (size,) + x.shape)]
    reshape x1 -> x2, local copies, waits for them, and re-layouts: 1.91 us -> 2.74 us  [exchange_gather(): return out.reshape((size * x.shape[0],) + x.shape[1:])]
  transfers between devices with their start and end apart: 4 -> 6, of which waited for: 4 -> 6; matrix products, arithmetic and copies ran while one was open for 2% -> 3% of each run, Pallas kernels for 0% -> 0%
where the time goes in v3:
time: 126 us; the launch traced here: 125 us
  waiting for transfers between devices  53.3 us (42%)
  blocking collectives  20.9 us (17%)
  starting transfers between devices  16.4 us (13%)
  local copies, waits for them, and re-layouts  15.6 us (12%)
  matrix products  8.26 us (7%)
  other arithmetic  5.62 us (4%)
  between operations  4.82 us (4%)
    all_to_all x1, waiting for transfers between devices, exchange_scatter_sum(): return jnp.sum(lax.all_to_all(blocks, axis, 0, 0, tiled=False), axis=0)  23.9 us
    all_to_all x1, blocking collectives, exchange_sum(): return jnp.sum(lax.all_to_all(spread, axis, 0, 0, tiled=False), axis=0)  20.9 us
    all_to_all x2, waiting for transfers between devices, exchange_gather(): out = lax.all_to_all(spread, axis, 0, 0, tiled=False)  19.8 us
    all_to_all x2, starting transfers between devices, exchange_gather(): out = lax.all_to_all(spread, axis, 0, 0, tiled=False)  9.83 us
    ppermute x3, waiting for transfers between devices, tree_sum(): x = x + lax.ppermute(x, axis, xor_pairs(size, bit))  9.65 us
    all_to_all x1, starting transfers between devices, exchange_scatter_sum(): return jnp.sum(lax.all_to_all(blocks, axis, 0, 0, tiled=False), axis=0)  4.67 us
    unnamed x34, local copies, waits for them, and re-layouts  4.49 us
    reshape x2, local copies, waits for them, and re-layouts, exchange_gather(): return out.reshape((size * x.shape[0],) + x.shape[1:])  2.74 us
  transfers between devices with their start and end apart: 6, of which 6 were waited for; matrix products, arithmetic and copies ran while one was open for 3% of the time, Pallas kernels for 0%

profile of v3, /device:TPU:16, one launch (start us, length us, event | category | flops | bytes accessed | tf_op | source)
XLA Modules:
  0.0 124.8 jit_solution(17747801139840887318)
XLA Ops:
  0.6 3.5 %copy.74 = bf16[2,5,1024,128]{3,2,1,0:T(8,128)(2,1)} copy(bf16[2,5,1024,128]{3,2,1,0:T(8,128)(2,1)} %param.30) | data formatting | bytes 5242880
  4.2 0.7 copy-done.4
  5.2 20.9 %all_to_all.20 = f32[32,1,128]{2,1,0:T(1,128)S(1)} all-to-all(f32[32,1,128]{2,1,0:T(1,128)S(1)} %reshape.147), channel_id=1, replica_groups=mesh['gx'=32,'gy'=8] {'gx'}, dimensions={0} | all-to-all | bytes 32768 | tf_op jit(solution)/shard_map/all_to_all | solution.py:54
  26.0 0.5 broadcast.116
  26.6 0.7 reduce
  27.4 0.5 fusion.7
  28.0 0.5 fusion.8
  28.6 1.7 %reshape.139 = f32[32,2,4480]{2,1,0:T(2,128)} reshape(f32[64,4480]{1,0:T(8,128)S(1)} %pad_maximum_fusion) | data formatting | bytes 2293760 | tf_op jit(solution)/shard_map/reshape | solution.py:58
  30.2 4.7 %all-to-all-start.1 = ((f32[32,2,4480]{2,1,0:T(2,128)}), f32[32,2,4480]{2,1,0:T(2,128)}, u32[]{:S(2)}, u32[]{:S(2)}) async-start(f32[32,2,4480]{2,1,0:T(2,128)} %reshape.139), calls=%async_computation.1 | async-start | bytes 2293760 | tf_op jit(solution)/shard_map/all_to_all | solution.py:59
  35.1 0.6 fusion.64
  39.7 0.7 iota_compare_fusion.6
  40.3 23.9 %all-to-all-done.1 = f32[32,2,4480]{2,1,0:T(2,128)} async-done(((f32[32,2,4480]{2,1,0:T(2,128)}), f32[32,2,4480]{2,1,0:T(2,128)}, u32[]{:S(2)}, u32[]{:S(2)}) %all-to-all-start.1) | async-done | bytes 1146912 | tf_op jit(solution)/shard_map/all_to_all | solution.py:59
  64.2 1.6 %reduce_sum.58 = f32[2,4480]{1,0:T(2,128)S(1)} reduce(f32[32,2,4480]{2,1,0:T(2,128)} %all-to-all-done.1, f32[]{:T(128)} %constant.10.clone.1), dimensions={0}, to_apply=%region_4.5 | reduce | flops 277760 | bytes 1182724 | tf_op jit(solution)/shard_map/reduce_sum | solution.py:59
  66.4 1.3 %dynamic_update_slice.12 = bf16[2,5,1024,128]{3,2,1,0:T(8,128)(2,1)} dynamic-update-slice(bf16[2,5,1024,128]{3,2,1,0:T(8,128)(2,1)} %copy.74, bf16[1,5,1,128]{3,2,1,0:T(2,128)(2,1)S(1)} %get-tuple-element.18, s32[]{:T(128)} %constant.45.clone.1, s32[]{:T(128)} %constant.45.clone.1, s32[]{:T(128)S(6)} %select_n.24, s32[]{:T(128)} %constant.45.clone.1) | dynamic-update-slice | bytes 2564 | tf_op jit(solution)/shard_map/dynamic_update_slice | solution.py:141
  67.7 1.3 %dynamic_update_slice.13 = bf16[2,5,1024,128]{3,2,1,0:T(8,128)(2,1)} dynamic-update-slice(bf16[2,5,1024,128]{3,2,1,0:T(8,128)(2,1)} %dynamic_update_slice.12, bf16[1,5,1,128]{3,2,1,0:T(2,128)(2,1)S(1)} %get-tuple-element.17, s32[]{:T(128)} %constant.17.clone.1, s32[]{:T(128)} %constant.45.clone.1, s32[]{:T(128)S(6)} %select_n.25, s32[]{:T(128)} %constant.45.clone.1) | dynamic-update-slice | bytes 2564 | tf_op jit(solution)/shard_map/dynamic_update_slice | solution.py:141
  69.0 2.5 %fusion.54 = f32[2,5,1,1024]{3,2,1,0:T(1,128)S(1)} fusion(bf16[2,5,1024,128]{3,2,1,0:T(8,128)(2,1)} %dynamic_update_slice.13, bf16[2,5,128,1]{2,0,1,3:T(2,128)(2,1)S(1)} %maximum_bitcast_fusion), kind=kOutput, calls=%fused_computation.64 | convolution fusion | flops 2621440 | bytes 2664960 | tf_op jit(solution)/shard_map/shd,shpd->shp/dot_general | solution.py:34
  72.5 0.9 broadcast_in_dim.45
  73.4 5.2 %all-to-all-start.2 = ((bf16[32,2,640]{2,1,0:T(2,128)(2,1)}), bf16[32,2,640]{2,1,0:T(2,128)(2,1)S(1)}, u32[]{:S(2)}, u32[]{:S(2)}) async-start(bf16[32,2,640]{2,1,0:T(2,128)(2,1)} %broadcast_in_dim.45), calls=%async_computation.2 | async-start | bytes 163840 | tf_op jit(solution)/shard_map/all_to_all | solution.py:64
  78.7 1.5 %fusion.43 = bf16[2,2560]{1,0:T(2,128)(2,1)} fusion(f32[2,4480]{1,0:T(2,128)} %copy-done.6, f32[2560]{0:T(1024)} %param.27), kind=kLoop, calls=%fused_computation.47 | loop fusion | flops 337920 | bytes 40960 | tf_op jit(solution)/shard_map/convert_element_type | solution.py:129
  80.2 8.6 %all-to-all-done.2 = bf16[32,2,640]{2,1,0:T(2,128)(2,1)S(1)} async-done(((bf16[32,2,640]{2,1,0:T(2,128)(2,1)}), bf16[32,2,640]{2,1,0:T(2,128)(2,1)S(1)}, u32[]{:S(2)}, u32[]{:S(2)}) %all-to-all-start.2) | async-done | bytes 81952 | tf_op jit(solution)/shard_map/all_to_all | solution.py:64
  88.8 1.6 %broadcast_in_dim.46 = bf16[32,2,2560]{2,1,0:T(2,128)(2,1)} broadcast(bf16[2,2560]{1,0:T(2,128)(2,1)} %fusion.43), dimensions={1,2} | broadcast | bytes 337920 | tf_op jit(solution)/shard_map/broadcast_in_dim | solution.py:63
  90.4 4.6 %all-to-all-start.3 = ((bf16[32,2,2560]{2,1,0:T(2,128)(2,1)}), bf16[32,2,2560]{2,1,0:T(2,128)(2,1)}, u32[]{:S(2)}, u32[]{:S(2)}) async-start(bf16[32,2,2560]{2,1,0:T(2,128)(2,1)} %broadcast_in_dim.46), calls=%async_computation.3 | async-start | bytes 655360 | tf_op jit(solution)/shard_map/all_to_all | solution.py:64
  95.0 0.9 reshape.141
  95.9 11.2 %all-to-all-done.3 = bf16[32,2,2560]{2,1,0:T(2,128)(2,1)} async-done(((bf16[32,2,2560]{2,1,0:T(2,128)(2,1)}), bf16[32,2,2560]{2,1,0:T(2,128)(2,1)}, u32[]{:S(2)}, u32[]{:S(2)}) %all-to-all-start.3) | async-done | bytes 327712 | tf_op jit(solution)/shard_map/all_to_all | solution.py:64
  107.1 1.8 %reshape.142 = bf16[64,2560]{1,0:T(8,128)(2,1)} reshape(bf16[32,2,2560]{2,1,0:T(2,128)(2,1)} %all-to-all-done.3) | data formatting | bytes 655360 | tf_op jit(solution)/shard_map/reshape | solution.py:65
  108.9 1.6 %fusion.65 = f32[64,160]{1,0:T(8,128)S(1)} fusion(bf16[64,2560]{1,0:T(8,128)(2,1)} %reshape.142, bf16[2560,160]{0,1:T(8,128)(2,1)} %param.28), kind=kOutput, calls=%fused_computation.93 | convolution fusion | flops 52428800 | bytes 1187840 | tf_op jit(solution)/shard_map/dot_general | solution.py:162
  110.6 1.1 convolution_add_fusion.1
  111.8 1.2 collective-permute-done
  113.1 1.4 %collective-permute-start.1 = (f32[64,160]{1,0:T(8,128)S(1)}, f32[64,160]{1,0:T(8,128)S(1)}, u32[]{:S(2)}, u32[]{:S(2)}) collective-permute-start(f32[64,160]{1,0:T(8,128)S(1)} %add.107), channel_id=1, source_target_pairs={{0,2},{1,3},{2,0},{3,1},{4,6},{5,7},{6,4},{7,5},{8,10},{9,11},{10,... | collective-permute-start | bytes 122888 | tf_op jit(solution)/shard_map/ppermute | solution.py:48
  114.4 3.0 %collective-permute-done.1 = f32[64,160]{1,0:T(8,128)S(1)} collective-permute-done((f32[64,160]{1,0:T(8,128)S(1)}, f32[64,160]{1,0:T(8,128)S(1)}, u32[]{:S(2)}, u32[]{:S(2)}) %collective-permute-start.1) | collective-permute-done | bytes 40992 | tf_op jit(solution)/shard_map/ppermute | solution.py:48
  117.9 5.4 %collective-permute-done.2 = f32[64,160]{1,0:T(8,128)S(1)} collective-permute-done((f32[64,160]{1,0:T(8,128)S(1)}, f32[64,160]{1,0:T(8,128)S(1)}, u32[]{:S(2)}, u32[]{:S(2)}) %collective-permute-start.2) | collective-permute-done | bytes 40992 | tf_op jit(solution)/shard_map/ppermute | solution.py:48
  123.3 1.6 %fusion.4 = bf16[64,160]{1,0:T(8,128)(2,1)} fusion(bf16[64,160]{1,0:T(8,128)(2,1)S(1)} %copy-done.4, f32[64,160]{1,0:T(8,128)S(1)} %add.108, f32[64,160]{1,0:T(8,128)S(1)} %collective-permute-done.2, f32[160]{0:T(256)} %param.29, f32[160]{0:T(256)} %param.25, s32[64]{0:T(128)} %param.33), kind=kOutput, calls=%fused_computation.7 | convolution fusion | flops 7929856 | bytes 124416 | tf_op jit(solution)/shard_map/dot_general | solution.py:166
  (67 shorter events, 2.8 us)
Async XLA Ops:
  0.6 26.8 %copy-start = (bf16[160,2560]{1,0:T(8,128)(2,1)S(1)}, bf16[160,2560]{1,0:T(8,128)(2,1)}, u32[]{:S(2)}) copy-start(bf16[160,2560]{1,0:T(8,128)(2,1)} %param.26) | copy-start | bytes 2457604
  4.2 0.8 copy-start.4
  4.2 23.3 %copy-start.8 = (s32[64]{0:T(128)S(1)}, s32[64]{0:T(128)}, u32[]{:S(2)}) copy-start(s32[64]{0:T(128)} %param.33) | copy-start | bytes 772
  4.2 23.3 %copy-start.10 = (f32[160]{0:T(256)S(1)}, f32[160]{0:T(256)}, u32[]{:S(2)}) copy-start(f32[160]{0:T(256)} %param.21) | copy-start | bytes 1924
  4.2 23.3 %copy-start.11 = (f32[160]{0:T(256)S(1)}, f32[160]{0:T(256)}, u32[]{:S(2)}) copy-start(f32[160]{0:T(256)} %param.20) | copy-start | bytes 1924
  4.2 23.8 %copy-start.3 = (bf16[160,1920]{1,0:T(8,128)(2,1)S(1)}, bf16[160,1920]{1,0:T(8,128)(2,1)}, u32[]{:S(2)}) copy-start(bf16[160,1920]{1,0:T(8,128)(2,1)} %param.22) | copy-start | bytes 1843204
  4.2 23.8 %copy-start.12 = (f32[160]{0:T(256)S(1)}, f32[160]{0:T(256)}, u32[]{:S(2)}) copy-start(f32[160]{0:T(256)} %param.19) | copy-start | bytes 1924
  4.2 23.8 %copy-start.13 = (f32[160]{0:T(256)S(1)}, f32[160]{0:T(256)}, u32[]{:S(2)}) copy-start(f32[160]{0:T(256)} %param.18) | copy-start | bytes 1924
  28.5 6.4 %copy-start.14 = (s32[64]{0:T(128)S(1)}, s32[64]{0:T(128)}, u32[]{:S(2)}) copy-start(s32[64]{0:T(128)} %param.32) | copy-start | bytes 772
  28.5 37.3 %copy-start.7 = (f32[1920]{0:T(1024)S(1)}, f32[1920]{0:T(1024)}, u32[]{:S(2)}) copy-start(f32[1920]{0:T(1024)} %param.23) | copy-start | bytes 23044
  30.2 34.0 %all-to-all-start.1 = ((f32[32,2,4480]{2,1,0:T(2,128)}), f32[32,2,4480]{2,1,0:T(2,128)}, u32[]{:S(2)}, u32[]{:S(2)}) async-start(f32[32,2,4480]{2,1,0:T(2,128)} %reshape.139), calls=%async_computation.1 | async-start | bytes 2293760 | tf_op jit(solution)/shard_map/all_to_all | solution.py:59
  34.9 37.0 %copy-start.2 = (bf16[2,5,1024,128]{3,2,1,0:T(8,128)(2,1)S(1)}, bf16[2,5,1024,128]{3,2,1,0:T(8,128)(2,1)}, u32[]{:S(2)}) copy-start(bf16[2,5,1024,128]{3,2,1,0:T(8,128)(2,1)} %param.31) | copy-start | bytes 7864324
  65.8 5.7 %copy-start.6 = (f32[2,4480]{1,0:T(2,128)}, f32[2,4480]{1,0:T(2,128)S(1)}, u32[]{:S(2)}) copy-start(f32[2,4480]{1,0:T(2,128)S(1)} %reduce_sum.58) | copy-start | bytes 107524
  65.9 5.6 %copy-start.9 = (pred[2,1024]{1,0:T(4,128)(4,1)S(1)}, pred[2,1024]{1,0:T(4,128)(4,1)}, u32[]{:S(2)}) copy-start(pred[2,1024]{1,0:T(4,128)(4,1)} %iota_compare_fusion.6) | copy-start | bytes 6148
  71.9 38.6 %copy-start.1 = (bf16[2,5,1024,128]{3,2,1,0:T(8,128)(2,1)}, bf16[2,5,1024,128]{3,2,1,0:T(8,128)(2,1)S(1)}, u32[]{:S(2)}) copy-start(bf16[2,5,1024,128]{3,2,1,0:T(8,128)(2,1)S(1)} %dynamic_update_slice.15) | copy-start | bytes 7864324
  73.4 15.4 %all-to-all-start.2 = ((bf16[32,2,640]{2,1,0:T(2,128)(2,1)}), bf16[32,2,640]{2,1,0:T(2,128)(2,1)S(1)}, u32[]{:S(2)}, u32[]{:S(2)}) async-start(bf16[32,2,640]{2,1,0:T(2,128)(2,1)} %broadcast_in_dim.45), calls=%async_computation.2 | async-start | bytes 163840 | tf_op jit(solution)/shard_map/all_to_all | solution.py:64
  88.8 1.6 %copy-start.5 = (bf16[32,2,640]{2,1,0:T(2,128)(2,1)}, bf16[32,2,640]{2,1,0:T(2,128)(2,1)S(1)}, u32[]{:S(2)}) copy-start(bf16[32,2,640]{2,1,0:T(2,128)(2,1)S(1)} %all-to-all-done.2) | copy-start | bytes 245764
  90.4 16.7 %all-to-all-start.3 = ((bf16[32,2,2560]{2,1,0:T(2,128)(2,1)}), bf16[32,2,2560]{2,1,0:T(2,128)(2,1)}, u32[]{:S(2)}, u32[]{:S(2)}) async-start(bf16[32,2,2560]{2,1,0:T(2,128)(2,1)} %broadcast_in_dim.46), calls=%async_computation.3 | async-start | bytes 655360 | tf_op jit(solution)/shard_map/all_to_all | solution.py:64
  111.7 1.3 %collective-permute-start = (f32[64,160]{1,0:T(8,128)S(1)}, f32[64,160]{1,0:T(8,128)S(1)}, u32[]{:S(2)}, u32[]{:S(2)}) collective-permute-start(f32[64,160]{1,0:T(8,128)S(1)} %convolution_add_fusion.1), channel_id=1, source_target_pairs={{0,1},{1,0},{2,3},{3,2},{4,5},{5,4},{6,7},{7,6},{8,9},{9,8},{10,11... | collective-permute-start | bytes 122888 | tf_op jit(solution)/shard_map/ppermute | solution.py:48
  113.1 4.4 %collective-permute-start.1 = (f32[64,160]{1,0:T(8,128)S(1)}, f32[64,160]{1,0:T(8,128)S(1)}, u32[]{:S(2)}, u32[]{:S(2)}) collective-permute-start(f32[64,160]{1,0:T(8,128)S(1)} %add.107), channel_id=1, source_target_pairs={{0,2},{1,3},{2,0},{3,1},{4,6},{5,7},{6,4},{7,5},{8,10},{9,11},{10,... | collective-permute-start | bytes 122888 | tf_op jit(solution)/shard_map/ppermute | solution.py:48
  117.4 5.9 %collective-permute-start.2 = (f32[64,160]{1,0:T(8,128)S(1)}, f32[64,160]{1,0:T(8,128)S(1)}, u32[]{:S(2)}, u32[]{:S(2)}) collective-permute-start(f32[64,160]{1,0:T(8,128)S(1)} %add.108), channel_id=1, source_target_pairs={{0,4},{1,5},{2,6},{3,7},{4,0},{5,1},{6,2},{7,3},{8,12},{9,13},{10,... | collective-permute-start | bytes 122888 | tf_op jit(solution)/shard_map/ppermute | solution.py:48

commit v4 on v2

--- a/solution.py
+++ b/solution.py
@@ -91,6 +91,26 @@
     spread = jnp.broadcast_to(x[None], (size,) + x.shape)
     out = lax.all_to_all(spread, axis, 0, 0, tiled=False)
     return out.reshape((size * x.shape[0],) + x.shape[1:])
+
+
+def split_bf16(v):
+    high = v.astype(jnp.bfloat16)
+    return high, (v - high.astype(jnp.float32)).astype(jnp.bfloat16)
+
+
+def split_products(x, gain, bias, weight):
+    rows = x.shape[0]
+    scaled_high, scaled_low = split_bf16(x * gain)
+    gain_high, gain_low = split_bf16(gain[None])
+    bias_high, bias_low = split_bf16(bias[None])
+    lhs = jnp.concatenate([scaled_high, scaled_low, gain_high, gain_low, bias_high, bias_low])
+    prod = jnp.dot(lhs, weight, preferred_element_type=jnp.float32)
+    main = prod[:rows] + prod[rows : 2 * rows]
+    base = 2 * rows
+    terms = jnp.stack(
+        [prod[base] + prod[base + 1], prod[base + 2] + prod[base + 3]]
+    )
+    return main, terms
 
 
 def bit_order(size, first):
@@ -125,36 +145,37 @@
     gx_bits = bit_order(gx_size, (0, 2, 1, 3, 4))
     gy_bits = bit_order(gy_size, (0, 1, 2))
     wide_in = hidden_in.astype(jnp.float32)
-    stats = exchange_sum(
-        jnp.stack([jnp.sum(wide_in, axis=1), jnp.sum(wide_in * wide_in, axis=1)]),
-        "gx",
-        gx_size,
-    )
-    sum_rows, sum_squares = stats[0], stats[1]
-    row_mean = sum_rows / D
-    row_var = sum_squares / D - row_mean * row_mean
-    normed = (wide_in - row_mean[:, None]) * lax.rsqrt(row_var + 1e-05)[:, None]
-    attn_in = (normed * norm1_gain + norm1_bias).astype(jnp.bfloat16)
-    mlp_in = (normed * norm2_gain + norm2_bias).astype(jnp.bfloat16)
     slot_ids = lax.iota(jnp.int32, requests)
     matches = assignment[:, None] == slot_ids[None, :]
     to_request = matches.astype(jnp.float32)
     to_slot = matches.T.astype(jnp.bfloat16)
-    attn_slot = jnp.dot(to_slot, attn_in, preferred_element_type=jnp.float32).astype(jnp.bfloat16)
-    mlp_slot = jnp.dot(to_slot, mlp_in, preferred_element_type=jnp.float32).astype(jnp.bfloat16)
+    x_slot = jnp.dot(to_slot, hidden_in, preferred_element_type=jnp.float32)
     slot_len = jnp.sum(jnp.where(matches, lengths[:, None], 0), axis=0)
     my_len = lax.dynamic_slice_in_dim(slot_len, lax.axis_index("gx") * rows_dev, rows_dev, 0)
     qkv_cols = w_qkv.shape[1]
-    partial = jnp.concatenate(
-        [
-            jnp.dot(attn_slot, w_qkv, preferred_element_type=jnp.float32),
-            jnp.dot(mlp_slot, w_up, preferred_element_type=jnp.float32),
-        ],
-        axis=1,
-    )
-    reduced = exchange_scatter_sum(partial, "gx", gx_size)
-    qkv = reduced[:, :qkv_cols] + b_qkv
-    up = reduced[:, qkv_cols:] + b_up
+    up_cols = w_up.shape[1]
+    gx_rows, gx_terms = split_products(x_slot, norm1_gain, norm1_bias, w_qkv)
+    up_rows, up_terms = split_products(x_slot, norm2_gain, norm2_bias, w_up)
+    local_stats = jnp.stack([jnp.sum(x_slot, axis=1), jnp.sum(x_slot * x_slot, axis=1)], axis=1)
+    reduced = exchange_scatter_sum(
+        jnp.concatenate([gx_rows, up_rows, local_stats], axis=1), "gx", gx_size
+    )
+    terms = tree_sum(jnp.concatenate([gx_terms, up_terms], axis=1), "gx", gx_size, gx_bits)
+    row_mean = reduced[:, -2] / D
+    row_var = reduced[:, -1] / D - row_mean * row_mean
+    row_scale = lax.rsqrt(row_var + 1e-05)[:, None]
+    row_mean = row_mean[:, None]
+    qkv = (
+        row_scale * (reduced[:, :qkv_cols] - row_mean * terms[0:1, :qkv_cols])
+        + terms[1:2, :qkv_cols]
+        + b_qkv
+    )
+    up = (
+        row_scale
+        * (reduced[:, qkv_cols : qkv_cols + up_cols] - row_mean * terms[0:1, qkv_cols:])
+        + terms[1:2, qkv_cols:]
+        + b_up
+    )
     qkv = qkv.reshape(rows_dev, heads_dev, 3, HD)
     position = my_len - 1
     query = rotate(qkv[:, :, 0], position).astype(jnp.bfloat16)

time: 111 us -> 128 us (1.15)
  blocking collectives: 40 us -> 20.8 us
  starting transfers between devices: 6.55 us -> 25.6 us
  local copies, waits for them, and re-layouts: 12.4 us -> 20.2 us
  waiting for transfers between devices: 32.8 us -> 38.1 us
  other arithmetic: 6.27 us -> 9.01 us
    ppermute x3 -> x8, waiting for transfers between devices: 9.66 us -> 38.1 us  [tree_sum(): x = x + lax.ppermute(x, axis, xor_pairs(size, bit))]
    all_to_all x1, waiting for transfers between devices: 23.1 us -> 0.01 us  [exchange_scatter_sum(): return jnp.sum(lax.all_to_all(blocks, axis, 0, 0, tiled=False), axis=0)]
    all_to_all x1 -> x0, blocking collectives: 20.9 us -> none  [exchange_sum(): return jnp.sum(lax.all_to_all(spread, axis, 0, 0, tiled=False), axis=0)]
    ppermute x3 -> x8, starting transfers between devices: 1.88 us -> 14.1 us  [tree_sum(): x = x + lax.ppermute(x, axis, xor_pairs(size, bit))]
    concatenate x0 -> x7, local copies, waits for them, and re-layouts: none -> 8.29 us  [the longest x5 8.23 us: on_device(): jnp.concatenate([gx_rows, up_rows, local_stats], axis=1)]
    all_to_all x1, starting transfers between devices: 4.66 us -> 11.4 us  [exchange_scatter_sum(): return jnp.sum(lax.all_to_all(blocks, axis, 0, 0, tiled=False), axis=0)]
    add x1 -> x5, other arithmetic: 0.01 us -> 1.78 us  [the longest x2 0.96 us: split_products(): main = prod[:rows] + prod[rows:2 * rows]]
    reshape x1 -> x0, local copies, waits for them, and re-layouts: 1.68 us -> none  [exchange_scatter_sum(): blocks = x.reshape((size, x.shape[0] // size) + x.shape[1:])]
  transfers between devices with their start and end apart: 4 -> 9, of which waited for: 4 -> 7; matrix products, arithmetic and copies ran while one was open for 2% -> 4% of each run, Pallas kernels for 0% -> 0%
where the time goes in v4:
time: 128 us; the launch traced here: 127 us
  waiting for transfers between devices  38.1 us (30%)
  starting transfers between devices  25.6 us (20%)
  blocking collectives  20.8 us (16%)
  local copies, waits for them, and re-layouts  20.2 us (16%)
  other arithmetic  9.01 us (7%)
  matrix products  8.26 us (6%)
  between operations  4.91 us (4%)
    ppermute x8, waiting for transfers between devices, tree_sum(): x = x + lax.ppermute(x, axis, xor_pairs(size, bit))  38.1 us
    all_to_all x1, blocking collectives, exchange_gather(): out = lax.all_to_all(spread, axis, 0, 0, tiled=False)  20.8 us
    ppermute x8, starting transfers between devices, tree_sum(): x = x + lax.ppermute(x, axis, xor_pairs(size, bit))  14.1 us
    all_to_all x1, starting transfers between devices, exchange_scatter_sum(): return jnp.sum(lax.all_to_all(blocks, axis, 0, 0, tiled=False), axis=0)  11.4 us
    concatenate x5, local copies, waits for them, and re-layouts, on_device(): jnp.concatenate([gx_rows, up_rows, local_stats], axis=1)  8.23 us
    unnamed x40, local copies, waits for them, and re-layouts  4.97 us
    dynamic_update_slice x2, local copies, waits for them, and re-layouts, on_device(): lax.dynamic_update_slice(new_keys, new_key[local_slot][None, :, None, :],...  2.63 us
  transfers between devices with their start and end apart: 9, of which 7 were waited for; matrix products, arithmetic and copies ran while one was open for 4% of the time, Pallas kernels for 0%

profile of v4, /device:TPU:16, one launch (start us, length us, event | category | flops | bytes accessed | tf_op | source)
XLA Modules:
  0.0 126.8 jit_solution(16372822001567767597)
XLA Ops:
  0.6 3.5 %copy.75 = bf16[2,5,1024,128]{3,2,1,0:T(8,128)(2,1)} copy(bf16[2,5,1024,128]{3,2,1,0:T(8,128)(2,1)} %param.30) | data formatting | bytes 5242880
  6.1 1.1 concatenate.33
  7.6 0.9 slice_add_fusion
  8.5 2.3 %concatenate.35 = f32[32,2,2560]{2,1,0:T(2,128)} reshape(f32[64,2560]{1,0:T(8,128)} %slice_add_fusion) | data formatting | bytes 1310720 | tf_op jit(solution)/shard_map/concatenate | solution.py:161
  10.8 4.5 %concatenate.38 = f32[32,2,4482]{2,1,0:T(2,128)} concatenate(f32[32,2,1920]{2,1,0:T(2,128)} %concatenate.33, f32[32,2,2560]{2,1,0:T(2,128)} %concatenate.35, f32[32,2,1]{2,1,0:T(2,128)S(1)} %concatenate.43, f32[32,2,1]{2,1,0:T(2,128)S(1)} %concatenate.44), dimensions={2} | concatenate | bytes 2294784 | tf_op jit(solution)/shard_map/concatenate | solution.py:161
  15.3 11.4 %all-to-all-start = ((f32[32,2,4482]{2,1,0:T(2,128)}), f32[32,2,4482]{2,1,0:T(2,128)}, u32[]{:S(2)}, u32[]{:S(2)}) async-start(f32[32,2,4482]{2,1,0:T(2,128)} %concatenate.38), calls=%async_computation | async-start | bytes 2359296 | tf_op jit(solution)/shard_map/all_to_all | solution.py:87
  27.4 1.7 %collective-permute-start = (f32[2,4480]{1,0:T(2,128)}, f32[2,4480]{1,0:T(2,128)S(1)}, u32[]{:S(2)}, u32[]{:S(2)}) collective-permute-start(f32[2,4480]{1,0:T(2,128)} %maximum_maximum_fusion), channel_id=1, source_target_pairs={{0,8},{8,0},{16,24},{24,16},{32,40},{40,32},{48,56},{56,48},{64,72... | collective-permute-start | bytes 107528 | tf_op jit(solution)/shard_map/ppermute | solution.py:47
  30.0 2.2 %collective-permute-done = f32[2,4480]{1,0:T(2,128)S(1)} collective-permute-done((f32[2,4480]{1,0:T(2,128)}, f32[2,4480]{1,0:T(2,128)S(1)}, u32[]{:S(2)}, u32[]{:S(2)}) %collective-permute-start) | collective-permute-done | bytes 35872 | tf_op jit(solution)/shard_map/ppermute | solution.py:47
  32.2 2.1 %collective-permute-start.1 = (f32[2,4480]{1,0:T(2,128)S(1)}, f32[2,4480]{1,0:T(2,128)S(1)}, u32[]{:S(2)}, u32[]{:S(2)}) collective-permute-start(f32[2,4480]{1,0:T(2,128)S(1)} %fusion.56), channel_id=1, source_target_pairs={{0,32},{8,40},{16,48},{24,56},{32,0},{40,8},{48,16},{56,24},{64,96... | collective-permute-start | bytes 107528 | tf_op jit(solution)/shard_map/ppermute | solution.py:47
  34.3 20.4 %collective-permute-done.1 = f32[2,4480]{1,0:T(2,128)S(1)} collective-permute-done((f32[2,4480]{1,0:T(2,128)S(1)}, f32[2,4480]{1,0:T(2,128)S(1)}, u32[]{:S(2)}, u32[]{:S(2)}) %collective-permute-start.1) | collective-permute-done | bytes 35872 | tf_op jit(solution)/shard_map/ppermute | solution.py:47
  54.7 2.9 %collective-permute-start.2 = (f32[2,4480]{1,0:T(2,128)S(1)}, f32[2,4480]{1,0:T(2,128)S(1)}, u32[]{:S(2)}, u32[]{:S(2)}) collective-permute-start(f32[2,4480]{1,0:T(2,128)S(1)} %fusion.57), channel_id=1, source_target_pairs={{0,16},{8,24},{16,0},{24,8},{32,48},{40,56},{48,32},{56,40},{64,80... | collective-permute-start | bytes 107528 | tf_op jit(solution)/shard_map/ppermute | solution.py:47
  57.6 2.6 %collective-permute-done.2 = f32[2,4480]{1,0:T(2,128)S(1)} collective-permute-done((f32[2,4480]{1,0:T(2,128)S(1)}, f32[2,4480]{1,0:T(2,128)S(1)}, u32[]{:S(2)}, u32[]{:S(2)}) %collective-permute-start.2) | collective-permute-done | bytes 35872 | tf_op jit(solution)/shard_map/ppermute | solution.py:47
  60.3 1.0 collective-permute-start.3
  62.0 3.3 %collective-permute-done.3 = f32[2,4480]{1,0:T(2,128)S(1)} collective-permute-done((f32[2,4480]{1,0:T(2,128)S(1)}, f32[2,4480]{1,0:T(2,128)S(1)}, u32[]{:S(2)}, u32[]{:S(2)}) %collective-permute-start.3) | collective-permute-done | bytes 35872 | tf_op jit(solution)/shard_map/ppermute | solution.py:47
  65.2 4.6 %collective-permute-start.4 = (f32[2,4480]{1,0:T(2,128)S(1)}, f32[2,4480]{1,0:T(2,128)}, u32[]{:S(2)}, u32[]{:S(2)}) collective-permute-start(f32[2,4480]{1,0:T(2,128)S(1)} %add.137), channel_id=1, source_target_pairs={{0,128},{8,136},{16,144},{24,152},{32,160},{40,168},{48,176},{56,1... | collective-permute-start | bytes 107528 | tf_op jit(solution)/shard_map/ppermute | solution.py:47
  74.2 0.8 add.138
  75.7 1.6 %reduce_sum.48 = f32[2,4482]{1,0:T(2,128)S(1)} reduce(f32[32,2,4482]{2,1,0:T(2,128)} %all-to-all-done, f32[]{:T(128)} %constant.10.clone.1), dimensions={0}, to_apply=%region_3.4 | reduce | flops 277884 | bytes 1183252 | tf_op jit(solution)/shard_map/reduce_sum | solution.py:87
  78.1 0.8 fusion.27
  79.1 0.8 subtract_convert_fusion.3
  80.1 1.3 %dynamic_update_slice.12 = bf16[2,5,1024,128]{3,2,1,0:T(8,128)(2,1)} dynamic-update-slice(bf16[2,5,1024,128]{3,2,1,0:T(8,128)(2,1)} %copy.75, bf16[1,5,1,128]{3,2,1,0:T(2,128)(2,1)S(1)} %get-tuple-element.44, s32[]{:T(128)} %constant.45.clone.1, s32[]{:T(128)} %constant.45.clone.1, s32[]{:T(128)S(6)} %select_n.24, s32[]{:T(128)} %constant.45.clone.1) | dynamic-update-slice | bytes 2564 | tf_op jit(solution)/shard_map/dynamic_update_slice | solution.py:189
  81.4 1.3 %dynamic_update_slice.13 = bf16[2,5,1024,128]{3,2,1,0:T(8,128)(2,1)} dynamic-update-slice(bf16[2,5,1024,128]{3,2,1,0:T(8,128)(2,1)} %dynamic_update_slice.12, bf16[1,5,1,128]{3,2,1,0:T(2,128)(2,1)S(1)} %get-tuple-element.43, s32[]{:T(128)} %constant.17.clone.1, s32[]{:T(128)} %constant.45.clone.1, s32[]{:T(128)S(6)} %select_n.25, s32[]{:T(128)} %constant.45.clone.1) | dynamic-update-slice | bytes 2564 | tf_op jit(solution)/shard_map/dynamic_update_slice | solution.py:189
  82.7 2.5 %fusion.31 = f32[2,5,1,1024]{3,2,1,0:T(1,128)S(1)} fusion(bf16[2,5,1024,128]{3,2,1,0:T(8,128)(2,1)} %dynamic_update_slice.13, bf16[2,5,128,1]{2,0,1,3:T(2,128)(2,1)S(1)} %maximum_bitcast_fusion), kind=kOutput, calls=%fused_computation.66 | convolution fusion | flops 2621440 | bytes 2664960 | tf_op jit(solution)/shard_map/shd,shpd->shp/dot_general | solution.py:33
  86.9 1.0 fusion.17
  88.2 20.8 %all_to_all.10 = bf16[32,2,3200]{2,1,0:T(2,128)(2,1)} all-to-all(bf16[32,2,3200]{2,1,0:T(2,128)(2,1)S(1)} %broadcast_in_dim.37), channel_id=1, replica_groups=mesh['gx'=32,'gy'=8] {'gx'}, dimensions={0} | all-to-all | bytes 819200 | tf_op jit(solution)/shard_map/all_to_all | solution.py:92
  109.0 1.9 %reshape.136 = bf16[64,3200]{1,0:T(8,128)(2,1)} reshape(bf16[32,2,3200]{2,1,0:T(2,128)(2,1)} %all_to_all.10) | data formatting | bytes 819200 | tf_op jit(solution)/shard_map/reshape | solution.py:93
  110.9 1.1 fusion.8
  112.1 1.6 %convolution_add_fusion.1 = f32[64,160]{1,0:T(8,128)S(1)} fusion(f32[64,160]{1,0:T(8,128)S(1)} %fusion.8, bf16[2560,160]{0,1:T(8,128)(2,1)} %param.28, bf16[64,3200]{1,0:T(8,128)(2,1)} %reshape.136), kind=kOutput, calls=%fused_computation.4 | convolution fusion | flops 52439040 | bytes 1228800 | tf_op jit(solution)/shard_map/dot_general | solution.py:213
  113.8 1.2 collective-permute-done.5
  115.1 1.4 %collective-permute-start.6 = (f32[64,160]{1,0:T(8,128)S(1)}, f32[64,160]{1,0:T(8,128)S(1)}, u32[]{:S(2)}, u32[]{:S(2)}) collective-permute-start(f32[64,160]{1,0:T(8,128)S(1)} %add.154), channel_id=1, source_target_pairs={{0,2},{1,3},{2,0},{3,1},{4,6},{5,7},{6,4},{7,5},{8,10},{9,11},{10,... | collective-permute-start | bytes 122888 | tf_op jit(solution)/shard_map/ppermute | solution.py:47
  116.4 3.0 %collective-permute-done.6 = f32[64,160]{1,0:T(8,128)S(1)} collective-permute-done((f32[64,160]{1,0:T(8,128)S(1)}, f32[64,160]{1,0:T(8,128)S(1)}, u32[]{:S(2)}, u32[]{:S(2)}) %collective-permute-start.6) | collective-permute-done | bytes 40992 | tf_op jit(solution)/shard_map/ppermute | solution.py:47
  119.9 5.4 %collective-permute-done.7 = f32[64,160]{1,0:T(8,128)S(1)} collective-permute-done((f32[64,160]{1,0:T(8,128)S(1)}, f32[64,160]{1,0:T(8,128)S(1)}, u32[]{:S(2)}, u32[]{:S(2)}) %collective-permute-start.7) | collective-permute-done | bytes 40992 | tf_op jit(solution)/shard_map/ppermute | solution.py:47
  125.3 1.5 %fusion.4 = bf16[64,160]{1,0:T(8,128)(2,1)} fusion(f32[64,160]{1,0:T(8,128)S(1)} %add.155, f32[64,160]{1,0:T(8,128)S(1)} %collective-permute-done.7, bf16[64,160]{1,0:T(8,128)(2,1)S(1)} %copy-done.4, f32[160]{0:T(256)S(1)} %copy-done.15, f32[160]{0:T(256)} %param.25, s32[64]{0:T(128)S(1)} %copy-done.14), kind=kOutput, calls=%fused_computation.6 | convolution fusion | flops 7929856 | bytes 124416 | tf_op jit(solution)/shard_map/dot_general | solution.py:215
  (101 shorter events, 9.4 us)
Async XLA Ops:
  0.6 6.6 %copy-start = (bf16[160,2560]{1,0:T(8,128)(2,1)S(1)}, bf16[160,2560]{1,0:T(8,128)(2,1)}, u32[]{:S(2)}) copy-start(bf16[160,2560]{1,0:T(8,128)(2,1)} %param.26) | copy-start | bytes 2457604
  4.2 0.7 copy-start.16
  4.2 0.7 copy-start.17
  4.2 0.7 copy-start.10
  4.2 0.8 copy-start.9
  4.2 0.8 copy-start.4
  4.2 0.8 copy-start.13
  4.2 1.6 %copy-start.3 = (bf16[160,1920]{1,0:T(8,128)(2,1)S(1)}, bf16[160,1920]{1,0:T(8,128)(2,1)}, u32[]{:S(2)}) copy-start(bf16[160,1920]{1,0:T(8,128)(2,1)} %param.22) | copy-start | bytes 1843204
  10.8 18.4 %copy-start.18 = (s32[64]{0:T(128)S(1)}, s32[64]{0:T(128)}, u32[]{:S(2)}) copy-start(s32[64]{0:T(128)} %param.32) | copy-start | bytes 772
  15.3 60.4 %all-to-all-start = ((f32[32,2,4482]{2,1,0:T(2,128)}), f32[32,2,4482]{2,1,0:T(2,128)}, u32[]{:S(2)}, u32[]{:S(2)}) async-start(f32[32,2,4482]{2,1,0:T(2,128)} %concatenate.38), calls=%async_computation | async-start | bytes 2359296 | tf_op jit(solution)/shard_map/all_to_all | solution.py:87
  27.4 4.7 %collective-permute-start = (f32[2,4480]{1,0:T(2,128)}, f32[2,4480]{1,0:T(2,128)S(1)}, u32[]{:S(2)}, u32[]{:S(2)}) collective-permute-start(f32[2,4480]{1,0:T(2,128)} %maximum_maximum_fusion), channel_id=1, source_target_pairs={{0,8},{8,0},{16,24},{24,16},{32,40},{40,32},{48,56},{56,48},{64,72... | collective-permute-start | bytes 107528 | tf_op jit(solution)/shard_map/ppermute | solution.py:47
  30.0 56.1 %copy-start.2 = (bf16[2,5,1024,128]{3,2,1,0:T(8,128)(2,1)S(1)}, bf16[2,5,1024,128]{3,2,1,0:T(8,128)(2,1)}, u32[]{:S(2)}) copy-start(bf16[2,5,1024,128]{3,2,1,0:T(8,128)(2,1)} %param.31) | copy-start | bytes 7864324
  32.2 22.5 %collective-permute-start.1 = (f32[2,4480]{1,0:T(2,128)S(1)}, f32[2,4480]{1,0:T(2,128)S(1)}, u32[]{:S(2)}, u32[]{:S(2)}) collective-permute-start(f32[2,4480]{1,0:T(2,128)S(1)} %fusion.56), channel_id=1, source_target_pairs={{0,32},{8,40},{16,48},{24,56},{32,0},{40,8},{48,16},{56,24},{64,96... | collective-permute-start | bytes 107528 | tf_op jit(solution)/shard_map/ppermute | solution.py:47
  54.7 5.5 %collective-permute-start.2 = (f32[2,4480]{1,0:T(2,128)S(1)}, f32[2,4480]{1,0:T(2,128)S(1)}, u32[]{:S(2)}, u32[]{:S(2)}) collective-permute-start(f32[2,4480]{1,0:T(2,128)S(1)} %fusion.57), channel_id=1, source_target_pairs={{0,16},{8,24},{16,0},{24,8},{32,48},{40,56},{48,32},{56,40},{64,80... | collective-permute-start | bytes 107528 | tf_op jit(solution)/shard_map/ppermute | solution.py:47
  60.3 4.9 %collective-permute-start.3 = (f32[2,4480]{1,0:T(2,128)S(1)}, f32[2,4480]{1,0:T(2,128)S(1)}, u32[]{:S(2)}, u32[]{:S(2)}) collective-permute-start(f32[2,4480]{1,0:T(2,128)S(1)} %add.136), channel_id=1, source_target_pairs={{0,64},{8,72},{16,80},{24,88},{32,96},{40,104},{48,112},{56,120},{... | collective-permute-start | bytes 107528 | tf_op jit(solution)/shard_map/ppermute | solution.py:47
  65.2 9.0 %collective-permute-start.4 = (f32[2,4480]{1,0:T(2,128)S(1)}, f32[2,4480]{1,0:T(2,128)}, u32[]{:S(2)}, u32[]{:S(2)}) collective-permute-start(f32[2,4480]{1,0:T(2,128)S(1)} %add.137), channel_id=1, source_target_pairs={{0,128},{8,136},{16,144},{24,152},{32,160},{40,168},{48,176},{56,1... | collective-permute-start | bytes 107528 | tf_op jit(solution)/shard_map/ppermute | solution.py:47
  77.5 0.6 copy-start.7
  77.5 2.4 %copy-start.8 = (f32[2]{0:T(128)}, f32[2]{0:T(128)S(1)}, u32[]{:S(2)}) copy-start(f32[2]{0:T(128)S(1)} %get-tuple-element.6) | copy-start | bytes 28
  79.9 5.4 %copy-start.12 = (pred[2,1024]{1,0:T(4,128)(4,1)S(1)}, pred[2,1024]{1,0:T(4,128)(4,1)}, u32[]{:S(2)}) copy-start(pred[2,1024]{1,0:T(4,128)(4,1)} %iota_compare_fusion.3) | copy-start | bytes 6148
  82.7 4.1 %copy-start.5 = (f32[2560]{0:T(1024)S(1)}, f32[2560]{0:T(1024)}, u32[]{:S(2)}) copy-start(f32[2560]{0:T(1024)} %get-tuple-element.9) | copy-start | bytes 30724
  86.1 0.6 copy-start.11
  86.2 27.5 %copy-start.1 = (bf16[2,5,1024,128]{3,2,1,0:T(8,128)(2,1)}, bf16[2,5,1024,128]{3,2,1,0:T(8,128)(2,1)S(1)}, u32[]{:S(2)}) copy-start(bf16[2,5,1024,128]{3,2,1,0:T(8,128)(2,1)S(1)} %dynamic_update_slice.15) | copy-start | bytes 7864324
  86.2 0.7 copy-start.6
  86.8 38.5 %copy-start.14 = (s32[64]{0:T(128)S(1)}, s32[64]{0:T(128)}, u32[]{:S(2)}) copy-start(s32[64]{0:T(128)} %param.33) | copy-start | bytes 772
  86.8 38.5 %copy-start.15 = (f32[160]{0:T(256)S(1)}, f32[160]{0:T(256)}, u32[]{:S(2)}) copy-start(f32[160]{0:T(256)} %param.29) | copy-start | bytes 1924
  113.7 1.3 %collective-permute-start.5 = (f32[64,160]{1,0:T(8,128)S(1)}, f32[64,160]{1,0:T(8,128)S(1)}, u32[]{:S(2)}, u32[]{:S(2)}) collective-permute-start(f32[64,160]{1,0:T(8,128)S(1)} %convolution_add_fusion.1), channel_id=1, source_target_pairs={{0,1},{1,0},{2,3},{3,2},{4,5},{5,4},{6,7},{7,6},{8,9},{9,8},{10,11... | collective-permute-start | bytes 122888 | tf_op jit(solution)/shard_map/ppermute | solution.py:47
  115.1 4.4 %collective-permute-start.6 = (f32[64,160]{1,0:T(8,128)S(1)}, f32[64,160]{1,0:T(8,128)S(1)}, u32[]{:S(2)}, u32[]{:S(2)}) collective-permute-start(f32[64,160]{1,0:T(8,128)S(1)} %add.154), channel_id=1, source_target_pairs={{0,2},{1,3},{2,0},{3,1},{4,6},{5,7},{6,4},{7,5},{8,10},{9,11},{10,... | collective-permute-start | bytes 122888 | tf_op jit(solution)/shard_map/ppermute | solution.py:47
  119.4 5.9 %collective-permute-start.7 = (f32[64,160]{1,0:T(8,128)S(1)}, f32[64,160]{1,0:T(8,128)S(1)}, u32[]{:S(2)}, u32[]{:S(2)}) collective-permute-start(f32[64,160]{1,0:T(8,128)S(1)} %add.155), channel_id=1, source_target_pairs={{0,4},{1,5},{2,6},{3,7},{4,0},{5,1},{6,2},{7,3},{8,12},{9,13},{10,... | collective-permute-start | bytes 122888 | tf_op jit(solution)/shard_map/ppermute | solution.py:47

commit v5 on v3

--- a/solution.py
+++ b/solution.py
@@ -54,17 +54,6 @@
     return jnp.sum(lax.all_to_all(spread, axis, 0, 0, tiled=False), axis=0)
 
 
-def exchange_scatter_sum(x, axis, size):
-    blocks = x.reshape((size, x.shape[0] // size) + x.shape[1:])
-    return jnp.sum(lax.all_to_all(blocks, axis, 0, 0, tiled=False), axis=0)
-
-
-def exchange_gather(x, axis, size):
-    spread = jnp.broadcast_to(x[None], (size,) + x.shape)
-    out = lax.all_to_all(spread, axis, 0, 0, tiled=False)
-    return out.reshape((size * x.shape[0],) + x.shape[1:])
-
-
 def bit_order(size, first):
     bits = [b for b in first if (1 << b) < size]
     return bits + [b for b in range(size.bit_length() - 1) if b not in bits]
@@ -116,24 +105,27 @@
     slot_len = jnp.sum(jnp.where(matches, lengths[:, None], 0), axis=0)
     my_len = lax.dynamic_slice_in_dim(slot_len, lax.axis_index("gx") * rows_dev, rows_dev, 0)
     qkv_cols = w_qkv.shape[1]
+    blocks = (gx_size, requests // gx_size, attn_slot.shape[1])
     partial = jnp.concatenate(
         [
-            jnp.dot(attn_slot, w_qkv, preferred_element_type=jnp.float32),
-            jnp.dot(mlp_slot, w_up, preferred_element_type=jnp.float32),
+            jnp.einsum(
+                "sbk,kn->sbn", attn_slot.reshape(blocks), w_qkv, preferred_element_type=jnp.float32
+            ),
+            jnp.einsum(
+                "sbk,kn->sbn", mlp_slot.reshape(blocks), w_up, preferred_element_type=jnp.float32
+            ),
         ],
-        axis=1,
+        axis=2,
     )
-    reduced = exchange_scatter_sum(partial, "gx", gx_size)
+    reduced = jnp.sum(lax.all_to_all(partial, "gx", 0, 0, tiled=False), axis=0)
     qkv = reduced[:, :qkv_cols] + b_qkv
     up = reduced[:, qkv_cols:] + b_up
-    hidden = jax.nn.gelu(up, approximate=False).astype(jnp.bfloat16)
-    hidden_all = exchange_gather(hidden, "gx", gx_size)
     qkv = qkv.reshape(rows_dev, heads_dev, 3, HD)
     position = my_len - 1
     query = rotate(qkv[:, :, 0], position).astype(jnp.bfloat16)
     new_key = rotate(qkv[:, :, 1], position).astype(jnp.bfloat16)
     new_value = qkv[:, :, 2].astype(jnp.bfloat16)
-    new_keys = key_cache
+    new_keys = jnp.where(slot_len[0] > 0, key_cache, jnp.zeros_like(key_cache))
     new_values = value_cache
     zero_index = jnp.int32(0)
     for local_slot in range(rows_dev):
@@ -157,11 +149,20 @@
         "shp,shpd->shd", weights_low, new_values, preferred_element_type=jnp.float32
     )
     attended = (weighted / total[:, :, None]).astype(jnp.bfloat16).reshape(rows_dev, heads_dev * HD)
-    attended_all = exchange_gather(attended, "gx", gx_size)
-    mlp_part = lax.optimization_barrier(
-        jnp.dot(hidden_all, w_down, preferred_element_type=jnp.float32)
+    hidden = jax.nn.gelu(up, approximate=False).astype(jnp.bfloat16)
+    both = jnp.concatenate([attended, hidden], axis=1)
+    gathered = lax.all_to_all(
+        jnp.broadcast_to(both[None], (gx_size,) + both.shape), "gx", 0, 0, tiled=False
     )
-    slot_part = jnp.dot(attended_all, w_out, preferred_element_type=jnp.float32) + mlp_part
+    attn_cols = attended.shape[1]
+    slot_part = (
+        jnp.einsum(
+            "sbk,kn->sbn", gathered[:, :, :attn_cols], w_out, preferred_element_type=jnp.float32
+        )
+        + jnp.einsum(
+            "sbk,kn->sbn", gathered[:, :, attn_cols:], w_down, preferred_element_type=jnp.float32
+        )
+    ).reshape(requests, w_out.shape[1])
     branches = tree_sum(slot_part, "gy", gy_size, gy_bits)
     branches = jnp.dot(to_request, branches, precision=lax.Precision.HIGHEST)
     hidden_out = (wide_in + branches + b_out + b_down).astype(jnp.bfloat16)

time: 126 us -> 105 us (0.83)
  waiting for transfers between devices: 53.3 us -> 31.2 us
  blocking collectives: 20.9 us -> 40 us
  starting transfers between devices: 16.4 us -> 6.55 us
  local copies, waits for them, and re-layouts: 15.6 us -> 7.72 us
  other arithmetic: 5.62 us -> 8.7 us
  matrix products: 8.26 us -> 5.38 us
    all_to_all x3 -> x1, waiting for transfers between devices: 43.7 us -> 21.6 us  [layer(): reduced = jnp.sum(lax.all_to_all(partial, 'gx', 0, 0, tiled=False), axis=0)]
    all_to_all x0 -> x1, blocking collectives: none -> 19.2 us  [layer(): lax.all_to_all(jnp.broadcast_to(both[None], (gx_size,) + both.shape), 'gx...]
    all_to_all x3 -> x1, starting transfers between devices: 14.5 us -> 4.67 us  [layer(): reduced = jnp.sum(lax.all_to_all(partial, 'gx', 0, 0, tiled=False), axis=0)]
    reshape x3, local copies, waits for them, and re-layouts: 4.42 us -> 0.09 us  [the longest x1 0.05 us: layer(): slot_part = (jnp.einsum('sbk,kn->sbn', gathered[:, :, :attn_cols], w_out,...]
    unnamed x34 -> x39, local copies, waits for them, and re-layouts: 4.49 us -> 1.04 us
    broadcast_in_dim x2 -> x1, local copies, waits for them, and re-layouts: 2.54 us -> 0.21 us  [layer(): jnp.broadcast_to(both[None], (gx_size,) + both.shape)]
    dot_general x4 -> x6, matrix products: 3.75 us -> 1.58 us  [the longest x1 0.39 us: layer(): jnp.einsum('sbk,kn->sbn', gathered[:, :, attn_cols:], w_down, preferred_e...]
    concatenate x0 -> x1, local copies, waits for them, and re-layouts: none -> 1.89 us  [layer(): jnp.concatenate([jnp.einsum('sbk,kn->sbn', attn_slot.reshape(blocks), w_q...]
  transfers between devices with their start and end apart: 6 -> 4, of which waited for: 6 -> 4; matrix products, arithmetic and copies ran while one was open for 3% -> 4% of each run, Pallas kernels for 0% -> 0%
where the time goes in v5:
time: 105 us
  blocking collectives  40 us (38%)
  waiting for transfers between devices  31.2 us (30%)
  other arithmetic  8.7 us (8%)
  local copies, waits for them, and re-layouts  7.72 us (7%)
  starting transfers between devices  6.55 us (6%)
  matrix products  5.38 us (5%)
  between operations  5.02 us (5%)
    all_to_all x1, waiting for transfers between devices, layer(): reduced = jnp.sum(lax.all_to_all(partial, 'gx', 0, 0, tiled=False), axis=0)  21.6 us
    all_to_all x1, blocking collectives, exchange_sum(): return jnp.sum(lax.all_to_all(spread, axis, 0, 0, tiled=False), axis=0)  20.9 us
    all_to_all x1, blocking collectives, layer(): lax.all_to_all(jnp.broadcast_to(both[None], (gx_size,) + both.shape), 'gx...  19.2 us
    ppermute x3, waiting for transfers between devices, tree_sum(): x = x + lax.ppermute(x, axis, xor_pairs(size, bit))  9.66 us
    all_to_all x1, starting transfers between devices, layer(): reduced = jnp.sum(lax.all_to_all(partial, 'gx', 0, 0, tiled=False), axis=0)  4.67 us
    dynamic_update_slice x2, local copies, waits for them, and re-layouts, layer(): lax.dynamic_update_slice(new_keys, new_key[local_slot][None, :, None, :],...  2.63 us
    dot_general x1, matrix products, block_scores(): jnp.einsum('shd,shpd->shp', query, keys, preferred_element_type=jnp.float32)  2.51 us
  transfers between devices with their start and end apart: 4, of which 4 were waited for; matrix products, arithmetic and copies ran while one was open for 4% of the time, Pallas kernels for 0%

profile of v5, /device:TPU:16, one launch (start us, length us, event | category | flops | bytes accessed | tf_op | source)
XLA Modules:
  0.0 104.7 jit_solution(1271095291729427189)
XLA Ops:
  0.7 0.8 copy-done.7
  1.7 20.9 %all_to_all.15 = f32[32,1,128]{2,1,0:T(1,128)S(1)} all-to-all(f32[32,1,128]{2,1,0:T(1,128)S(1)} %reshape.156), channel_id=1, replica_groups=mesh['gx'=32,'gy'=8] {'gx'}, dimensions={0} | all-to-all | bytes 32768 | tf_op jit(solution)/shard_map/all_to_all | solution.py:54
  22.6 0.5 broadcast.116
  23.1 0.7 reduce
  24.0 0.3 convolution_convert_fusion
  24.3 0.3 convolution_convert_fusion.1
  24.6 0.2 fusion.10
  24.9 0.3 fusion.8
  25.2 1.9 %copy.66 = f32[32,2,4480]{2,1,0:T(2,128)} copy(f32[32,2,4480]{2,0,1:T(8,128)S(1)} %pad_maximum_fusion) | data formatting | bytes 2293760 | tf_op jit(solution)/shard_map/concatenate | solution.py:109
  27.1 4.7 %all-to-all-start.1 = ((f32[32,2,4480]{2,1,0:T(2,128)}), f32[32,2,4480]{2,1,0:T(2,128)}, u32[]{:S(2)}, u32[]{:S(2)}) async-start(f32[32,2,4480]{2,1,0:T(2,128)} %copy.66), calls=%async_computation.1 | async-start | bytes 2293760 | tf_op jit(solution)/shard_map/all_to_all | solution.py:120
  32.0 0.6 fusion.61
  36.5 0.7 multiply_cosine_fusion
  37.2 0.7 iota_compare_fusion.4
  37.9 1.7 %broadcast_select_fusion = bf16[2,5,1024,128]{3,2,1,0:T(8,128)(2,1)} fusion(bf16[2,5,1024,128]{3,2,1,0:T(8,128)(2,1)S(1)} %copy-done.3, pred[]{:T(512)} %bitcast.8), kind=kLoop, calls=%fused_computation.1 | loop fusion | flops 1310720 | bytes 5242881 | tf_op jit(solution)/shard_map/jit(_where)/select_n | solution.py:128
  39.5 21.6 %all-to-all-done.1 = f32[32,2,4480]{2,1,0:T(2,128)} async-done(((f32[32,2,4480]{2,1,0:T(2,128)}), f32[32,2,4480]{2,1,0:T(2,128)}, u32[]{:S(2)}, u32[]{:S(2)}) %all-to-all-start.1) | async-done | bytes 1146912 | tf_op jit(solution)/shard_map/all_to_all | solution.py:120
  61.1 1.6 %reduce_sum.58 = f32[2,4480]{1,0:T(2,128)S(1)} reduce(f32[32,2,4480]{2,1,0:T(2,128)} %all-to-all-done.1, f32[]{:T(128)} %constant.12.clone.1), dimensions={0}, to_apply=%region_4.5 | reduce | flops 277760 | bytes 1182724 | tf_op jit(solution)/shard_map/reduce_sum | solution.py:120
  62.8 0.9 fusion.42
  63.9 0.7 subtract_convert_fusion.1
  64.8 1.3 %dynamic_update_slice.12 = bf16[2,5,1024,128]{3,2,1,0:T(8,128)(2,1)} dynamic-update-slice(bf16[2,5,1024,128]{3,2,1,0:T(8,128)(2,1)} %broadcast_select_fusion, bf16[1,5,1,128]{3,2,1,0:T(2,128)(2,1)S(1)} %get-tuple-element.18, s32[]{:T(128)} %constant.47.clone.1, s32[]{:T(128)} %constant.47.clone.1, s32[]{:T(128)S(6)} %select_n.34, s32[]{:T(128)} %constant.47.clone.1) | dynamic-update-slice | bytes 2564 | tf_op jit(solution)/shard_map/dynamic_update_slice | solution.py:133
  66.1 1.3 %dynamic_update_slice.13 = bf16[2,5,1024,128]{3,2,1,0:T(8,128)(2,1)} dynamic-update-slice(bf16[2,5,1024,128]{3,2,1,0:T(8,128)(2,1)} %dynamic_update_slice.12, bf16[1,5,1,128]{3,2,1,0:T(2,128)(2,1)S(1)} %get-tuple-element.17, s32[]{:T(128)} %constant.21.clone.1, s32[]{:T(128)} %constant.47.clone.1, s32[]{:T(128)S(6)} %select_n.35, s32[]{:T(128)} %constant.47.clone.1) | dynamic-update-slice | bytes 2564 | tf_op jit(solution)/shard_map/dynamic_update_slice | solution.py:133
  67.4 2.5 %fusion.51 = f32[2,5,1,1024]{3,2,1,0:T(1,128)S(1)} fusion(bf16[2,5,1024,128]{3,2,1,0:T(8,128)(2,1)} %dynamic_update_slice.13, bf16[2,5,128,1]{2,0,1,3:T(2,128)(2,1)S(1)} %maximum_bitcast_fusion), kind=kOutput, calls=%fused_computation.75 | convolution fusion | flops 2621440 | bytes 2664960 | tf_op jit(solution)/shard_map/shd,shpd->shp/dot_general | solution.py:34
  69.9 1.0 fusion.6
  71.2 0.4 fusion.26
  72.0 19.2 %all_to_all.16 = bf16[32,2,3200]{2,1,0:T(2,128)(2,1)S(1)} all-to-all(bf16[32,2,3200]{2,1,0:T(2,128)(2,1)S(1)} %broadcast_in_dim.43), channel_id=1, replica_groups=mesh['gx'=32,'gy'=8] {'gx'}, dimensions={0} | all-to-all | bytes 819200 | tf_op jit(solution)/shard_map/all_to_all | solution.py:154
  91.4 0.3 slice.109
  91.7 0.4 convolution_add_fusion.1
  92.3 1.2 %collective-permute-done = f32[64,160]{1,0:T(8,128)S(1)} collective-permute-done((f32[64,160]{1,0:T(8,128)S(1)}, f32[64,160]{1,0:T(8,128)S(1)}, u32[]{:S(2)}, u32[]{:S(2)}) %collective-permute-start) | collective-permute-done | bytes 40992 | tf_op jit(solution)/shard_map/ppermute | solution.py:48
  93.6 1.4 %collective-permute-start.1 = (f32[64,160]{1,0:T(8,128)S(1)}, f32[64,160]{1,0:T(8,128)S(1)}, u32[]{:S(2)}, u32[]{:S(2)}) collective-permute-start(f32[64,160]{1,0:T(8,128)S(1)} %add.107), channel_id=1, source_target_pairs={{0,2},{1,3},{2,0},{3,1},{4,6},{5,7},{6,4},{7,5},{8,10},{9,11},{10,... | collective-permute-start | bytes 122888 | tf_op jit(solution)/shard_map/ppermute | solution.py:48
  94.9 3.0 %collective-permute-done.1 = f32[64,160]{1,0:T(8,128)S(1)} collective-permute-done((f32[64,160]{1,0:T(8,128)S(1)}, f32[64,160]{1,0:T(8,128)S(1)}, u32[]{:S(2)}, u32[]{:S(2)}) %collective-permute-start.1) | collective-permute-done | bytes 40992 | tf_op jit(solution)/shard_map/ppermute | solution.py:48
  97.9 0.4 collective-permute-start.2
  98.4 5.4 %collective-permute-done.2 = f32[64,160]{1,0:T(8,128)S(1)} collective-permute-done((f32[64,160]{1,0:T(8,128)S(1)}, f32[64,160]{1,0:T(8,128)S(1)}, u32[]{:S(2)}, u32[]{:S(2)}) %collective-permute-start.2) | collective-permute-done | bytes 40992 | tf_op jit(solution)/shard_map/ppermute | solution.py:48
  103.8 0.8 fusion.4
  (76 shorter events, 2.2 us)
Async XLA Ops:
  0.6 24.2 %copy-start = (bf16[160,2560]{1,0:T(8,128)(2,1)S(1)}, bf16[160,2560]{1,0:T(8,128)(2,1)}, u32[]{:S(2)}) copy-start(bf16[160,2560]{1,0:T(8,128)(2,1)} %param.26) | copy-start | bytes 2457604
  0.6 0.8 copy-start.7
  0.7 23.6 %copy-start.16 = (f32[160]{0:T(256)S(1)}, f32[160]{0:T(256)}, u32[]{:S(2)}) copy-start(f32[160]{0:T(256)} %param.18) | copy-start | bytes 1924
  0.7 23.6 %copy-start.15 = (f32[160]{0:T(256)S(1)}, f32[160]{0:T(256)}, u32[]{:S(2)}) copy-start(f32[160]{0:T(256)} %param.19) | copy-start | bytes 1924
  0.7 23.3 %copy-start.14 = (f32[160]{0:T(256)S(1)}, f32[160]{0:T(256)}, u32[]{:S(2)}) copy-start(f32[160]{0:T(256)} %param.20) | copy-start | bytes 1924
  0.7 23.3 %copy-start.13 = (f32[160]{0:T(256)S(1)}, f32[160]{0:T(256)}, u32[]{:S(2)}) copy-start(f32[160]{0:T(256)} %param.21) | copy-start | bytes 1924
  0.7 23.9 %copy-start.5 = (bf16[160,1920]{1,0:T(8,128)(2,1)S(1)}, bf16[160,1920]{1,0:T(8,128)(2,1)}, u32[]{:S(2)}) copy-start(bf16[160,1920]{1,0:T(8,128)(2,1)} %param.22) | copy-start | bytes 1843204
  0.7 23.3 %copy-start.11 = (s32[64]{0:T(128)S(1)}, s32[64]{0:T(128)}, u32[]{:S(2)}) copy-start(s32[64]{0:T(128)} %param.33) | copy-start | bytes 772
  25.2 6.6 %copy-start.17 = (s32[64]{0:T(128)S(1)}, s32[64]{0:T(128)}, u32[]{:S(2)}) copy-start(s32[64]{0:T(128)} %param.32) | copy-start | bytes 772
  25.2 12.6 %copy-start.3 = (bf16[2,5,1024,128]{3,2,1,0:T(8,128)(2,1)S(1)}, bf16[2,5,1024,128]{3,2,1,0:T(8,128)(2,1)}, u32[]{:S(2)}) copy-start(bf16[2,5,1024,128]{3,2,1,0:T(8,128)(2,1)} %param.30) | copy-start | bytes 7864324
  27.1 34.0 %all-to-all-start.1 = ((f32[32,2,4480]{2,1,0:T(2,128)}), f32[32,2,4480]{2,1,0:T(2,128)}, u32[]{:S(2)}, u32[]{:S(2)}) async-start(f32[32,2,4480]{2,1,0:T(2,128)} %copy.66), calls=%async_computation.1 | async-start | bytes 2293760 | tf_op jit(solution)/shard_map/all_to_all | solution.py:120
  37.9 24.9 %copy-start.8 = (f32[1920]{0:T(1024)S(1)}, f32[1920]{0:T(1024)}, u32[]{:S(2)}) copy-start(f32[1920]{0:T(1024)} %param.23) | copy-start | bytes 23044
  39.5 31.6 %copy-start.2 = (bf16[2,5,1024,128]{3,2,1,0:T(8,128)(2,1)S(1)}, bf16[2,5,1024,128]{3,2,1,0:T(8,128)(2,1)}, u32[]{:S(2)}) copy-start(bf16[2,5,1024,128]{3,2,1,0:T(8,128)(2,1)} %param.31) | copy-start | bytes 7864324
  71.2 20.9 %copy-start.1 = (bf16[2,5,1024,128]{3,2,1,0:T(8,128)(2,1)}, bf16[2,5,1024,128]{3,2,1,0:T(8,128)(2,1)S(1)}, u32[]{:S(2)}) copy-start(bf16[2,5,1024,128]{3,2,1,0:T(8,128)(2,1)S(1)} %dynamic_update_slice.15) | copy-start | bytes 7864324
  71.2 20.0 %copy-start.6 = (bf16[640,160]{0,1:T(8,128)(2,1)S(1)}, bf16[640,160]{0,1:T(8,128)(2,1)}, u32[]{:S(2)}) copy-start(bf16[640,160]{0,1:T(8,128)(2,1)} %param.24) | copy-start | bytes 614404
  71.2 20.5 %copy-start.4 = (bf16[2560,160]{0,1:T(8,128)(2,1)S(1)}, bf16[2560,160]{0,1:T(8,128)(2,1)}, u32[]{:S(2)}) copy-start(bf16[2560,160]{0,1:T(8,128)(2,1)} %param.28) | copy-start | bytes 2457604
  71.7 32.1 %copy-start.9 = (f32[160]{0:T(256)S(1)}, f32[160]{0:T(256)}, u32[]{:S(2)}) copy-start(f32[160]{0:T(256)} %param.29) | copy-start | bytes 1924
  71.7 32.1 %copy-start.10 = (f32[160]{0:T(256)S(1)}, f32[160]{0:T(256)}, u32[]{:S(2)}) copy-start(f32[160]{0:T(256)} %param.25) | copy-start | bytes 1924
  71.7 32.1 %copy-start.12 = (s32[64]{0:T(128)S(1)}, s32[64]{0:T(128)}, u32[]{:S(2)}) copy-start(s32[64]{0:T(128)} %param.33) | copy-start | bytes 772
  92.2 1.3 %collective-permute-start = (f32[64,160]{1,0:T(8,128)S(1)}, f32[64,160]{1,0:T(8,128)S(1)}, u32[]{:S(2)}, u32[]{:S(2)}) collective-permute-start(f32[64,160]{1,0:T(8,128)S(1)} %reshape.147), channel_id=1, source_target_pairs={{0,1},{1,0},{2,3},{3,2},{4,5},{5,4},{6,7},{7,6},{8,9},{9,8},{10,11... | collective-permute-start | bytes 122888 | tf_op jit(solution)/shard_map/ppermute | solution.py:48
  93.6 4.4 %collective-permute-start.1 = (f32[64,160]{1,0:T(8,128)S(1)}, f32[64,160]{1,0:T(8,128)S(1)}, u32[]{:S(2)}, u32[]{:S(2)}) collective-permute-start(f32[64,160]{1,0:T(8,128)S(1)} %add.107), channel_id=1, source_target_pairs={{0,2},{1,3},{2,0},{3,1},{4,6},{5,7},{6,4},{7,5},{8,10},{9,11},{10,... | collective-permute-start | bytes 122888 | tf_op jit(solution)/shard_map/ppermute | solution.py:48
  97.9 5.9 %collective-permute-start.2 = (f32[64,160]{1,0:T(8,128)S(1)}, f32[64,160]{1,0:T(8,128)S(1)}, u32[]{:S(2)}, u32[]{:S(2)}) collective-permute-start(f32[64,160]{1,0:T(8,128)S(1)} %add.108), channel_id=1, source_target_pairs={{0,4},{1,5},{2,6},{3,7},{4,0},{5,1},{6,2},{7,3},{8,12},{9,13},{10,... | collective-permute-start | bytes 122888 | tf_op jit(solution)/shard_map/ppermute | solution.py:48

commit v6 on v5

--- a/solution.py
+++ b/solution.py
@@ -43,20 +43,22 @@
     return [(i, i ^ (1 << bit)) for i in range(size)]
 
 
-def tree_sum(x, axis, size, bits):
-    for bit in bits:
-        x = x + lax.ppermute(x, axis, xor_pairs(size, bit))
-    return x
-
-
 def exchange_sum(x, axis, size):
     spread = jnp.broadcast_to(x[None], (size,) + x.shape)
     return jnp.sum(lax.all_to_all(spread, axis, 0, 0, tiled=False), axis=0)
 
 
-def bit_order(size, first):
-    bits = [b for b in first if (1 << b) < size]
-    return bits + [b for b in range(size.bit_length() - 1) if b not in bits]
+def pair_sum(x, axis, rounds):
+    for pairs in rounds:
+        x = x + lax.ppermute(x, axis, pairs)
+    return x
+
+
+def gy_pairs(size):
+    rounds = [xor_pairs(size, bit) for bit in range(size.bit_length() - 1)]
+    if size == 8:
+        rounds[2] = [(i, (3 - i // 2) * 2 + i % 2) for i in range(size)]
+    return rounds
 
 
 def layer(
@@ -83,7 +85,6 @@
     requests = hidden_in.shape[0]
     rows_dev = key_cache.shape[0]
     heads_dev = key_cache.shape[1]
-    gy_bits = bit_order(gy_size, (0, 1, 2))
     wide_in = hidden_in.astype(jnp.float32)
     stats = exchange_sum(
         jnp.stack([jnp.sum(wide_in, axis=1), jnp.sum(wide_in * wide_in, axis=1)]),
@@ -126,7 +127,7 @@
     new_key = rotate(qkv[:, :, 1], position).astype(jnp.bfloat16)
     new_value = qkv[:, :, 2].astype(jnp.bfloat16)
     new_keys = jnp.where(slot_len[0] > 0, key_cache, jnp.zeros_like(key_cache))
-    new_values = value_cache
+    new_values = jnp.where(slot_len[0] > 0, value_cache, jnp.zeros_like(value_cache))
     zero_index = jnp.int32(0)
     for local_slot in range(rows_dev):
         slot_index = jnp.int32(local_slot)
@@ -140,14 +141,27 @@
             new_value[local_slot][None, :, None, :],
             (slot_index, zero_index, position[local_slot], zero_index),
         )
-    scores, valid = block_scores(query, new_keys, my_len)
+    old_scores, valid = block_scores(query, key_cache, my_len)
+    fresh = jnp.einsum(
+        "shd,shd->sh", query, new_key, preferred_element_type=jnp.float32
+    ) * HD ** (-0.5)
+    places = lax.iota(jnp.int32, key_cache.shape[2])
+    scores = jnp.where(
+        places[None, None, :] == position[:, None, None], fresh[:, :, None], old_scores
+    )
     top_score = jnp.max(scores, axis=2)
     weights = jnp.where(valid, jnp.exp(scores - top_score[:, :, None]), 0.0)
     total = jnp.sum(weights, axis=2)
     weights_low = weights.astype(jnp.bfloat16)
+    at_new = places[None, None, :] == position[:, None, None]
     weighted = jnp.einsum(
-        "shp,shpd->shd", weights_low, new_values, preferred_element_type=jnp.float32
-    )
+        "shp,shpd->shd",
+        jnp.where(at_new, jnp.zeros_like(weights_low), weights_low),
+        value_cache,
+        preferred_element_type=jnp.float32,
+    ) + jnp.sum(
+        jnp.where(at_new, weights_low, jnp.zeros_like(weights_low)).astype(jnp.float32), axis=2
+    )[:, :, None] * new_value.astype(jnp.float32)
     attended = (weighted / total[:, :, None]).astype(jnp.bfloat16).reshape(rows_dev, heads_dev * HD)
     hidden = jax.nn.gelu(up, approximate=False).astype(jnp.bfloat16)
     both = jnp.concatenate([attended, hidden], axis=1)
@@ -163,7 +177,7 @@
             "sbk,kn->sbn", gathered[:, :, attn_cols:], w_down, preferred_element_type=jnp.float32
         )
     ).reshape(requests, w_out.shape[1])
-    branches = tree_sum(slot_part, "gy", gy_size, gy_bits)
+    branches = pair_sum(slot_part, "gy", gy_pairs(gy_size))
     branches = jnp.dot(to_request, branches, precision=lax.Precision.HIGHEST)
     hidden_out = (wide_in + branches + b_out + b_down).astype(jnp.bfloat16)
     return (hidden_out, new_keys, new_values)

time: 105 us -> 113 us (1.076)
  the two profiles are of different devices: /device:TPU:16 before, /device:TPU:1 now
where the time goes in v6:
time: 113 us; the launch traced here: 112 us
  waiting for transfers between devices  36.9 us (33%)
  blocking collectives  20.3 us (18%)
  starting transfers between devices  20.2 us (18%)
  local copies, waits for them, and re-layouts  12.2 us (11%)
  other arithmetic  9.1 us (8%)
  matrix products  8.32 us (7%)
  between operations  4.65 us (4%)
    all_to_all x1, waiting for transfers between devices, layer(): reduced = jnp.sum(lax.all_to_all(partial, 'gx', 0, 0, tiled=False), axis=0)  26.9 us
    all_to_all x1, blocking collectives, exchange_sum(): return jnp.sum(lax.all_to_all(spread, axis, 0, 0, tiled=False), axis=0)  20.3 us
    ppermute x3, starting transfers between devices, pair_sum(): x = x + lax.ppermute(x, axis, pairs)  8.67 us
    all_to_all x1, waiting for transfers between devices, layer(): lax.all_to_all(jnp.broadcast_to(both[None], (gx_size,) + both.shape), 'gx...  7.64 us
    all_to_all x1, starting transfers between devices, layer(): lax.all_to_all(jnp.broadcast_to(both[None], (gx_size,) + both.shape), 'gx...  6.88 us
    all_to_all x1, starting transfers between devices, layer(): reduced = jnp.sum(lax.all_to_all(partial, 'gx', 0, 0, tiled=False), axis=0)  4.67 us
    select_n x1, other arithmetic, layer(): jnp.where(slot_len[0] > 0, value_cache, jnp.zeros_like(value_cache))  4.44 us
    dynamic_update_slice x2, local copies, waits for them, and re-layouts, layer(): lax.dynamic_update_slice(new_values, new_value[local_slot][None, :, None,...  2.63 us
  transfers between devices with their start and end apart: 5, of which 3 were waited for; matrix products, arithmetic and copies ran while one was open for 10% of the time, Pallas kernels for 0%

profile of v6, /device:TPU:1, one launch (start us, length us, event | category | flops | bytes accessed | tf_op | source)
XLA Modules:
  0.0 111.6 jit_solution(17553942546527596407)
XLA Ops:
  0.6 0.9 convert_reduce_fusion
  1.7 20.3 %all_to_all.15 = f32[32,1,128]{2,1,0:T(1,128)S(1)} all-to-all(f32[32,1,128]{2,1,0:T(1,128)S(1)} %reshape.185), channel_id=1, replica_groups=mesh['gx'=32,'gy'=8] {'gx'}, dimensions={0} | all-to-all | bytes 32768 | tf_op jit(solution)/shard_map/all_to_all | solution.py:48
  22.0 0.5 broadcast.147
  22.5 0.7 reduce.2
  23.3 1.0 convolution_convert_fusion
  24.4 1.0 convolution_convert_fusion.1
  25.5 1.3 %fusion.10 = f32[32,2,1920]{2,0,1:T(8,128)S(1)} fusion(bf16[160,1920]{1,0:T(8,128)(2,1)} %param.22, bf16[32,2,160]{2,1,0:T(2,128)(2,1)S(1)} %reshape.168), kind=kOutput, calls=%fused_computation.17 | convolution fusion | flops 39321600 | bytes 1126400 | tf_op jit(solution)/shard_map/sbk,kn->sbn/dot_general | solution.py:112
  27.2 1.9 %copy.81 = f32[32,2,4480]{2,1,0:T(2,128)} copy(f32[32,2,4480]{2,0,1:T(8,128)S(1)} %pad_maximum_fusion) | data formatting | bytes 2293760 | tf_op jit(solution)/shard_map/concatenate | solution.py:110
  29.1 4.7 %all-to-all-start.1 = ((f32[32,2,4480]{2,1,0:T(2,128)}), f32[32,2,4480]{2,1,0:T(2,128)}, u32[]{:S(2)}, u32[]{:S(2)}) async-start(f32[32,2,4480]{2,1,0:T(2,128)} %copy.81), calls=%async_computation.1 | async-start | bytes 2293760 | tf_op jit(solution)/shard_map/all_to_all | solution.py:121
  34.2 26.9 %all-to-all-done.1 = f32[32,2,4480]{2,1,0:T(2,128)} async-done(((f32[32,2,4480]{2,1,0:T(2,128)}), f32[32,2,4480]{2,1,0:T(2,128)}, u32[]{:S(2)}, u32[]{:S(2)}) %all-to-all-start.1) | async-done | bytes 1146912 | tf_op jit(solution)/shard_map/all_to_all | solution.py:121
  61.1 1.6 %reduce_sum.67 = f32[2,4480]{1,0:T(2,128)S(1)} reduce(f32[32,2,4480]{2,1,0:T(2,128)} %all-to-all-done.1, f32[]{:T(128)} %constant.12.clone.1), dimensions={0}, to_apply=%region_4.5 | reduce | flops 277760 | bytes 1182724 | tf_op jit(solution)/shard_map/reduce_sum | solution.py:121
  63.5 0.8 fusion.53
  64.2 0.3 convert_reduce_fusion.1
  64.7 0.4 fusion.27
  65.3 1.0 broadcast_in_dim.67
  66.3 6.9 %all-to-all-start.2 = ((bf16[32,2,3200]{2,1,0:T(2,128)(2,1)}), bf16[32,2,3200]{2,1,0:T(2,128)(2,1)}, u32[]{:S(2)}, u32[]{:S(2)}) async-start(bf16[32,2,3200]{2,1,0:T(2,128)(2,1)} %broadcast_in_dim.67), calls=%async_computation.2 | async-start | bytes 819200 | tf_op jit(solution)/shard_map/all_to_all | solution.py:168
  73.2 4.4 %broadcast_select_fusion = (bf16[2,5,1024,128]{3,2,1,0:T(8,128)(2,1)}, bf16[2,5,1024,128]{3,2,1,0:T(8,128)(2,1)}) fusion(bf16[2,5,1024,128]{3,2,1,0:T(8,128)(2,1)} %param.31, pred[]{:T(512)} %bitcast.17, bf16[2,5,1024,128]{3,2,1,0:T(8,128)(2,1)S(1)} %copy-done.1), kind=kLoop, calls=%fused_computation.1 | loop fusion | flops 2621440 | bytes 10485761 | tf_op jit(solution)/shard_map/jit(_where)/select_n | solution.py:130
  77.6 7.6 %all-to-all-done.2 = bf16[32,2,3200]{2,1,0:T(2,128)(2,1)} async-done(((bf16[32,2,3200]{2,1,0:T(2,128)(2,1)}), bf16[32,2,3200]{2,1,0:T(2,128)(2,1)}, u32[]{:S(2)}, u32[]{:S(2)}) %all-to-all-start.2) | async-done | bytes 409632 | tf_op jit(solution)/shard_map/all_to_all | solution.py:168
  85.3 0.9 slice.109
  86.2 1.1 fusion.13
  87.3 1.2 %slice.110 = bf16[32,2,2560]{2,1,0:T(2,128)(2,1)S(1)} slice(bf16[32,2,3200]{2,1,0:T(2,128)(2,1)} %all-to-all-done.2), slice={[0:32], [0:2], [640:3200]} | slice | bytes 655360 | tf_op jit(solution)/shard_map/slice | solution.py:177
  88.6 1.5 %convolution_add_fusion.1 = f32[32,2,160]{2,0,1:T(8,128)S(1)} fusion(f32[32,2,160]{2,0,1:T(8,128)S(1)} %fusion.13, bf16[2560,160]{0,1:T(8,128)(2,1)} %param.28, bf16[32,2,2560]{2,1,0:T(2,128)(2,1)S(1)} %slice.110), kind=kOutput, calls=%fused_computation.7 | convolution fusion | flops 52439040 | bytes 1228800 | tf_op jit(solution)/shard_map/sbk,kn->sbn/dot_general | solution.py:176
  90.2 4.5 %collective-permute-start = (f32[64,160]{1,0:T(8,128)S(1)}, f32[64,160]{1,0:T(8,128)S(1)}, u32[]{:S(2)}, u32[]{:S(2)}) collective-permute-start(f32[64,160]{1,0:T(8,128)S(1)} %reshape.172), channel_id=1, source_target_pairs={{0,1},{1,0},{2,3},{3,2},{4,5},{5,4},{6,7},{7,6},{8,9},{9,8},{10,11... | collective-permute-start | bytes 122888 | tf_op jit(solution)/shard_map/ppermute | solution.py:53
  94.7 0.6 fusion.63
  98.9 1.4 %collective-permute-start.1 = (f32[64,160]{1,0:T(8,128)S(1)}, f32[64,160]{1,0:T(8,128)S(1)}, u32[]{:S(2)}, u32[]{:S(2)}) collective-permute-start(f32[64,160]{1,0:T(8,128)S(1)} %add.109), channel_id=1, source_target_pairs={{0,2},{1,3},{2,0},{3,1},{4,6},{5,7},{6,4},{7,5},{8,10},{9,11},{10,... | collective-permute-start | bytes 122888 | tf_op jit(solution)/shard_map/ppermute | solution.py:53
  100.3 2.3 %collective-permute-done.1 = f32[64,160]{1,0:T(8,128)S(1)} collective-permute-done((f32[64,160]{1,0:T(8,128)S(1)}, f32[64,160]{1,0:T(8,128)S(1)}, u32[]{:S(2)}, u32[]{:S(2)}) %collective-permute-start.1) | collective-permute-done | bytes 40992 | tf_op jit(solution)/shard_map/ppermute | solution.py:53
  102.7 2.8 %collective-permute-start.2 = (f32[64,160]{1,0:T(8,128)S(1)}, f32[64,160]{1,0:T(8,128)S(1)}, u32[]{:S(2)}, u32[]{:S(2)}) collective-permute-start(f32[64,160]{1,0:T(8,128)S(1)} %add.110), channel_id=1, source_target_pairs={{0,6},{1,7},{2,4},{3,5},{4,2},{5,3},{6,0},{7,1},{8,14},{9,15},{10,... | collective-permute-start | bytes 122888 | tf_op jit(solution)/shard_map/ppermute | solution.py:53
  105.5 1.3 %dynamic_update_slice.14 = bf16[2,5,1024,128]{3,2,1,0:T(8,128)(2,1)} dynamic-update-slice(bf16[2,5,1024,128]{3,2,1,0:T(8,128)(2,1)} %get-tuple-element.33, bf16[1,5,1,128]{3,2,1,0:T(2,128)(2,1)S(1)} %get-tuple-element.15, s32[]{:T(128)} %constant.47.clone.1, s32[]{:T(128)} %constant.47.clone.1, s32[]{:T(128)S(6)} %select_n.54, s32[]{:T(128)} %constant.47.clone.1) | dynamic-update-slice | bytes 2564 | tf_op jit(solution)/shard_map/dynamic_update_slice | solution.py:139
  106.8 1.3 %dynamic_update_slice.12 = bf16[2,5,1024,128]{3,2,1,0:T(8,128)(2,1)} dynamic-update-slice(bf16[2,5,1024,128]{3,2,1,0:T(8,128)(2,1)} %get-tuple-element.34, bf16[1,5,1,128]{3,2,1,0:T(2,128)(2,1)S(1)} %get-tuple-element.21, s32[]{:T(128)} %constant.47.clone.1, s32[]{:T(128)} %constant.47.clone.1, s32[]{:T(128)S(6)} %select_n.54, s32[]{:T(128)} %constant.47.clone.1) | dynamic-update-slice | bytes 2564 | tf_op jit(solution)/shard_map/dynamic_update_slice | solution.py:134
  108.1 1.3 %dynamic_update_slice.13 = bf16[2,5,1024,128]{3,2,1,0:T(8,128)(2,1)} dynamic-update-slice(bf16[2,5,1024,128]{3,2,1,0:T(8,128)(2,1)} %dynamic_update_slice.12, bf16[1,5,1,128]{3,2,1,0:T(2,128)(2,1)S(1)} %get-tuple-element.20, s32[]{:T(128)} %constant.104.clone.1, s32[]{:T(128)} %constant.47.clone.1, s32[]{:T(128)S(6)} %select_n.55, s32[]{:T(128)} %constant.47.clone.1) | dynamic-update-slice | bytes 2564 | tf_op jit(solution)/shard_map/dynamic_update_slice | solution.py:134
  109.4 1.3 %dynamic_update_slice.15 = bf16[2,5,1024,128]{3,2,1,0:T(8,128)(2,1)} dynamic-update-slice(bf16[2,5,1024,128]{3,2,1,0:T(8,128)(2,1)} %dynamic_update_slice.14, bf16[1,5,1,128]{3,2,1,0:T(2,128)(2,1)S(1)} %get-tuple-element.14, s32[]{:T(128)} %constant.104.clone.1, s32[]{:T(128)} %constant.47.clone.1, s32[]{:T(128)S(6)} %select_n.55, s32[]{:T(128)} %constant.47.clone.1) | dynamic-update-slice | bytes 2564 | tf_op jit(solution)/shard_map/dynamic_update_slice | solution.py:139
  110.8 0.8 fusion.4
  (59 shorter events, 2.2 us)
Async XLA Ops:
  0.6 26.2 %copy-start = (bf16[160,2560]{1,0:T(8,128)(2,1)S(1)}, bf16[160,2560]{1,0:T(8,128)(2,1)}, u32[]{:S(2)}) copy-start(bf16[160,2560]{1,0:T(8,128)(2,1)} %param.26) | copy-start | bytes 2457604
  27.1 6.7 %copy-start.8 = (s32[64]{0:T(128)S(1)}, s32[64]{0:T(128)}, u32[]{:S(2)}) copy-start(s32[64]{0:T(128)} %param.33) | copy-start | bytes 772
  27.2 6.6 %copy-start.9 = (s32[64]{0:T(128)S(1)}, s32[64]{0:T(128)}, u32[]{:S(2)}) copy-start(s32[64]{0:T(128)} %param.32) | copy-start | bytes 772
  27.2 35.5 %copy-start.4 = (f32[2560]{0:T(1024)S(1)}, f32[2560]{0:T(1024)}, u32[]{:S(2)}) copy-start(f32[2560]{0:T(1024)} %param.27) | copy-start | bytes 30724
  27.2 35.7 %copy-start.5 = (f32[1920]{0:T(1024)S(1)}, f32[1920]{0:T(1024)}, u32[]{:S(2)}) copy-start(f32[1920]{0:T(1024)} %param.23) | copy-start | bytes 23044
  27.2 36.3 %copy-start.1 = (bf16[2,5,1024,128]{3,2,1,0:T(8,128)(2,1)S(1)}, bf16[2,5,1024,128]{3,2,1,0:T(8,128)(2,1)}, u32[]{:S(2)}) copy-start(bf16[2,5,1024,128]{3,2,1,0:T(8,128)(2,1)} %param.30) | copy-start | bytes 7864324
  29.1 32.0 %all-to-all-start.1 = ((f32[32,2,4480]{2,1,0:T(2,128)}), f32[32,2,4480]{2,1,0:T(2,128)}, u32[]{:S(2)}, u32[]{:S(2)}) async-start(f32[32,2,4480]{2,1,0:T(2,128)} %copy.81), calls=%async_computation.1 | async-start | bytes 2293760 | tf_op jit(solution)/shard_map/all_to_all | solution.py:121
  63.0 1.7 %copy-start.2 = (bf16[2,5,1024,128]{3,2,1,0:T(8,128)(2,1)S(1)}, bf16[2,5,1024,128]{3,2,1,0:T(8,128)(2,1)}, u32[]{:S(2)}) copy-start(bf16[2,5,1024,128]{3,2,1,0:T(8,128)(2,1)} %param.31) | copy-start | bytes 7864324
  66.3 19.0 %all-to-all-start.2 = ((bf16[32,2,3200]{2,1,0:T(2,128)(2,1)}), bf16[32,2,3200]{2,1,0:T(2,128)(2,1)}, u32[]{:S(2)}, u32[]{:S(2)}) async-start(bf16[32,2,3200]{2,1,0:T(2,128)(2,1)} %broadcast_in_dim.67), calls=%async_computation.2 | async-start | bytes 819200 | tf_op jit(solution)/shard_map/all_to_all | solution.py:168
  77.6 33.1 %copy-start.3 = (bf16[64,160]{1,0:T(8,128)(2,1)S(1)}, bf16[64,160]{1,0:T(8,128)(2,1)}, u32[]{:S(2)}) copy-start(bf16[64,160]{1,0:T(8,128)(2,1)} %param.17) | copy-start | bytes 61444
  77.6 33.1 %copy-start.6 = (f32[160]{0:T(256)S(1)}, f32[160]{0:T(256)}, u32[]{:S(2)}) copy-start(f32[160]{0:T(256)} %param.29) | copy-start | bytes 1924
  77.6 33.1 %copy-start.7 = (f32[160]{0:T(256)S(1)}, f32[160]{0:T(256)}, u32[]{:S(2)}) copy-start(f32[160]{0:T(256)} %param.25) | copy-start | bytes 1924
  90.2 8.7 %collective-permute-start = (f32[64,160]{1,0:T(8,128)S(1)}, f32[64,160]{1,0:T(8,128)S(1)}, u32[]{:S(2)}, u32[]{:S(2)}) collective-permute-start(f32[64,160]{1,0:T(8,128)S(1)} %reshape.172), channel_id=1, source_target_pairs={{0,1},{1,0},{2,3},{3,2},{4,5},{5,4},{6,7},{7,6},{8,9},{9,8},{10,11... | collective-permute-start | bytes 122888 | tf_op jit(solution)/shard_map/ppermute | solution.py:53
  98.9 3.7 %collective-permute-start.1 = (f32[64,160]{1,0:T(8,128)S(1)}, f32[64,160]{1,0:T(8,128)S(1)}, u32[]{:S(2)}, u32[]{:S(2)}) collective-permute-start(f32[64,160]{1,0:T(8,128)S(1)} %add.109), channel_id=1, source_target_pairs={{0,2},{1,3},{2,0},{3,1},{4,6},{5,7},{6,4},{7,5},{8,10},{9,11},{10,... | collective-permute-start | bytes 122888 | tf_op jit(solution)/shard_map/ppermute | solution.py:53
  102.7 8.1 %collective-permute-start.2 = (f32[64,160]{1,0:T(8,128)S(1)}, f32[64,160]{1,0:T(8,128)S(1)}, u32[]{:S(2)}, u32[]{:S(2)}) collective-permute-start(f32[64,160]{1,0:T(8,128)S(1)} %add.110), channel_id=1, source_target_pairs={{0,6},{1,7},{2,4},{3,5},{4,2},{5,3},{6,0},{7,1},{8,14},{9,15},{10,... | collective-permute-start | bytes 122888 | tf_op jit(solution)/shard_map/ppermute | solution.py:53

commit v7 on v6

--- a/solution.py
+++ b/solution.py
@@ -126,21 +126,6 @@
     query = rotate(qkv[:, :, 0], position).astype(jnp.bfloat16)
     new_key = rotate(qkv[:, :, 1], position).astype(jnp.bfloat16)
     new_value = qkv[:, :, 2].astype(jnp.bfloat16)
-    new_keys = jnp.where(slot_len[0] > 0, key_cache, jnp.zeros_like(key_cache))
-    new_values = jnp.where(slot_len[0] > 0, value_cache, jnp.zeros_like(value_cache))
-    zero_index = jnp.int32(0)
-    for local_slot in range(rows_dev):
-        slot_index = jnp.int32(local_slot)
-        new_keys = lax.dynamic_update_slice(
-            new_keys,
-            new_key[local_slot][None, :, None, :],
-            (slot_index, zero_index, position[local_slot], zero_index),
-        )
-        new_values = lax.dynamic_update_slice(
-            new_values,
-            new_value[local_slot][None, :, None, :],
-            (slot_index, zero_index, position[local_slot], zero_index),
-        )
     old_scores, valid = block_scores(query, key_cache, my_len)
     fresh = jnp.einsum(
         "shd,shd->sh", query, new_key, preferred_element_type=jnp.float32
@@ -164,6 +149,9 @@
     )[:, :, None] * new_value.astype(jnp.float32)
     attended = (weighted / total[:, :, None]).astype(jnp.bfloat16).reshape(rows_dev, heads_dev * HD)
     hidden = jax.nn.gelu(up, approximate=False).astype(jnp.bfloat16)
+    at_row = (places[None, :] == position[:, None])[:, None, :, None]
+    new_keys = jnp.where(at_row, new_key[:, :, None, :], key_cache)
+    new_values = jnp.where(at_row, new_value[:, :, None, :], value_cache)
     both = jnp.concatenate([attended, hidden], axis=1)
     gathered = lax.all_to_all(
         jnp.broadcast_to(both[None], (gx_size,) + both.shape), "gx", 0, 0, tiled=False

time: 113 us -> 103 us (0.912); the launches traced: 112 us -> 103 us
  blocking collectives: 20.3 us -> 39 us
  waiting for transfers between devices: 36.9 us -> 29.6 us
  local copies, waits for them, and re-layouts: 12.2 us -> 5.02 us
  starting transfers between devices: 20.2 us -> 13.3 us
  between operations: 4.65 us -> 1.03 us
  matrix products: 8.32 us -> 6.24 us
    all_to_all x0 -> x1, blocking collectives: none -> 18.7 us  [layer(): lax.all_to_all(jnp.broadcast_to(both[None], (gx_size,) + both.shape), 'gx...]
    all_to_all x1 -> x0, waiting for transfers between devices: 7.64 us -> none  [layer(): lax.all_to_all(jnp.broadcast_to(both[None], (gx_size,) + both.shape), 'gx...]
    all_to_all x1 -> x0, starting transfers between devices: 6.88 us -> none  [layer(): lax.all_to_all(jnp.broadcast_to(both[None], (gx_size,) + both.shape), 'gx...]
    dynamic_update_slice x4 -> x0, local copies, waits for them, and re-layouts: 5.26 us -> none  [the longest x2 2.63 us: layer(): lax.dynamic_update_slice(new_values, new_value[local_slot][None, :, None,...]
    dot_general x1, matrix products: 1.54 us -> 0.38 us  [layer(): jnp.einsum('sbk,kn->sbn', gathered[:, :, attn_cols:], w_down, preferred_e...]
  transfers between devices with their start and end apart: 5 -> 4, of which waited for: 3 -> 3; matrix products, arithmetic and copies ran while one was open for 10% -> 4% of each run, Pallas kernels for 0% -> 0%
where the time goes in v7:
time: 103 us
  blocking collectives  39 us (38%)
  waiting for transfers between devices  29.6 us (29%)
  starting transfers between devices  13.3 us (13%)
  other arithmetic  8.61 us (8%)
  matrix products  6.24 us (6%)
  local copies, waits for them, and re-layouts  5.02 us (5%)
  between operations  1.03 us (1%)
    all_to_all x1, waiting for transfers between devices, layer(): reduced = jnp.sum(lax.all_to_all(partial, 'gx', 0, 0, tiled=False), axis=0)  26.9 us
    all_to_all x1, blocking collectives, exchange_sum(): return jnp.sum(lax.all_to_all(spread, axis, 0, 0, tiled=False), axis=0)  20.3 us
    all_to_all x1, blocking collectives, layer(): lax.all_to_all(jnp.broadcast_to(both[None], (gx_size,) + both.shape), 'gx...  18.7 us
    ppermute x3, starting transfers between devices, pair_sum(): x = x + lax.ppermute(x, axis, pairs)  8.67 us
    all_to_all x1, starting transfers between devices, layer(): reduced = jnp.sum(lax.all_to_all(partial, 'gx', 0, 0, tiled=False), axis=0)  4.66 us
    select_n x1, other arithmetic, layer(): new_values = jnp.where(at_row, new_value[:, :, None, :], value_cache)  3.96 us
    ppermute x3, waiting for transfers between devices, pair_sum(): x = x + lax.ppermute(x, axis, pairs)  2.72 us
  transfers between devices with their start and end apart: 4, of which 3 were waited for; matrix products, arithmetic and copies ran while one was open for 4% of the time, Pallas kernels for 0%

profile of v7, /device:TPU:1, one launch (start us, length us, event | category | flops | bytes accessed | tf_op | source)
XLA Modules:
  0.0 102.8 jit_solution(5572268852595485959)
XLA Ops:
  0.6 0.9 convert_reduce_fusion
  1.7 20.3 %all_to_all.15 = f32[32,1,128]{2,1,0:T(1,128)S(1)} all-to-all(f32[32,1,128]{2,1,0:T(1,128)S(1)} %reshape.220), channel_id=1, replica_groups=mesh['gx'=32,'gy'=8] {'gx'}, dimensions={0} | all-to-all | bytes 32768 | tf_op jit(solution)/shard_map/all_to_all | solution.py:48
  22.0 0.5 broadcast.154
  22.5 0.7 reduce.2
  23.3 1.0 convolution_convert_fusion
  24.4 1.0 convolution_convert_fusion.1
  25.5 1.3 %fusion.10 = f32[32,2,1920]{2,0,1:T(8,128)S(1)} fusion(bf16[160,1920]{1,0:T(8,128)(2,1)} %param.22, bf16[32,2,160]{2,1,0:T(2,128)(2,1)S(1)} %reshape.204), kind=kOutput, calls=%fused_computation.17 | convolution fusion | flops 39321600 | bytes 1126400 | tf_op jit(solution)/shard_map/sbk,kn->sbn/dot_general | solution.py:112
  26.8 0.3 fusion.8
  27.2 1.9 %copy.73 = f32[32,2,4480]{2,1,0:T(2,128)} copy(f32[32,2,4480]{2,0,1:T(8,128)S(1)} %pad_maximum_fusion) | data formatting | bytes 2293760 | tf_op jit(solution)/shard_map/concatenate | solution.py:110
  29.1 4.7 %all-to-all-start.1 = ((f32[32,2,4480]{2,1,0:T(2,128)}), f32[32,2,4480]{2,1,0:T(2,128)}, u32[]{:S(2)}, u32[]{:S(2)}) async-start(f32[32,2,4480]{2,1,0:T(2,128)} %copy.73), calls=%async_computation.1 | async-start | bytes 2293760 | tf_op jit(solution)/shard_map/all_to_all | solution.py:121
  34.0 0.1 multiply_cosine_fusion
  34.2 26.9 %all-to-all-done.1 = f32[32,2,4480]{2,1,0:T(2,128)} async-done(((f32[32,2,4480]{2,1,0:T(2,128)}), f32[32,2,4480]{2,1,0:T(2,128)}, u32[]{:S(2)}, u32[]{:S(2)}) %all-to-all-start.1) | async-done | bytes 1146912 | tf_op jit(solution)/shard_map/all_to_all | solution.py:121
  61.1 1.6 %reduce_sum.67 = f32[2,4480]{1,0:T(2,128)S(1)} reduce(f32[32,2,4480]{2,1,0:T(2,128)} %all-to-all-done.1, f32[]{:T(128)} %constant.11.clone.1), dimensions={0}, to_apply=%region_4.5 | reduce | flops 277760 | bytes 1182724 | tf_op jit(solution)/shard_map/reduce_sum | solution.py:121
  62.8 0.2 fusion.44
  63.3 0.2 fusion.51
  63.4 0.8 fusion.52
  64.2 0.3 convert_reduce_fusion.1
  64.6 0.4 fusion.27
  65.1 0.2 broadcast_in_dim.131
  65.3 18.7 %all_to_all.16 = bf16[32,2,3200]{2,1,0:T(2,128)(2,1)S(1)} all-to-all(bf16[32,2,3200]{2,1,0:T(2,128)(2,1)S(1)} %broadcast_in_dim.131), channel_id=1, replica_groups=mesh['gx'=32,'gy'=8] {'gx'}, dimensions={0} | all-to-all | bytes 819200 | tf_op jit(solution)/shard_map/all_to_all | solution.py:156
  84.1 0.2 fusion.13
  84.3 0.3 slice.74
  84.6 0.4 convolution_add_fusion.1
  85.0 0.7 copy.79
  85.7 0.9 reshape.208
  86.5 4.5 %collective-permute-start = (f32[64,160]{1,0:T(8,128)S(1)}, f32[64,160]{1,0:T(8,128)S(1)}, u32[]{:S(2)}, u32[]{:S(2)}) collective-permute-start(f32[64,160]{1,0:T(8,128)S(1)} %reshape.208), channel_id=1, source_target_pairs={{0,1},{1,0},{2,3},{3,2},{4,5},{5,4},{6,7},{7,6},{8,9},{9,8},{10,11... | collective-permute-start | bytes 122888 | tf_op jit(solution)/shard_map/ppermute | solution.py:53
  91.0 0.9 collective-permute-done
  91.9 1.4 %collective-permute-start.1 = (f32[64,160]{1,0:T(8,128)S(1)}, f32[64,160]{1,0:T(8,128)S(1)}, u32[]{:S(2)}, u32[]{:S(2)}) collective-permute-start(f32[64,160]{1,0:T(8,128)S(1)} %add.101), channel_id=1, source_target_pairs={{0,2},{1,3},{2,0},{3,1},{4,6},{5,7},{6,4},{7,5},{8,10},{9,11},{10,... | collective-permute-start | bytes 122888 | tf_op jit(solution)/shard_map/ppermute | solution.py:53
  93.3 1.8 %collective-permute-done.1 = f32[64,160]{1,0:T(8,128)S(1)} collective-permute-done((f32[64,160]{1,0:T(8,128)S(1)}, f32[64,160]{1,0:T(8,128)S(1)}, u32[]{:S(2)}, u32[]{:S(2)}) %collective-permute-start.1) | collective-permute-done | bytes 40992 | tf_op jit(solution)/shard_map/ppermute | solution.py:53
  95.2 2.8 %collective-permute-start.2 = (f32[64,160]{1,0:T(8,128)S(1)}, f32[64,160]{1,0:T(8,128)S(1)}, u32[]{:S(2)}, u32[]{:S(2)}) collective-permute-start(f32[64,160]{1,0:T(8,128)S(1)} %add.102), channel_id=1, source_target_pairs={{0,6},{1,7},{2,4},{3,5},{4,2},{5,3},{6,0},{7,1},{8,14},{9,15},{10,... | collective-permute-start | bytes 122888 | tf_op jit(solution)/shard_map/ppermute | solution.py:53
  98.0 4.0 %broadcast_select_fusion = (bf16[2,5,1024,128]{3,2,1,0:T(8,128)(2,1)}, bf16[2,5,1024,128]{3,2,1,0:T(8,128)(2,1)}) fusion(bf16[2,5,1024,128]{3,2,1,0:T(8,128)(2,1)} %param.31, pred[2,1024]{1,0:T(4,128)(4,1)S(1)} %get-tuple-element.30, bf16[2,5,128]{2,1,0:T(8,128)(2,1)S(1)} %copy.81, bf16[2,5,1024,128]{3,2,1,0:T(8,128)(2,1)S(1)} %copy-done.1, ...), kind=kLoop, calls=%fused_computation.1 | loop fusion | flops 2621440 | bytes 10492928 | tf_op jit(solution)/shard_map/jit(_where)/select_n | solution.py:154
  102.0 0.8 fusion.4
  (57 shorter events, 1.3 us)
Async XLA Ops:
  0.6 26.2 %copy-start = (bf16[160,2560]{1,0:T(8,128)(2,1)S(1)}, bf16[160,2560]{1,0:T(8,128)(2,1)}, u32[]{:S(2)}) copy-start(bf16[160,2560]{1,0:T(8,128)(2,1)} %param.26) | copy-start | bytes 2457604
  27.1 6.6 %copy-start.10 = (s32[64]{0:T(128)S(1)}, s32[64]{0:T(128)}, u32[]{:S(2)}) copy-start(s32[64]{0:T(128)} %param.33) | copy-start | bytes 772
  27.2 6.6 %copy-start.11 = (s32[64]{0:T(128)S(1)}, s32[64]{0:T(128)}, u32[]{:S(2)}) copy-start(s32[64]{0:T(128)} %param.32) | copy-start | bytes 772
  27.2 35.5 %copy-start.7 = (f32[1920]{0:T(1024)S(1)}, f32[1920]{0:T(1024)}, u32[]{:S(2)}) copy-start(f32[1920]{0:T(1024)} %param.23) | copy-start | bytes 23044
  27.2 35.6 %copy-start.6 = (f32[2560]{0:T(1024)S(1)}, f32[2560]{0:T(1024)}, u32[]{:S(2)}) copy-start(f32[2560]{0:T(1024)} %param.27) | copy-start | bytes 30724
  27.2 36.2 %copy-start.1 = (bf16[2,5,1024,128]{3,2,1,0:T(8,128)(2,1)S(1)}, bf16[2,5,1024,128]{3,2,1,0:T(8,128)(2,1)}, u32[]{:S(2)}) copy-start(bf16[2,5,1024,128]{3,2,1,0:T(8,128)(2,1)} %param.30) | copy-start | bytes 7864324
  29.1 32.0 %all-to-all-start.1 = ((f32[32,2,4480]{2,1,0:T(2,128)}), f32[32,2,4480]{2,1,0:T(2,128)}, u32[]{:S(2)}, u32[]{:S(2)}) async-start(f32[32,2,4480]{2,1,0:T(2,128)} %copy.73), calls=%async_computation.1 | async-start | bytes 2293760 | tf_op jit(solution)/shard_map/all_to_all | solution.py:121
  62.8 1.8 %copy-start.2 = (bf16[2,5,1024,128]{3,2,1,0:T(8,128)(2,1)S(1)}, bf16[2,5,1024,128]{3,2,1,0:T(8,128)(2,1)}, u32[]{:S(2)}) copy-start(bf16[2,5,1024,128]{3,2,1,0:T(8,128)(2,1)} %param.31) | copy-start | bytes 7864324
  64.2 19.9 %copy-start.4 = (bf16[640,160]{0,1:T(8,128)(2,1)S(1)}, bf16[640,160]{0,1:T(8,128)(2,1)}, u32[]{:S(2)}) copy-start(bf16[640,160]{0,1:T(8,128)(2,1)} %param.24) | copy-start | bytes 614404
  64.5 20.1 %copy-start.3 = (bf16[2560,160]{0,1:T(8,128)(2,1)S(1)}, bf16[2560,160]{0,1:T(8,128)(2,1)}, u32[]{:S(2)}) copy-start(bf16[2560,160]{0,1:T(8,128)(2,1)} %param.28) | copy-start | bytes 2457604
  86.5 5.4 %collective-permute-start = (f32[64,160]{1,0:T(8,128)S(1)}, f32[64,160]{1,0:T(8,128)S(1)}, u32[]{:S(2)}, u32[]{:S(2)}) collective-permute-start(f32[64,160]{1,0:T(8,128)S(1)} %reshape.208), channel_id=1, source_target_pairs={{0,1},{1,0},{2,3},{3,2},{4,5},{5,4},{6,7},{7,6},{8,9},{9,8},{10,11... | collective-permute-start | bytes 122888 | tf_op jit(solution)/shard_map/ppermute | solution.py:53
  91.9 3.2 %collective-permute-start.1 = (f32[64,160]{1,0:T(8,128)S(1)}, f32[64,160]{1,0:T(8,128)S(1)}, u32[]{:S(2)}, u32[]{:S(2)}) collective-permute-start(f32[64,160]{1,0:T(8,128)S(1)} %add.101), channel_id=1, source_target_pairs={{0,2},{1,3},{2,0},{3,1},{4,6},{5,7},{6,4},{7,5},{8,10},{9,11},{10,... | collective-permute-start | bytes 122888 | tf_op jit(solution)/shard_map/ppermute | solution.py:53
  95.2 6.8 %copy-start.5 = (bf16[64,160]{1,0:T(8,128)(2,1)S(1)}, bf16[64,160]{1,0:T(8,128)(2,1)}, u32[]{:S(2)}) copy-start(bf16[64,160]{1,0:T(8,128)(2,1)} %param.17) | copy-start | bytes 61444
  95.2 6.8 %copy-start.8 = (f32[160]{0:T(256)S(1)}, f32[160]{0:T(256)}, u32[]{:S(2)}) copy-start(f32[160]{0:T(256)} %param.29) | copy-start | bytes 1924
  95.2 6.8 %copy-start.9 = (f32[160]{0:T(256)S(1)}, f32[160]{0:T(256)}, u32[]{:S(2)}) copy-start(f32[160]{0:T(256)} %param.25) | copy-start | bytes 1924
  95.2 6.8 %collective-permute-start.2 = (f32[64,160]{1,0:T(8,128)S(1)}, f32[64,160]{1,0:T(8,128)S(1)}, u32[]{:S(2)}, u32[]{:S(2)}) collective-permute-start(f32[64,160]{1,0:T(8,128)S(1)} %add.102), channel_id=1, source_target_pairs={{0,6},{1,7},{2,4},{3,5},{4,2},{5,3},{6,0},{7,1},{8,14},{9,15},{10,... | collective-permute-start | bytes 122888 | tf_op jit(solution)/shard_map/ppermute | solution.py:53

commit v8 on v7

--- a/solution.py
+++ b/solution.py
@@ -91,18 +91,18 @@
         "gx",
         gx_size,
     )
+    slot_ids = lax.iota(jnp.int32, requests)
+    matches = assignment[:, None] == slot_ids[None, :]
+    to_request = matches.astype(jnp.float32)
+    x_slot = jnp.dot(matches.T.astype(jnp.bfloat16), hidden_in, preferred_element_type=jnp.float32)
+    w_both = jnp.concatenate([w_out, w_down], axis=0)
+    stats = jnp.sum(jnp.where(matches[None], stats[:, :, None], 0.0), axis=1)
     sum_rows, sum_squares = stats[0], stats[1]
     row_mean = sum_rows / D
     row_var = sum_squares / D - row_mean * row_mean
-    normed = (wide_in - row_mean[:, None]) * lax.rsqrt(row_var + 1e-05)[:, None]
-    attn_in = (normed * norm1_gain + norm1_bias).astype(jnp.bfloat16)
-    mlp_in = (normed * norm2_gain + norm2_bias).astype(jnp.bfloat16)
-    slot_ids = lax.iota(jnp.int32, requests)
-    matches = assignment[:, None] == slot_ids[None, :]
-    to_request = matches.astype(jnp.float32)
-    to_slot = matches.T.astype(jnp.bfloat16)
-    attn_slot = jnp.dot(to_slot, attn_in, preferred_element_type=jnp.float32).astype(jnp.bfloat16)
-    mlp_slot = jnp.dot(to_slot, mlp_in, preferred_element_type=jnp.float32).astype(jnp.bfloat16)
+    normed = (x_slot - row_mean[:, None]) * lax.rsqrt(row_var + 1e-05)[:, None]
+    attn_slot = (normed * norm1_gain + norm1_bias).astype(jnp.bfloat16)
+    mlp_slot = (normed * norm2_gain + norm2_bias).astype(jnp.bfloat16)
     slot_len = jnp.sum(jnp.where(matches, lengths[:, None], 0), axis=0)
     my_len = lax.dynamic_slice_in_dim(slot_len, lax.axis_index("gx") * rows_dev, rows_dev, 0)
     qkv_cols = w_qkv.shape[1]
@@ -156,14 +156,8 @@
     gathered = lax.all_to_all(
         jnp.broadcast_to(both[None], (gx_size,) + both.shape), "gx", 0, 0, tiled=False
     )
-    attn_cols = attended.shape[1]
-    slot_part = (
-        jnp.einsum(
-            "sbk,kn->sbn", gathered[:, :, :attn_cols], w_out, preferred_element_type=jnp.float32
-        )
-        + jnp.einsum(
-            "sbk,kn->sbn", gathered[:, :, attn_cols:], w_down, preferred_element_type=jnp.float32
-        )
+    slot_part = jnp.einsum(
+        "sbk,kn->sbn", gathered, w_both, preferred_element_type=jnp.float32
     ).reshape(requests, w_out.shape[1])
     branches = pair_sum(slot_part, "gy", gy_pairs(gy_size))
     branches = jnp.dot(to_request, branches, precision=lax.Precision.HIGHEST)

time: 103 us -> 103 us (level)
  blocking collectives: 39 us -> 18.7 us
  starting transfers between devices: 13.3 us -> 25.2 us
  waiting for transfers between devices: 29.6 us -> 37.4 us
  matrix products: 6.24 us -> 5.1 us
    all_to_all x1 -> x0, blocking collectives: 20.3 us -> none  [exchange_sum(): return jnp.sum(lax.all_to_all(spread, axis, 0, 0, tiled=False), axis=0)]
    all_to_all x0 -> x1, starting transfers between devices: none -> 11.9 us  [exchange_sum(): return jnp.sum(lax.all_to_all(spread, axis, 0, 0, tiled=False), axis=0)]
    all_to_all x0 -> x1, waiting for transfers between devices: none -> 7.8 us  [exchange_sum(): return jnp.sum(lax.all_to_all(spread, axis, 0, 0, tiled=False), axis=0)]
    dot_general x4 -> x2, matrix products: 2.62 us -> 1.48 us  [the longest x1 1.04 us: layer(): jnp.dot(matches.T.astype(jnp.bfloat16), hidden_in, preferred_element_type...]
  transfers between devices with their start and end apart: 4 -> 5, of which waited for: 3 -> 4; matrix products, arithmetic and copies ran while one was open for 4% -> 5% of each run, Pallas kernels for 0% -> 0%
where the time goes in v8:
time: 103 us; the launch traced here: 102 us
  waiting for transfers between devices  37.4 us (36%)
  starting transfers between devices  25.2 us (24%)
  blocking collectives  18.7 us (18%)
  other arithmetic  9.44 us (9%)
  local copies, waits for them, and re-layouts  5.34 us (5%)
  matrix products  5.1 us (5%)
    all_to_all x1, waiting for transfers between devices, layer(): reduced = jnp.sum(lax.all_to_all(partial, 'gx', 0, 0, tiled=False), axis=0)  26.9 us
    all_to_all x1, blocking collectives, layer(): lax.all_to_all(jnp.broadcast_to(both[None], (gx_size,) + both.shape), 'gx...  18.7 us
    all_to_all x1, starting transfers between devices, exchange_sum(): return jnp.sum(lax.all_to_all(spread, axis, 0, 0, tiled=False), axis=0)  11.9 us
    ppermute x3, starting transfers between devices, pair_sum(): x = x + lax.ppermute(x, axis, pairs)  8.69 us
    all_to_all x1, waiting for transfers between devices, exchange_sum(): return jnp.sum(lax.all_to_all(spread, axis, 0, 0, tiled=False), axis=0)  7.8 us
    all_to_all x1, starting transfers between devices, layer(): reduced = jnp.sum(lax.all_to_all(partial, 'gx', 0, 0, tiled=False), axis=0)  4.66 us
    select_n x1, other arithmetic, layer(): new_values = jnp.where(at_row, new_value[:, :, None, :], value_cache)  3.96 us
    ppermute x3, waiting for transfers between devices, pair_sum(): x = x + lax.ppermute(x, axis, pairs)  2.71 us
  transfers between devices with their start and end apart: 5, of which 4 were waited for; matrix products, arithmetic and copies ran while one was open for 5% of the time, Pallas kernels for 0%

profile of v8, /device:TPU:1, one launch (start us, length us, event | category | flops | bytes accessed | tf_op | source)
XLA Modules:
  0.0 102.2 jit_solution(11317835665779706009)
XLA Ops:
  0.6 0.9 convert_reduce_fusion
  1.6 0.7 reshape.236
  2.3 11.9 %all-to-all-start = ((f32[32,1,128]{2,1,0:T(1,128)}), f32[32,1,128]{2,1,0:T(1,128)S(1)}, u32[]{:S(2)}, u32[]{:S(2)}) async-start(f32[32,1,128]{2,1,0:T(1,128)} %reshape.236), calls=%async_computation | async-start | bytes 32768 | tf_op jit(solution)/shard_map/all_to_all | solution.py:48
  14.2 0.7 iota_compare_fusion
  14.9 7.8 %all-to-all-done = f32[32,1,128]{2,1,0:T(1,128)S(1)} async-done(((f32[32,1,128]{2,1,0:T(1,128)}), f32[32,1,128]{2,1,0:T(1,128)S(1)}, u32[]{:S(2)}, u32[]{:S(2)}) %all-to-all-start) | async-done | bytes 16416 | tf_op jit(solution)/shard_map/all_to_all | solution.py:48
  22.7 0.5 broadcast.165
  23.2 0.7 reduce.2
  24.2 1.0 %add_convert_fusion.1 = (bf16[64,160]{1,0:T(8,128)(2,1)S(1)}, bf16[64,160]{1,0:T(8,128)(2,1)S(1)}) fusion(f32[160]{0:T(256)} %param.19, f32[160]{0:T(256)} %param.18, f32[160]{0:T(256)} %param.21, f32[160]{0:T(256)} %param.20, f32[64]{0:T(128)S(1)} %fusion.39, f32[64]{0:T(128)S(1)} %multiply_bitcast_fusion, bf16[64,160]{1,0:T(8,128)(2,1)} %param.17, ...), kind=kOutput, calls=%fused_computation.27 | convolution fusion | flops 1396736 | bytes 64768 | tf_op jit(solution)/shard_map/dot_general | solution.py:97
  25.3 1.3 %fusion.13 = f32[32,2,1920]{2,0,1:T(8,128)S(1)} fusion(bf16[160,1920]{1,0:T(8,128)(2,1)} %param.22, bf16[32,2,160]{2,1,0:T(2,128)(2,1)S(1)} %reshape.221), kind=kOutput, calls=%fused_computation.19 | convolution fusion | flops 39321600 | bytes 1126400 | tf_op jit(solution)/shard_map/sbk,kn->sbn/dot_general | solution.py:112
  26.6 0.3 fusion.11
  27.0 1.9 %copy.71 = f32[32,2,4480]{2,1,0:T(2,128)} copy(f32[32,2,4480]{2,0,1:T(8,128)S(1)} %pad_maximum_fusion) | data formatting | bytes 2293760 | tf_op jit(solution)/shard_map/concatenate | solution.py:110
  28.9 4.7 %all-to-all-start.1 = ((f32[32,2,4480]{2,1,0:T(2,128)}), f32[32,2,4480]{2,1,0:T(2,128)}, u32[]{:S(2)}, u32[]{:S(2)}) async-start(f32[32,2,4480]{2,1,0:T(2,128)} %copy.71), calls=%async_computation.1 | async-start | bytes 2293760 | tf_op jit(solution)/shard_map/all_to_all | solution.py:121
  33.8 0.1 multiply_cosine_fusion
  34.0 26.9 %all-to-all-done.1 = f32[32,2,4480]{2,1,0:T(2,128)} async-done(((f32[32,2,4480]{2,1,0:T(2,128)}), f32[32,2,4480]{2,1,0:T(2,128)}, u32[]{:S(2)}, u32[]{:S(2)}) %all-to-all-start.1) | async-done | bytes 1146912 | tf_op jit(solution)/shard_map/all_to_all | solution.py:121
  60.9 1.6 %reduce_sum.77 = f32[2,4480]{1,0:T(2,128)S(1)} reduce(f32[32,2,4480]{2,1,0:T(2,128)} %all-to-all-done.1, f32[]{:T(128)} %constant.11.clone.1), dimensions={0}, to_apply=%region_5.6 | reduce | flops 277760 | bytes 1182724 | tf_op jit(solution)/shard_map/reduce_sum | solution.py:121
  62.6 0.2 fusion.27
  63.1 0.2 fusion.33
  63.3 0.8 fusion.34
  64.0 0.3 convert_reduce_fusion.1
  64.4 0.4 fusion.20
  64.9 0.2 broadcast_in_dim.156
  65.2 18.7 %all_to_all.15 = bf16[32,2,3200]{2,1,0:T(2,128)(2,1)S(1)} all-to-all(bf16[32,2,3200]{2,1,0:T(2,128)(2,1)S(1)} %broadcast_in_dim.156), channel_id=1, replica_groups=mesh['gx'=32,'gy'=8] {'gx'}, dimensions={0} | all-to-all | bytes 819200 | tf_op jit(solution)/shard_map/all_to_all | solution.py:156
  83.9 0.4 fusion.8
  84.3 0.7 copy.76
  85.0 0.9 reshape.225
  85.9 4.5 %collective-permute-start = (f32[64,160]{1,0:T(8,128)S(1)}, f32[64,160]{1,0:T(8,128)S(1)}, u32[]{:S(2)}, u32[]{:S(2)}) collective-permute-start(f32[64,160]{1,0:T(8,128)S(1)} %reshape.225), channel_id=1, source_target_pairs={{0,1},{1,0},{2,3},{3,2},{4,5},{5,4},{6,7},{7,6},{8,9},{9,8},{10,11... | collective-permute-start | bytes 122888 | tf_op jit(solution)/shard_map/ppermute | solution.py:53
  90.4 0.9 collective-permute-done
  91.3 1.4 %collective-permute-start.1 = (f32[64,160]{1,0:T(8,128)S(1)}, f32[64,160]{1,0:T(8,128)S(1)}, u32[]{:S(2)}, u32[]{:S(2)}) collective-permute-start(f32[64,160]{1,0:T(8,128)S(1)} %add.97), channel_id=1, source_target_pairs={{0,2},{1,3},{2,0},{3,1},{4,6},{5,7},{6,4},{7,5},{8,10},{9,11},{10,... | collective-permute-start | bytes 122888 | tf_op jit(solution)/shard_map/ppermute | solution.py:53
  92.7 1.8 %collective-permute-done.1 = f32[64,160]{1,0:T(8,128)S(1)} collective-permute-done((f32[64,160]{1,0:T(8,128)S(1)}, f32[64,160]{1,0:T(8,128)S(1)}, u32[]{:S(2)}, u32[]{:S(2)}) %collective-permute-start.1) | collective-permute-done | bytes 40992 | tf_op jit(solution)/shard_map/ppermute | solution.py:53
  94.6 2.8 %collective-permute-start.2 = (f32[64,160]{1,0:T(8,128)S(1)}, f32[64,160]{1,0:T(8,128)S(1)}, u32[]{:S(2)}, u32[]{:S(2)}) collective-permute-start(f32[64,160]{1,0:T(8,128)S(1)} %add.98), channel_id=1, source_target_pairs={{0,6},{1,7},{2,4},{3,5},{4,2},{5,3},{6,0},{7,1},{8,14},{9,15},{10,... | collective-permute-start | bytes 122888 | tf_op jit(solution)/shard_map/ppermute | solution.py:53
  97.4 4.0 %broadcast_select_fusion = (bf16[2,5,1024,128]{3,2,1,0:T(8,128)(2,1)}, bf16[2,5,1024,128]{3,2,1,0:T(8,128)(2,1)}) fusion(bf16[2,5,1024,128]{3,2,1,0:T(8,128)(2,1)} %param.31, pred[2,1024]{1,0:T(4,128)(4,1)S(1)} %get-tuple-element.32, bf16[2,5,128]{2,1,0:T(8,128)(2,1)S(1)} %copy.78, bf16[2,5,1024,128]{3,2,1,0:T(8,128)(2,1)S(1)} %copy-done.1, ...), kind=kLoop, calls=%fused_computation.1 | loop fusion | flops 2621440 | bytes 10492928 | tf_op jit(solution)/shard_map/jit(_where)/select_n | solution.py:154
  101.4 0.8 fusion.5
  (56 shorter events, 1.2 us)
Async XLA Ops:
  0.6 26.0 %copy-start = (bf16[160,2560]{1,0:T(8,128)(2,1)S(1)}, bf16[160,2560]{1,0:T(8,128)(2,1)}, u32[]{:S(2)}) copy-start(bf16[160,2560]{1,0:T(8,128)(2,1)} %param.26) | copy-start | bytes 2457604
  2.3 20.4 %all-to-all-start = ((f32[32,1,128]{2,1,0:T(1,128)}), f32[32,1,128]{2,1,0:T(1,128)S(1)}, u32[]{:S(2)}, u32[]{:S(2)}) async-start(f32[32,1,128]{2,1,0:T(1,128)} %reshape.236), calls=%async_computation | async-start | bytes 32768 | tf_op jit(solution)/shard_map/all_to_all | solution.py:48
  27.0 6.6 %copy-start.6 = (s32[64]{0:T(128)S(1)}, s32[64]{0:T(128)}, u32[]{:S(2)}) copy-start(s32[64]{0:T(128)} %param.33) | copy-start | bytes 772
  27.0 6.6 %copy-start.11 = (s32[64]{0:T(128)S(1)}, s32[64]{0:T(128)}, u32[]{:S(2)}) copy-start(s32[64]{0:T(128)} %param.32) | copy-start | bytes 772
  27.0 35.5 %copy-start.5 = (f32[1920]{0:T(1024)S(1)}, f32[1920]{0:T(1024)}, u32[]{:S(2)}) copy-start(f32[1920]{0:T(1024)} %param.23) | copy-start | bytes 23044
  27.0 35.6 %copy-start.4 = (f32[2560]{0:T(1024)S(1)}, f32[2560]{0:T(1024)}, u32[]{:S(2)}) copy-start(f32[2560]{0:T(1024)} %param.27) | copy-start | bytes 30724
  27.0 36.2 %copy-start.1 = (bf16[2,5,1024,128]{3,2,1,0:T(8,128)(2,1)S(1)}, bf16[2,5,1024,128]{3,2,1,0:T(8,128)(2,1)}, u32[]{:S(2)}) copy-start(bf16[2,5,1024,128]{3,2,1,0:T(8,128)(2,1)} %param.30) | copy-start | bytes 7864324
  28.9 32.0 %all-to-all-start.1 = ((f32[32,2,4480]{2,1,0:T(2,128)}), f32[32,2,4480]{2,1,0:T(2,128)}, u32[]{:S(2)}, u32[]{:S(2)}) async-start(f32[32,2,4480]{2,1,0:T(2,128)} %copy.71), calls=%async_computation.1 | async-start | bytes 2293760 | tf_op jit(solution)/shard_map/all_to_all | solution.py:121
  62.6 1.8 %copy-start.2 = (bf16[2,5,1024,128]{3,2,1,0:T(8,128)(2,1)S(1)}, bf16[2,5,1024,128]{3,2,1,0:T(8,128)(2,1)}, u32[]{:S(2)}) copy-start(bf16[2,5,1024,128]{3,2,1,0:T(8,128)(2,1)} %param.31) | copy-start | bytes 7864324
  64.0 19.8 %copy-start.9 = (bf16[2560,160]{0,1:T(8,128)(2,1)S(1)}, bf16[2560,160]{0,1:T(8,128)(2,1)}, u32[]{:S(2)}) copy-start(bf16[2560,160]{0,1:T(8,128)(2,1)} %param.28) | copy-start | bytes 2457604
  64.0 19.8 %copy-start.10 = (bf16[640,160]{0,1:T(8,128)(2,1)S(1)}, bf16[640,160]{0,1:T(8,128)(2,1)}, u32[]{:S(2)}) copy-start(bf16[640,160]{0,1:T(8,128)(2,1)} %param.24) | copy-start | bytes 614404
  85.9 5.4 %collective-permute-start = (f32[64,160]{1,0:T(8,128)S(1)}, f32[64,160]{1,0:T(8,128)S(1)}, u32[]{:S(2)}, u32[]{:S(2)}) collective-permute-start(f32[64,160]{1,0:T(8,128)S(1)} %reshape.225), channel_id=1, source_target_pairs={{0,1},{1,0},{2,3},{3,2},{4,5},{5,4},{6,7},{7,6},{8,9},{9,8},{10,11... | collective-permute-start | bytes 122888 | tf_op jit(solution)/shard_map/ppermute | solution.py:53
  91.3 3.2 %collective-permute-start.1 = (f32[64,160]{1,0:T(8,128)S(1)}, f32[64,160]{1,0:T(8,128)S(1)}, u32[]{:S(2)}, u32[]{:S(2)}) collective-permute-start(f32[64,160]{1,0:T(8,128)S(1)} %add.97), channel_id=1, source_target_pairs={{0,2},{1,3},{2,0},{3,1},{4,6},{5,7},{6,4},{7,5},{8,10},{9,11},{10,... | collective-permute-start | bytes 122888 | tf_op jit(solution)/shard_map/ppermute | solution.py:53
  94.5 6.8 %copy-start.3 = (bf16[64,160]{1,0:T(8,128)(2,1)S(1)}, bf16[64,160]{1,0:T(8,128)(2,1)}, u32[]{:S(2)}) copy-start(bf16[64,160]{1,0:T(8,128)(2,1)} %param.17) | copy-start | bytes 61444
  94.5 6.8 %copy-start.7 = (f32[160]{0:T(256)S(1)}, f32[160]{0:T(256)}, u32[]{:S(2)}) copy-start(f32[160]{0:T(256)} %param.29) | copy-start | bytes 1924
  94.6 6.8 %copy-start.8 = (f32[160]{0:T(256)S(1)}, f32[160]{0:T(256)}, u32[]{:S(2)}) copy-start(f32[160]{0:T(256)} %param.25) | copy-start | bytes 1924
  94.6 6.8 %collective-permute-start.2 = (f32[64,160]{1,0:T(8,128)S(1)}, f32[64,160]{1,0:T(8,128)S(1)}, u32[]{:S(2)}, u32[]{:S(2)}) collective-permute-start(f32[64,160]{1,0:T(8,128)S(1)} %add.98), channel_id=1, source_target_pairs={{0,6},{1,7},{2,4},{3,5},{4,2},{5,3},{6,0},{7,1},{8,14},{9,15},{10,... | collective-permute-start | bytes 122888 | tf_op jit(solution)/shard_map/ppermute | solution.py:53

commit v9 on v8

--- a/solution.py
+++ b/solution.py
@@ -106,19 +106,15 @@
     slot_len = jnp.sum(jnp.where(matches, lengths[:, None], 0), axis=0)
     my_len = lax.dynamic_slice_in_dim(slot_len, lax.axis_index("gx") * rows_dev, rows_dev, 0)
     qkv_cols = w_qkv.shape[1]
-    blocks = (gx_size, requests // gx_size, attn_slot.shape[1])
     partial = jnp.concatenate(
         [
-            jnp.einsum(
-                "sbk,kn->sbn", attn_slot.reshape(blocks), w_qkv, preferred_element_type=jnp.float32
-            ),
-            jnp.einsum(
-                "sbk,kn->sbn", mlp_slot.reshape(blocks), w_up, preferred_element_type=jnp.float32
-            ),
+            jnp.dot(attn_slot, w_qkv, preferred_element_type=jnp.float32),
+            jnp.dot(mlp_slot, w_up, preferred_element_type=jnp.float32),
         ],
-        axis=2,
+        axis=1,
     )
-    reduced = jnp.sum(lax.all_to_all(partial, "gx", 0, 0, tiled=False), axis=0)
+    received = lax.all_to_all(partial, "gx", 0, 1, tiled=True)
+    reduced = jnp.sum(received.reshape(rows_dev, gx_size, partial.shape[1]), axis=1)
     qkv = reduced[:, :qkv_cols] + b_qkv
     up = reduced[:, qkv_cols:] + b_up
     qkv = qkv.reshape(rows_dev, heads_dev, 3, HD)

time: 103 us -> 106 us (1.029)
  local copies, waits for them, and re-layouts: 5.34 us -> 6.48 us
    all_to_all x0 -> x1, local copies, waits for them, and re-layouts: none -> 3.09 us  [layer(): received = lax.all_to_all(partial, 'gx', 0, 1, tiled=True)]
    concatenate x1 -> x0, local copies, waits for them, and re-layouts: 1.89 us -> none  [layer(): jnp.concatenate([jnp.einsum('sbk,kn->sbn', attn_slot.reshape(blocks), w_q...]
where the time goes in v9:
time: 106 us; the launch traced here: 105 us
  waiting for transfers between devices  37.4 us (35%)
  starting transfers between devices  25.2 us (24%)
  blocking collectives  18.7 us (18%)
  other arithmetic  10.4 us (10%)
  local copies, waits for them, and re-layouts  6.48 us (6%)
  matrix products  5.83 us (6%)
    all_to_all x1, waiting for transfers between devices, layer(): received = lax.all_to_all(partial, 'gx', 0, 1, tiled=True)  26.9 us
    all_to_all x1, blocking collectives, layer(): lax.all_to_all(jnp.broadcast_to(both[None], (gx_size,) + both.shape), 'gx...  18.7 us
    all_to_all x1, starting transfers between devices, exchange_sum(): return jnp.sum(lax.all_to_all(spread, axis, 0, 0, tiled=False), axis=0)  11.9 us
    ppermute x3, starting transfers between devices, pair_sum(): x = x + lax.ppermute(x, axis, pairs)  8.71 us
    all_to_all x1, waiting for transfers between devices, exchange_sum(): return jnp.sum(lax.all_to_all(spread, axis, 0, 0, tiled=False), axis=0)  7.8 us
    all_to_all x1, starting transfers between devices, layer(): received = lax.all_to_all(partial, 'gx', 0, 1, tiled=True)  4.66 us
    select_n x1, other arithmetic, layer(): new_values = jnp.where(at_row, new_value[:, :, None, :], value_cache)  3.96 us
    all_to_all x1, local copies, waits for them, and re-layouts, layer(): received = lax.all_to_all(partial, 'gx', 0, 1, tiled=True)  3.09 us
  transfers between devices with their start and end apart: 5, of which 4 were waited for; matrix products, arithmetic and copies ran while one was open for 5% of the time, Pallas kernels for 0%

profile of v9, /device:TPU:1, one launch (start us, length us, event | category | flops | bytes accessed | tf_op | source)
XLA Modules:
  0.0 105.1 jit_solution(14801588571024214927)
XLA Ops:
  0.6 0.9 convert_reduce_fusion
  1.6 0.7 reshape.231
  2.3 11.9 %all-to-all-start = ((f32[32,1,128]{2,1,0:T(1,128)}), f32[32,1,128]{2,1,0:T(1,128)S(1)}, u32[]{:S(2)}, u32[]{:S(2)}) async-start(f32[32,1,128]{2,1,0:T(1,128)} %reshape.231), calls=%async_computation | async-start | bytes 32768 | tf_op jit(solution)/shard_map/all_to_all | solution.py:48
  14.2 0.7 iota_compare_fusion
  14.9 7.8 %all-to-all-done = f32[32,1,128]{2,1,0:T(1,128)S(1)} async-done(((f32[32,1,128]{2,1,0:T(1,128)}), f32[32,1,128]{2,1,0:T(1,128)S(1)}, u32[]{:S(2)}, u32[]{:S(2)}) %all-to-all-start) | async-done | bytes 16416 | tf_op jit(solution)/shard_map/all_to_all | solution.py:48
  22.7 0.5 broadcast.165
  23.2 0.7 reduce.4
  24.2 1.0 fusion.3
  25.2 1.3 %fusion.18 = f32[64,1920]{1,0:T(8,128)S(1)} fusion(bf16[160,1920]{1,0:T(8,128)(2,1)} %param.22, f32[64,160]{1,0:T(8,128)S(1)} %fusion.3, f32[160]{0:T(256)} %param.19, f32[160]{0:T(256)} %param.18), kind=kOutput, calls=%fused_computation.37 | convolution fusion | flops 39352320 | bytes 1148160 | tf_op jit(solution)/shard_map/dot_general | solution.py:111
  26.6 0.9 fusion.19
  27.5 1.1 %pad_maximum_fusion = f32[64,4480]{1,0:T(8,128)} fusion(f32[64,2560]{1,0:T(8,128)S(1)} %fusion.19, f32[64,1920]{1,0:T(8,128)S(1)} %fusion.18), kind=kLoop, calls=%fused_computation.3 | loop fusion | flops 286720 | bytes 2293760 | tf_op jit(solution)/shard_map/concatenate | solution.py:109
  28.6 3.1 %all_to_all.17 = f32[32,2,4480]{2,1,0:T(2,128)} reshape(f32[64,4480]{1,0:T(8,128)} %pad_maximum_fusion) | data formatting | bytes 2293760 | tf_op jit(solution)/shard_map/all_to_all | solution.py:116
  31.7 4.7 %all-to-all-start.1 = ((f32[32,2,4480]{2,1,0:T(2,128)}), f32[32,2,4480]{2,1,0:T(2,128)}, u32[]{:S(2)}, u32[]{:S(2)}) async-start(f32[32,2,4480]{2,1,0:T(2,128)} %all_to_all.17), calls=%async_computation.1 | async-start | bytes 2293760 | tf_op jit(solution)/shard_map/all_to_all | solution.py:116
  36.8 26.9 %all-to-all-done.1 = f32[32,2,4480]{2,1,0:T(2,128)} async-done(((f32[32,2,4480]{2,1,0:T(2,128)}), f32[32,2,4480]{2,1,0:T(2,128)}, u32[]{:S(2)}, u32[]{:S(2)}) %all-to-all-start.1) | async-done | bytes 1146912 | tf_op jit(solution)/shard_map/all_to_all | solution.py:116
  63.7 1.6 %reduce_sum.77 = f32[2,4480]{1,0:T(2,128)S(1)} reduce(f32[32,2,4480]{2,1,0:T(2,128)} %all-to-all-done.1, f32[]{:T(128)} %constant.11.clone.1), dimensions={0}, to_apply=%region_5.6 | reduce | flops 277760 | bytes 1182724 | tf_op jit(solution)/shard_map/reduce_sum | solution.py:117
  65.4 0.2 fusion.27
  65.9 0.2 fusion.33
  66.1 0.8 fusion.34
  66.9 0.3 convert_reduce_fusion.1
  67.2 0.4 fusion.16
  67.8 0.2 broadcast_in_dim.156
  68.0 18.7 %all_to_all.23 = bf16[32,2,3200]{2,1,0:T(2,128)(2,1)S(1)} all-to-all(bf16[32,2,3200]{2,1,0:T(2,128)(2,1)S(1)} %broadcast_in_dim.156), channel_id=1, replica_groups=mesh['gx'=32,'gy'=8] {'gx'}, dimensions={0} | all-to-all | bytes 819200 | tf_op jit(solution)/shard_map/all_to_all | solution.py:152
  86.7 0.4 fusion.8
  87.2 0.7 copy.59
  87.9 0.9 reshape.222
  88.8 4.5 %collective-permute-start = (f32[64,160]{1,0:T(8,128)S(1)}, f32[64,160]{1,0:T(8,128)S(1)}, u32[]{:S(2)}, u32[]{:S(2)}) collective-permute-start(f32[64,160]{1,0:T(8,128)S(1)} %reshape.222), channel_id=1, source_target_pairs={{0,1},{1,0},{2,3},{3,2},{4,5},{5,4},{6,7},{7,6},{8,9},{9,8},{10,11... | collective-permute-start | bytes 122888 | tf_op jit(solution)/shard_map/ppermute | solution.py:53
  93.2 0.9 collective-permute-done
  94.1 1.4 %collective-permute-start.1 = (f32[64,160]{1,0:T(8,128)S(1)}, f32[64,160]{1,0:T(8,128)S(1)}, u32[]{:S(2)}, u32[]{:S(2)}) collective-permute-start(f32[64,160]{1,0:T(8,128)S(1)} %add.97), channel_id=1, source_target_pairs={{0,2},{1,3},{2,0},{3,1},{4,6},{5,7},{6,4},{7,5},{8,10},{9,11},{10,... | collective-permute-start | bytes 122888 | tf_op jit(solution)/shard_map/ppermute | solution.py:53
  95.6 1.8 %collective-permute-done.1 = f32[64,160]{1,0:T(8,128)S(1)} collective-permute-done((f32[64,160]{1,0:T(8,128)S(1)}, f32[64,160]{1,0:T(8,128)S(1)}, u32[]{:S(2)}, u32[]{:S(2)}) %collective-permute-start.1) | collective-permute-done | bytes 40992 | tf_op jit(solution)/shard_map/ppermute | solution.py:53
  97.4 2.8 %collective-permute-start.2 = (f32[64,160]{1,0:T(8,128)S(1)}, f32[64,160]{1,0:T(8,128)S(1)}, u32[]{:S(2)}, u32[]{:S(2)}) collective-permute-start(f32[64,160]{1,0:T(8,128)S(1)} %add.98), channel_id=1, source_target_pairs={{0,6},{1,7},{2,4},{3,5},{4,2},{5,3},{6,0},{7,1},{8,14},{9,15},{10,... | collective-permute-start | bytes 122888 | tf_op jit(solution)/shard_map/ppermute | solution.py:53
  100.2 4.0 %broadcast_select_fusion = (bf16[2,5,1024,128]{3,2,1,0:T(8,128)(2,1)}, bf16[2,5,1024,128]{3,2,1,0:T(8,128)(2,1)}) fusion(bf16[2,5,1024,128]{3,2,1,0:T(8,128)(2,1)} %param.31, pred[2,1024]{1,0:T(4,128)(4,1)S(1)} %get-tuple-element.30, bf16[2,5,128]{2,1,0:T(8,128)(2,1)S(1)} %copy.61, bf16[2,5,1024,128]{3,2,1,0:T(8,128)(2,1)S(1)} %copy-done.1, ...), kind=kLoop, calls=%fused_computation.1 | loop fusion | flops 2621440 | bytes 10492928 | tf_op jit(solution)/shard_map/jit(_where)/select_n | solution.py:150
  104.2 0.8 fusion.5
  (54 shorter events, 1.2 us)
Async XLA Ops:
  0.6 26.0 %copy-start = (bf16[160,2560]{1,0:T(8,128)(2,1)S(1)}, bf16[160,2560]{1,0:T(8,128)(2,1)}, u32[]{:S(2)}) copy-start(bf16[160,2560]{1,0:T(8,128)(2,1)} %param.26) | copy-start | bytes 2457604
  2.3 20.4 %all-to-all-start = ((f32[32,1,128]{2,1,0:T(1,128)}), f32[32,1,128]{2,1,0:T(1,128)S(1)}, u32[]{:S(2)}, u32[]{:S(2)}) async-start(f32[32,1,128]{2,1,0:T(1,128)} %reshape.231), calls=%async_computation | async-start | bytes 32768 | tf_op jit(solution)/shard_map/all_to_all | solution.py:48
  28.6 7.8 %copy-start.6 = (s32[64]{0:T(128)S(1)}, s32[64]{0:T(128)}, u32[]{:S(2)}) copy-start(s32[64]{0:T(128)} %param.33) | copy-start | bytes 772
  28.6 7.8 %copy-start.11 = (s32[64]{0:T(128)S(1)}, s32[64]{0:T(128)}, u32[]{:S(2)}) copy-start(s32[64]{0:T(128)} %param.32) | copy-start | bytes 772
  28.6 36.7 %copy-start.5 = (f32[1920]{0:T(1024)S(1)}, f32[1920]{0:T(1024)}, u32[]{:S(2)}) copy-start(f32[1920]{0:T(1024)} %param.23) | copy-start | bytes 23044
  28.6 36.8 %copy-start.4 = (f32[2560]{0:T(1024)S(1)}, f32[2560]{0:T(1024)}, u32[]{:S(2)}) copy-start(f32[2560]{0:T(1024)} %param.27) | copy-start | bytes 30724
  28.6 37.4 %copy-start.1 = (bf16[2,5,1024,128]{3,2,1,0:T(8,128)(2,1)S(1)}, bf16[2,5,1024,128]{3,2,1,0:T(8,128)(2,1)}, u32[]{:S(2)}) copy-start(bf16[2,5,1024,128]{3,2,1,0:T(8,128)(2,1)} %param.30) | copy-start | bytes 7864324
  31.7 32.0 %all-to-all-start.1 = ((f32[32,2,4480]{2,1,0:T(2,128)}), f32[32,2,4480]{2,1,0:T(2,128)}, u32[]{:S(2)}, u32[]{:S(2)}) async-start(f32[32,2,4480]{2,1,0:T(2,128)} %all_to_all.17), calls=%async_computation.1 | async-start | bytes 2293760 | tf_op jit(solution)/shard_map/all_to_all | solution.py:116
  65.4 1.8 %copy-start.2 = (bf16[2,5,1024,128]{3,2,1,0:T(8,128)(2,1)S(1)}, bf16[2,5,1024,128]{3,2,1,0:T(8,128)(2,1)}, u32[]{:S(2)}) copy-start(bf16[2,5,1024,128]{3,2,1,0:T(8,128)(2,1)} %param.31) | copy-start | bytes 7864324
  66.9 19.8 %copy-start.9 = (bf16[2560,160]{0,1:T(8,128)(2,1)S(1)}, bf16[2560,160]{0,1:T(8,128)(2,1)}, u32[]{:S(2)}) copy-start(bf16[2560,160]{0,1:T(8,128)(2,1)} %param.28) | copy-start | bytes 2457604
  66.9 19.8 %copy-start.10 = (bf16[640,160]{0,1:T(8,128)(2,1)S(1)}, bf16[640,160]{0,1:T(8,128)(2,1)}, u32[]{:S(2)}) copy-start(bf16[640,160]{0,1:T(8,128)(2,1)} %param.24) | copy-start | bytes 614404
  88.8 5.4 %collective-permute-start = (f32[64,160]{1,0:T(8,128)S(1)}, f32[64,160]{1,0:T(8,128)S(1)}, u32[]{:S(2)}, u32[]{:S(2)}) collective-permute-start(f32[64,160]{1,0:T(8,128)S(1)} %reshape.222), channel_id=1, source_target_pairs={{0,1},{1,0},{2,3},{3,2},{4,5},{5,4},{6,7},{7,6},{8,9},{9,8},{10,11... | collective-permute-start | bytes 122888 | tf_op jit(solution)/shard_map/ppermute | solution.py:53
  94.1 3.2 %collective-permute-start.1 = (f32[64,160]{1,0:T(8,128)S(1)}, f32[64,160]{1,0:T(8,128)S(1)}, u32[]{:S(2)}, u32[]{:S(2)}) collective-permute-start(f32[64,160]{1,0:T(8,128)S(1)} %add.97), channel_id=1, source_target_pairs={{0,2},{1,3},{2,0},{3,1},{4,6},{5,7},{6,4},{7,5},{8,10},{9,11},{10,... | collective-permute-start | bytes 122888 | tf_op jit(solution)/shard_map/ppermute | solution.py:53
  97.4 6.8 %copy-start.3 = (bf16[64,160]{1,0:T(8,128)(2,1)S(1)}, bf16[64,160]{1,0:T(8,128)(2,1)}, u32[]{:S(2)}) copy-start(bf16[64,160]{1,0:T(8,128)(2,1)} %param.17) | copy-start | bytes 61444
  97.4 6.8 %copy-start.7 = (f32[160]{0:T(256)S(1)}, f32[160]{0:T(256)}, u32[]{:S(2)}) copy-start(f32[160]{0:T(256)} %param.29) | copy-start | bytes 1924
  97.4 6.8 %copy-start.8 = (f32[160]{0:T(256)S(1)}, f32[160]{0:T(256)}, u32[]{:S(2)}) copy-start(f32[160]{0:T(256)} %param.25) | copy-start | bytes 1924
  97.4 6.8 %collective-permute-start.2 = (f32[64,160]{1,0:T(8,128)S(1)}, f32[64,160]{1,0:T(8,128)S(1)}, u32[]{:S(2)}, u32[]{:S(2)}) collective-permute-start(f32[64,160]{1,0:T(8,128)S(1)} %add.98), channel_id=1, source_target_pairs={{0,6},{1,7},{2,4},{3,5},{4,2},{5,3},{6,0},{7,1},{8,14},{9,15},{10,... | collective-permute-start | bytes 122888 | tf_op jit(solution)/shard_map/ppermute | solution.py:53

commit v10 on v8

--- a/solution.py
+++ b/solution.py
@@ -87,15 +87,15 @@
     heads_dev = key_cache.shape[1]
     wide_in = hidden_in.astype(jnp.float32)
     stats = exchange_sum(
-        jnp.stack([jnp.sum(wide_in, axis=1), jnp.sum(wide_in * wide_in, axis=1)]),
+        jnp.concatenate([jnp.sum(wide_in, axis=1), jnp.sum(wide_in * wide_in, axis=1)]),
         "gx",
         gx_size,
-    )
+    ).reshape(2, requests)
     slot_ids = lax.iota(jnp.int32, requests)
     matches = assignment[:, None] == slot_ids[None, :]
     to_request = matches.astype(jnp.float32)
     x_slot = jnp.dot(matches.T.astype(jnp.bfloat16), hidden_in, preferred_element_type=jnp.float32)
-    w_both = jnp.concatenate([w_out, w_down], axis=0)
+    w_both = lax.optimization_barrier(jnp.concatenate([w_out, w_down], axis=0))
     stats = jnp.sum(jnp.where(matches[None], stats[:, :, None], 0.0), axis=1)
     sum_rows, sum_squares = stats[0], stats[1]
     row_mean = sum_rows / D

time: 103 us -> 104 us (level)
  blocking collectives: 18.7 us -> 0 us
  waiting for transfers between devices: 37.4 us -> 47.3 us
  starting transfers between devices: 25.2 us -> 32.1 us
  other arithmetic: 9.44 us -> 11 us
  matrix products: 5.1 us -> 6.45 us
    all_to_all x1 -> x0, blocking collectives: 18.7 us -> none  [layer(): lax.all_to_all(jnp.broadcast_to(both[None], (gx_size,) + both.shape), 'gx...]
    all_to_all x0 -> x1, waiting for transfers between devices: none -> 9.91 us  [layer(): lax.all_to_all(jnp.broadcast_to(both[None], (gx_size,) + both.shape), 'gx...]
    all_to_all x0 -> x1, starting transfers between devices: none -> 6.88 us  [layer(): lax.all_to_all(jnp.broadcast_to(both[None], (gx_size,) + both.shape), 'gx...]
    concatenate x0 -> x2, other arithmetic: none -> 2.29 us  [the longest x1 2.21 us: layer(): w_both = lax.optimization_barrier(jnp.concatenate([w_out, w_down], axis=0))]
    dot_general x1, matrix products: 0.45 us -> 1.79 us  [layer(): jnp.einsum('sbk,kn->sbn', gathered, w_both, preferred_element_type=jnp.fl...]
  transfers between devices with their start and end apart: 5 -> 6, of which waited for: 4 -> 5; matrix products, arithmetic and copies ran while one was open for 5% -> 7% of each run, Pallas kernels for 0% -> 0%
where the time goes in v10:
time: 104 us; the launch traced here: 103 us
  waiting for transfers between devices  47.3 us (45%)
  starting transfers between devices  32.1 us (31%)
  other arithmetic  11 us (11%)
  matrix products  6.45 us (6%)
  local copies, waits for them, and re-layouts  5.48 us (5%)
    all_to_all x1, waiting for transfers between devices, layer(): reduced = jnp.sum(lax.all_to_all(partial, 'gx', 0, 0, tiled=False), axis=0)  26.9 us
    all_to_all x1, starting transfers between devices, exchange_sum(): return jnp.sum(lax.all_to_all(spread, axis, 0, 0, tiled=False), axis=0)  11.9 us
    all_to_all x1, waiting for transfers between devices, layer(): lax.all_to_all(jnp.broadcast_to(both[None], (gx_size,) + both.shape), 'gx...  9.91 us
    ppermute x3, starting transfers between devices, pair_sum(): x = x + lax.ppermute(x, axis, pairs)  8.68 us
    all_to_all x1, waiting for transfers between devices, exchange_sum(): return jnp.sum(lax.all_to_all(spread, axis, 0, 0, tiled=False), axis=0)  7.8 us
    all_to_all x1, starting transfers between devices, layer(): lax.all_to_all(jnp.broadcast_to(both[None], (gx_size,) + both.shape), 'gx...  6.88 us
    all_to_all x1, starting transfers between devices, layer(): reduced = jnp.sum(lax.all_to_all(partial, 'gx', 0, 0, tiled=False), axis=0)  4.67 us
    select_n x1, other arithmetic, layer(): new_values = jnp.where(at_row, new_value[:, :, None, :], value_cache)  3.96 us
  transfers between devices with their start and end apart: 6, of which 5 were waited for; matrix products, arithmetic and copies ran while one was open for 7% of the time, Pallas kernels for 0%

profile of v10, /device:TPU:1, one launch (start us, length us, event | category | flops | bytes accessed | tf_op | source)
XLA Modules:
  0.0 103.4 jit_solution(10897676003412602452)
XLA Ops:
  0.6 0.9 convert_reduce_fusion
  1.7 0.6 broadcast_in_dim.151
  2.3 11.9 %all-to-all-start = ((f32[32,1,128]{2,1,0:T(1,128)}), f32[32,1,128]{2,1,0:T(1,128)S(1)}, u32[]{:S(2)}, u32[]{:S(2)}) async-start(f32[32,1,128]{2,1,0:T(1,128)} %broadcast_in_dim.151), calls=%async_computation | async-start | bytes 32768 | tf_op jit(solution)/shard_map/all_to_all | solution.py:48
  14.2 0.7 iota_compare_fusion
  14.9 7.8 %all-to-all-done = f32[32,1,128]{2,1,0:T(1,128)S(1)} async-done(((f32[32,1,128]{2,1,0:T(1,128)}), f32[32,1,128]{2,1,0:T(1,128)S(1)}, u32[]{:S(2)}, u32[]{:S(2)}) %all-to-all-start) | async-done | bytes 16416 | tf_op jit(solution)/shard_map/all_to_all | solution.py:48
  22.9 1.0 %add_convert_fusion.1 = (bf16[64,160]{1,0:T(8,128)(2,1)S(1)}, bf16[64,160]{1,0:T(8,128)(2,1)S(1)}) fusion(f32[160]{0:T(256)} %param.19, f32[160]{0:T(256)} %param.18, f32[160]{0:T(256)} %param.21, f32[160]{0:T(256)} %param.20, f32[64]{0:T(128)S(1)} %fusion.38, f32[64]{0:T(128)S(1)} %multiply_bitcast_fusion, bf16[64,160]{1,0:T(8,128)(2,1)} %param.17, ...), kind=kOutput, calls=%fused_computation.26 | convolution fusion | flops 1396736 | bytes 64768 | tf_op jit(solution)/shard_map/dot_general | solution.py:97
  24.0 1.3 %fusion.12 = f32[32,2,1920]{2,0,1:T(8,128)S(1)} fusion(bf16[160,1920]{1,0:T(8,128)(2,1)} %param.22, bf16[32,2,160]{2,1,0:T(2,128)(2,1)S(1)} %reshape.226), kind=kOutput, calls=%fused_computation.18 | convolution fusion | flops 39321600 | bytes 1126400 | tf_op jit(solution)/shard_map/sbk,kn->sbn/dot_general | solution.py:112
  25.3 0.3 fusion.10
  25.8 1.9 %copy.71 = f32[32,2,4480]{2,1,0:T(2,128)} copy(f32[32,2,4480]{2,0,1:T(8,128)S(1)} %pad_maximum_fusion) | data formatting | bytes 2293760 | tf_op jit(solution)/shard_map/concatenate | solution.py:110
  27.6 4.7 %all-to-all-start.1 = ((f32[32,2,4480]{2,1,0:T(2,128)}), f32[32,2,4480]{2,1,0:T(2,128)}, u32[]{:S(2)}, u32[]{:S(2)}) async-start(f32[32,2,4480]{2,1,0:T(2,128)} %copy.71), calls=%async_computation.1 | async-start | bytes 2293760 | tf_op jit(solution)/shard_map/all_to_all | solution.py:121
  32.5 0.1 multiply_cosine_fusion
  32.7 26.9 %all-to-all-done.1 = f32[32,2,4480]{2,1,0:T(2,128)} async-done(((f32[32,2,4480]{2,1,0:T(2,128)}), f32[32,2,4480]{2,1,0:T(2,128)}, u32[]{:S(2)}, u32[]{:S(2)}) %all-to-all-start.1) | async-done | bytes 1146912 | tf_op jit(solution)/shard_map/all_to_all | solution.py:121
  59.7 1.6 %reduce_sum.77 = f32[2,4480]{1,0:T(2,128)S(1)} reduce(f32[32,2,4480]{2,1,0:T(2,128)} %all-to-all-done.1, f32[]{:T(128)} %constant.11.clone.1), dimensions={0}, to_apply=%region_5.6 | reduce | flops 277760 | bytes 1182724 | tf_op jit(solution)/shard_map/reduce_sum | solution.py:121
  61.4 0.2 fusion.26
  61.8 0.2 fusion.32
  62.0 0.8 fusion.33
  62.8 0.3 convert_reduce_fusion.1
  63.1 0.4 fusion.19
  63.7 1.0 broadcast_in_dim.158
  64.6 6.9 %all-to-all-start.2 = ((bf16[32,2,3200]{2,1,0:T(2,128)(2,1)}), bf16[32,2,3200]{2,1,0:T(2,128)(2,1)}, u32[]{:S(2)}, u32[]{:S(2)}) async-start(bf16[32,2,3200]{2,1,0:T(2,128)(2,1)} %broadcast_in_dim.158), calls=%async_computation.2 | async-start | bytes 819200 | tf_op jit(solution)/shard_map/all_to_all | solution.py:156
  71.5 2.2 %pad_maximum_fusion.1 = bf16[3200,160]{0,1:T(8,128)(2,1)} fusion(bf16[2560,160]{0,1:T(8,128)(2,1)} %param.28, bf16[640,160]{0,1:T(8,128)(2,1)} %param.24), kind=kLoop, calls=%fused_computation.13 | loop fusion | flops 2048000 | bytes 2048000 | tf_op jit(solution)/shard_map/concatenate | solution.py:98
  73.7 9.9 %all-to-all-done.2 = bf16[32,2,3200]{2,1,0:T(2,128)(2,1)} async-done(((bf16[32,2,3200]{2,1,0:T(2,128)(2,1)}), bf16[32,2,3200]{2,1,0:T(2,128)(2,1)}, u32[]{:S(2)}, u32[]{:S(2)}) %all-to-all-start.2) | async-done | bytes 409632 | tf_op jit(solution)/shard_map/all_to_all | solution.py:156
  83.7 1.8 %fusion.8 = f32[32,2,160]{2,0,1:T(8,128)S(1)} fusion(bf16[3200,160]{0,1:T(8,128)(2,1)} %pad_maximum_fusion.1, bf16[32,2,3200]{2,1,0:T(2,128)(2,1)} %all-to-all-done.2), kind=kOutput, calls=%fused_computation.14 | convolution fusion | flops 65536000 | bytes 1474560 | tf_op jit(solution)/shard_map/sbk,kn->sbn/dot_general | solution.py:159
  85.5 0.7 copy.76
  86.2 0.9 reshape.230
  87.1 4.5 %collective-permute-start = (f32[64,160]{1,0:T(8,128)S(1)}, f32[64,160]{1,0:T(8,128)S(1)}, u32[]{:S(2)}, u32[]{:S(2)}) collective-permute-start(f32[64,160]{1,0:T(8,128)S(1)} %reshape.230), channel_id=1, source_target_pairs={{0,1},{1,0},{2,3},{3,2},{4,5},{5,4},{6,7},{7,6},{8,9},{9,8},{10,11... | collective-permute-start | bytes 122888 | tf_op jit(solution)/shard_map/ppermute | solution.py:53
  91.5 0.9 collective-permute-done
  92.5 1.4 %collective-permute-start.1 = (f32[64,160]{1,0:T(8,128)S(1)}, f32[64,160]{1,0:T(8,128)S(1)}, u32[]{:S(2)}, u32[]{:S(2)}) collective-permute-start(f32[64,160]{1,0:T(8,128)S(1)} %add.97), channel_id=1, source_target_pairs={{0,2},{1,3},{2,0},{3,1},{4,6},{5,7},{6,4},{7,5},{8,10},{9,11},{10,... | collective-permute-start | bytes 122888 | tf_op jit(solution)/shard_map/ppermute | solution.py:53
  93.9 1.8 %collective-permute-done.1 = f32[64,160]{1,0:T(8,128)S(1)} collective-permute-done((f32[64,160]{1,0:T(8,128)S(1)}, f32[64,160]{1,0:T(8,128)S(1)}, u32[]{:S(2)}, u32[]{:S(2)}) %collective-permute-start.1) | collective-permute-done | bytes 40992 | tf_op jit(solution)/shard_map/ppermute | solution.py:53
  95.7 2.8 %collective-permute-start.2 = (f32[64,160]{1,0:T(8,128)S(1)}, f32[64,160]{1,0:T(8,128)S(1)}, u32[]{:S(2)}, u32[]{:S(2)}) collective-permute-start(f32[64,160]{1,0:T(8,128)S(1)} %add.98), channel_id=1, source_target_pairs={{0,6},{1,7},{2,4},{3,5},{4,2},{5,3},{6,0},{7,1},{8,14},{9,15},{10,... | collective-permute-start | bytes 122888 | tf_op jit(solution)/shard_map/ppermute | solution.py:53
  98.5 4.0 %broadcast_select_fusion = (bf16[2,5,1024,128]{3,2,1,0:T(8,128)(2,1)}, bf16[2,5,1024,128]{3,2,1,0:T(8,128)(2,1)}) fusion(bf16[2,5,1024,128]{3,2,1,0:T(8,128)(2,1)} %param.31, pred[2,1024]{1,0:T(4,128)(4,1)S(1)} %get-tuple-element.32, bf16[2,5,128]{2,1,0:T(8,128)(2,1)S(1)} %copy.78, bf16[2,5,1024,128]{3,2,1,0:T(8,128)(2,1)S(1)} %copy-done.1, ...), kind=kLoop, calls=%fused_computation.1 | loop fusion | flops 2621440 | bytes 10492928 | tf_op jit(solution)/shard_map/jit(_where)/select_n | solution.py:154
  102.5 0.8 fusion.5
  (51 shorter events, 1.2 us)
Async XLA Ops:
  0.6 24.7 %copy-start = (bf16[160,2560]{1,0:T(8,128)(2,1)S(1)}, bf16[160,2560]{1,0:T(8,128)(2,1)}, u32[]{:S(2)}) copy-start(bf16[160,2560]{1,0:T(8,128)(2,1)} %param.26) | copy-start | bytes 2457604
  2.3 20.4 %all-to-all-start = ((f32[32,1,128]{2,1,0:T(1,128)}), f32[32,1,128]{2,1,0:T(1,128)S(1)}, u32[]{:S(2)}, u32[]{:S(2)}) async-start(f32[32,1,128]{2,1,0:T(1,128)} %broadcast_in_dim.151), calls=%async_computation | async-start | bytes 32768 | tf_op jit(solution)/shard_map/all_to_all | solution.py:48
  25.7 6.6 %copy-start.6 = (s32[64]{0:T(128)S(1)}, s32[64]{0:T(128)}, u32[]{:S(2)}) copy-start(s32[64]{0:T(128)} %param.33) | copy-start | bytes 772
  25.7 6.6 %copy-start.9 = (s32[64]{0:T(128)S(1)}, s32[64]{0:T(128)}, u32[]{:S(2)}) copy-start(s32[64]{0:T(128)} %param.32) | copy-start | bytes 772
  25.7 35.5 %copy-start.5 = (f32[1920]{0:T(1024)S(1)}, f32[1920]{0:T(1024)}, u32[]{:S(2)}) copy-start(f32[1920]{0:T(1024)} %param.23) | copy-start | bytes 23044
  25.7 35.6 %copy-start.4 = (f32[2560]{0:T(1024)S(1)}, f32[2560]{0:T(1024)}, u32[]{:S(2)}) copy-start(f32[2560]{0:T(1024)} %param.27) | copy-start | bytes 30724
  25.7 36.3 %copy-start.1 = (bf16[2,5,1024,128]{3,2,1,0:T(8,128)(2,1)S(1)}, bf16[2,5,1024,128]{3,2,1,0:T(8,128)(2,1)}, u32[]{:S(2)}) copy-start(bf16[2,5,1024,128]{3,2,1,0:T(8,128)(2,1)} %param.30) | copy-start | bytes 7864324
  27.6 32.0 %all-to-all-start.1 = ((f32[32,2,4480]{2,1,0:T(2,128)}), f32[32,2,4480]{2,1,0:T(2,128)}, u32[]{:S(2)}, u32[]{:S(2)}) async-start(f32[32,2,4480]{2,1,0:T(2,128)} %copy.71), calls=%async_computation.1 | async-start | bytes 2293760 | tf_op jit(solution)/shard_map/all_to_all | solution.py:121
  61.3 1.8 %copy-start.2 = (bf16[2,5,1024,128]{3,2,1,0:T(8,128)(2,1)S(1)}, bf16[2,5,1024,128]{3,2,1,0:T(8,128)(2,1)}, u32[]{:S(2)}) copy-start(bf16[2,5,1024,128]{3,2,1,0:T(8,128)(2,1)} %param.31) | copy-start | bytes 7864324
  64.6 19.0 %all-to-all-start.2 = ((bf16[32,2,3200]{2,1,0:T(2,128)(2,1)}), bf16[32,2,3200]{2,1,0:T(2,128)(2,1)}, u32[]{:S(2)}, u32[]{:S(2)}) async-start(bf16[32,2,3200]{2,1,0:T(2,128)(2,1)} %broadcast_in_dim.158), calls=%async_computation.2 | async-start | bytes 819200 | tf_op jit(solution)/shard_map/all_to_all | solution.py:156
  87.1 5.4 %collective-permute-start = (f32[64,160]{1,0:T(8,128)S(1)}, f32[64,160]{1,0:T(8,128)S(1)}, u32[]{:S(2)}, u32[]{:S(2)}) collective-permute-start(f32[64,160]{1,0:T(8,128)S(1)} %reshape.230), channel_id=1, source_target_pairs={{0,1},{1,0},{2,3},{3,2},{4,5},{5,4},{6,7},{7,6},{8,9},{9,8},{10,11... | collective-permute-start | bytes 122888 | tf_op jit(solution)/shard_map/ppermute | solution.py:53
  92.5 3.2 %collective-permute-start.1 = (f32[64,160]{1,0:T(8,128)S(1)}, f32[64,160]{1,0:T(8,128)S(1)}, u32[]{:S(2)}, u32[]{:S(2)}) collective-permute-start(f32[64,160]{1,0:T(8,128)S(1)} %add.97), channel_id=1, source_target_pairs={{0,2},{1,3},{2,0},{3,1},{4,6},{5,7},{6,4},{7,5},{8,10},{9,11},{10,... | collective-permute-start | bytes 122888 | tf_op jit(solution)/shard_map/ppermute | solution.py:53
  95.7 6.8 %copy-start.3 = (bf16[64,160]{1,0:T(8,128)(2,1)S(1)}, bf16[64,160]{1,0:T(8,128)(2,1)}, u32[]{:S(2)}) copy-start(bf16[64,160]{1,0:T(8,128)(2,1)} %param.17) | copy-start | bytes 61444
  95.7 6.8 %copy-start.7 = (f32[160]{0:T(256)S(1)}, f32[160]{0:T(256)}, u32[]{:S(2)}) copy-start(f32[160]{0:T(256)} %param.29) | copy-start | bytes 1924
  95.7 6.8 %copy-start.8 = (f32[160]{0:T(256)S(1)}, f32[160]{0:T(256)}, u32[]{:S(2)}) copy-start(f32[160]{0:T(256)} %param.25) | copy-start | bytes 1924
  95.7 6.8 %collective-permute-start.2 = (f32[64,160]{1,0:T(8,128)S(1)}, f32[64,160]{1,0:T(8,128)S(1)}, u32[]{:S(2)}, u32[]{:S(2)}) collective-permute-start(f32[64,160]{1,0:T(8,128)S(1)} %add.98), channel_id=1, source_target_pairs={{0,6},{1,7},{2,4},{3,5},{4,2},{5,3},{6,0},{7,1},{8,14},{9,15},{10,... | collective-permute-start | bytes 122888 | tf_op jit(solution)/shard_map/ppermute | solution.py:53

commit v11 on v10

--- a/solution.py
+++ b/solution.py
@@ -95,7 +95,7 @@
     matches = assignment[:, None] == slot_ids[None, :]
     to_request = matches.astype(jnp.float32)
     x_slot = jnp.dot(matches.T.astype(jnp.bfloat16), hidden_in, preferred_element_type=jnp.float32)
-    w_both = lax.optimization_barrier(jnp.concatenate([w_out, w_down], axis=0))
+    w_both = jnp.concatenate([w_out, w_down], axis=0)
     stats = jnp.sum(jnp.where(matches[None], stats[:, :, None], 0.0), axis=1)
     sum_rows, sum_squares = stats[0], stats[1]
     row_mean = sum_rows / D
@@ -118,9 +118,9 @@
         ],
         axis=2,
     )
-    reduced = jnp.sum(lax.all_to_all(partial, "gx", 0, 0, tiled=False), axis=0)
-    qkv = reduced[:, :qkv_cols] + b_qkv
-    up = reduced[:, qkv_cols:] + b_up
+    received = lax.all_to_all(partial, "gx", 0, 0, tiled=False)
+    qkv = jnp.sum(received[:, :, :qkv_cols], axis=0) + b_qkv
+    up = jnp.sum(received[:, :, qkv_cols:], axis=0) + b_up
     qkv = qkv.reshape(rows_dev, heads_dev, 3, HD)
     position = my_len - 1
     query = rotate(qkv[:, :, 0], position).astype(jnp.bfloat16)

time: 104 us -> 102 us (0.981)
  blocking collectives: 0 us -> 18.7 us
  waiting for transfers between devices: 47.3 us -> 37.4 us
  starting transfers between devices: 32.1 us -> 25.2 us
  other arithmetic: 11 us -> 9.58 us
  matrix products: 6.45 us -> 5.1 us
    all_to_all x0 -> x1, blocking collectives: none -> 18.7 us  [layer(): lax.all_to_all(jnp.broadcast_to(both[None], (gx_size,) + both.shape), 'gx...]
    all_to_all x2 -> x1, waiting for transfers between devices: 36.8 us -> 26.9 us  [layer(): received = lax.all_to_all(partial, 'gx', 0, 0, tiled=False)]
    all_to_all x2 -> x1, starting transfers between devices: 11.5 us -> 4.65 us  [layer(): received = lax.all_to_all(partial, 'gx', 0, 0, tiled=False)]
    concatenate x1 -> x0, other arithmetic: 2.21 us -> none  [layer(): w_both = lax.optimization_barrier(jnp.concatenate([w_out, w_down], axis=0))]
    dot_general x1, matrix products: 1.79 us -> 0.45 us  [layer(): jnp.einsum('sbk,kn->sbn', gathered, w_both, preferred_element_type=jnp.fl...]
    reduce_sum x1 -> x2, other arithmetic: 1.6 us -> 2.37 us  [the longest x1 1.23 us: layer(): up = jnp.sum(received[:, :, qkv_cols:], axis=0) + b_up]
  transfers between devices with their start and end apart: 6 -> 5, of which waited for: 5 -> 4; matrix products, arithmetic and copies ran while one was open for 7% -> 5% of each run, Pallas kernels for 0% -> 0%
where the time goes in v11:
time: 102 us
  waiting for transfers between devices  37.4 us (37%)
  starting transfers between devices  25.2 us (25%)
  blocking collectives  18.7 us (18%)
  other arithmetic  9.58 us (9%)
  matrix products  5.1 us (5%)
  local copies, waits for them, and re-layouts  4.75 us (5%)
    all_to_all x1, waiting for transfers between devices, layer(): received = lax.all_to_all(partial, 'gx', 0, 0, tiled=False)  26.9 us
    all_to_all x1, blocking collectives, layer(): lax.all_to_all(jnp.broadcast_to(both[None], (gx_size,) + both.shape), 'gx...  18.7 us
    all_to_all x1, starting transfers between devices, exchange_sum(): return jnp.sum(lax.all_to_all(spread, axis, 0, 0, tiled=False), axis=0)  11.9 us
    ppermute x3, starting transfers between devices, pair_sum(): x = x + lax.ppermute(x, axis, pairs)  8.68 us
    all_to_all x1, waiting for transfers between devices, exchange_sum(): return jnp.sum(lax.all_to_all(spread, axis, 0, 0, tiled=False), axis=0)  7.8 us
    all_to_all x1, starting transfers between devices, layer(): received = lax.all_to_all(partial, 'gx', 0, 0, tiled=False)  4.65 us
    select_n x1, other arithmetic, layer(): new_values = jnp.where(at_row, new_value[:, :, None, :], value_cache)  3.96 us
    ppermute x3, waiting for transfers between devices, pair_sum(): x = x + lax.ppermute(x, axis, pairs)  2.71 us
  transfers between devices with their start and end apart: 5, of which 4 were waited for; matrix products, arithmetic and copies ran while one was open for 5% of the time, Pallas kernels for 0%

profile of v11, /device:TPU:1, one launch (start us, length us, event | category | flops | bytes accessed | tf_op | source)
XLA Modules:
  0.0 101.7 jit_solution(18427790679441051240)
XLA Ops:
  0.6 0.9 convert_reduce_fusion
  1.7 0.6 broadcast_in_dim.151
  2.3 11.9 %all-to-all-start = ((f32[32,1,128]{2,1,0:T(1,128)}), f32[32,1,128]{2,1,0:T(1,128)S(1)}, u32[]{:S(2)}, u32[]{:S(2)}) async-start(f32[32,1,128]{2,1,0:T(1,128)} %broadcast_in_dim.151), calls=%async_computation | async-start | bytes 32768 | tf_op jit(solution)/shard_map/all_to_all | solution.py:48
  14.2 0.7 iota_compare_fusion
  14.9 7.8 %all-to-all-done = f32[32,1,128]{2,1,0:T(1,128)S(1)} async-done(((f32[32,1,128]{2,1,0:T(1,128)}), f32[32,1,128]{2,1,0:T(1,128)S(1)}, u32[]{:S(2)}, u32[]{:S(2)}) %all-to-all-start) | async-done | bytes 16416 | tf_op jit(solution)/shard_map/all_to_all | solution.py:48
  22.8 0.1 select_reduce_fusion
  22.9 1.0 %add_convert_fusion.1 = (bf16[64,160]{1,0:T(8,128)(2,1)S(1)}, bf16[64,160]{1,0:T(8,128)(2,1)S(1)}) fusion(f32[160]{0:T(256)} %param.19, f32[160]{0:T(256)} %param.18, f32[160]{0:T(256)} %param.21, f32[160]{0:T(256)} %param.20, f32[64]{0:T(128)S(1)} %fusion.39, f32[64]{0:T(128)S(1)} %multiply_bitcast_fusion, bf16[64,160]{1,0:T(8,128)(2,1)} %param.17, ...), kind=kOutput, calls=%fused_computation.29 | convolution fusion | flops 1396736 | bytes 64768 | tf_op jit(solution)/shard_map/dot_general | solution.py:97
  24.0 1.3 %fusion.13 = f32[32,2,1920]{2,0,1:T(8,128)S(1)} fusion(bf16[160,1920]{1,0:T(8,128)(2,1)} %param.22, bf16[32,2,160]{2,1,0:T(2,128)(2,1)S(1)} %reshape.230), kind=kOutput, calls=%fused_computation.20 | convolution fusion | flops 39321600 | bytes 1126400 | tf_op jit(solution)/shard_map/sbk,kn->sbn/dot_general | solution.py:112
  25.3 0.3 fusion.11
  25.7 1.9 %copy.68 = f32[32,2,4480]{2,1,0:T(2,128)} copy(f32[32,2,4480]{2,0,1:T(8,128)S(1)} %pad_maximum_fusion) | data formatting | bytes 2293760 | tf_op jit(solution)/shard_map/concatenate | solution.py:110
  27.6 4.7 %all-to-all-start.1 = ((f32[32,2,4480]{2,1,0:T(2,128)}), f32[32,2,4480]{2,1,0:T(2,128)}, u32[]{:S(2)}, u32[]{:S(2)}) async-start(f32[32,2,4480]{2,1,0:T(2,128)} %copy.68), calls=%async_computation.1 | async-start | bytes 2293760 | tf_op jit(solution)/shard_map/all_to_all | solution.py:121
  32.6 0.1 multiply_cosine_fusion
  32.8 26.9 %all-to-all-done.1 = f32[32,2,4480]{2,1,0:T(2,128)} async-done(((f32[32,2,4480]{2,1,0:T(2,128)}), f32[32,2,4480]{2,1,0:T(2,128)}, u32[]{:S(2)}, u32[]{:S(2)}) %all-to-all-start.1) | async-done | bytes 1146912 | tf_op jit(solution)/shard_map/all_to_all | solution.py:121
  59.6 1.1 %slice_reduce_fusion.1 = f32[2,1920]{1,0:T(2,128)S(1)} fusion(f32[32,2,4480]{2,1,0:T(2,128)} %all-to-all-done.1), kind=kLoop, calls=%fused_computation.22 | loop fusion | flops 119040 | bytes 506880 | tf_op jit(solution)/shard_map/reduce_sum | solution.py:122
  61.1 0.2 fusion.33
  61.3 0.8 fusion.34
  62.1 0.3 convert_reduce_fusion.1
  62.4 1.2 %slice_reduce_fusion = f32[2,2560]{1,0:T(2,128)S(1)} fusion(f32[32,2,4480]{2,1,0:T(2,128)} %all-to-all-done.1), kind=kLoop, calls=%fused_computation.19 | loop fusion | flops 158720 | bytes 675840 | tf_op jit(solution)/shard_map/reduce_sum | solution.py:123
  63.7 0.2 fusion.27
  63.9 0.4 fusion.20
  64.4 0.2 broadcast_in_dim.158
  64.6 18.7 %all_to_all.16 = bf16[32,2,3200]{2,1,0:T(2,128)(2,1)S(1)} all-to-all(bf16[32,2,3200]{2,1,0:T(2,128)(2,1)S(1)} %broadcast_in_dim.158), channel_id=1, replica_groups=mesh['gx'=32,'gy'=8] {'gx'}, dimensions={0} | all-to-all | bytes 819200 | tf_op jit(solution)/shard_map/all_to_all | solution.py:156
  83.4 0.4 fusion.8
  83.8 0.7 copy.73
  84.5 0.9 reshape.233
  85.4 4.5 %collective-permute-start = (f32[64,160]{1,0:T(8,128)S(1)}, f32[64,160]{1,0:T(8,128)S(1)}, u32[]{:S(2)}, u32[]{:S(2)}) collective-permute-start(f32[64,160]{1,0:T(8,128)S(1)} %reshape.233), channel_id=1, source_target_pairs={{0,1},{1,0},{2,3},{3,2},{4,5},{5,4},{6,7},{7,6},{8,9},{9,8},{10,11... | collective-permute-start | bytes 122888 | tf_op jit(solution)/shard_map/ppermute | solution.py:53
  89.9 0.9 collective-permute-done
  90.8 1.4 %collective-permute-start.1 = (f32[64,160]{1,0:T(8,128)S(1)}, f32[64,160]{1,0:T(8,128)S(1)}, u32[]{:S(2)}, u32[]{:S(2)}) collective-permute-start(f32[64,160]{1,0:T(8,128)S(1)} %add.101), channel_id=1, source_target_pairs={{0,2},{1,3},{2,0},{3,1},{4,6},{5,7},{6,4},{7,5},{8,10},{9,11},{10,... | collective-permute-start | bytes 122888 | tf_op jit(solution)/shard_map/ppermute | solution.py:53
  92.2 1.8 %collective-permute-done.1 = f32[64,160]{1,0:T(8,128)S(1)} collective-permute-done((f32[64,160]{1,0:T(8,128)S(1)}, f32[64,160]{1,0:T(8,128)S(1)}, u32[]{:S(2)}, u32[]{:S(2)}) %collective-permute-start.1) | collective-permute-done | bytes 40992 | tf_op jit(solution)/shard_map/ppermute | solution.py:53
  94.1 2.8 %collective-permute-start.2 = (f32[64,160]{1,0:T(8,128)S(1)}, f32[64,160]{1,0:T(8,128)S(1)}, u32[]{:S(2)}, u32[]{:S(2)}) collective-permute-start(f32[64,160]{1,0:T(8,128)S(1)} %add.102), channel_id=1, source_target_pairs={{0,6},{1,7},{2,4},{3,5},{4,2},{5,3},{6,0},{7,1},{8,14},{9,15},{10,... | collective-permute-start | bytes 122888 | tf_op jit(solution)/shard_map/ppermute | solution.py:53
  96.9 4.0 %broadcast_select_fusion = (bf16[2,5,1024,128]{3,2,1,0:T(8,128)(2,1)}, bf16[2,5,1024,128]{3,2,1,0:T(8,128)(2,1)}) fusion(bf16[2,5,1024,128]{3,2,1,0:T(8,128)(2,1)} %param.31, pred[2,1024]{1,0:T(4,128)(4,1)S(1)} %get-tuple-element.32, bf16[2,5,128]{2,1,0:T(8,128)(2,1)S(1)} %copy.75, bf16[2,5,1024,128]{3,2,1,0:T(8,128)(2,1)S(1)} %copy-done.1, ...), kind=kLoop, calls=%fused_computation.1 | loop fusion | flops 2621440 | bytes 10492928 | tf_op jit(solution)/shard_map/jit(_where)/select_n | solution.py:154
  100.9 0.8 fusion.5
  (55 shorter events, 1.1 us)
Async XLA Ops:
  0.6 24.7 %copy-start = (bf16[160,2560]{1,0:T(8,128)(2,1)S(1)}, bf16[160,2560]{1,0:T(8,128)(2,1)}, u32[]{:S(2)}) copy-start(bf16[160,2560]{1,0:T(8,128)(2,1)} %param.26) | copy-start | bytes 2457604
  2.3 20.4 %all-to-all-start = ((f32[32,1,128]{2,1,0:T(1,128)}), f32[32,1,128]{2,1,0:T(1,128)S(1)}, u32[]{:S(2)}, u32[]{:S(2)}) async-start(f32[32,1,128]{2,1,0:T(1,128)} %broadcast_in_dim.151), calls=%async_computation | async-start | bytes 32768 | tf_op jit(solution)/shard_map/all_to_all | solution.py:48
  25.7 6.6 %copy-start.5 = (f32[1920]{0:T(1024)S(1)}, f32[1920]{0:T(1024)}, u32[]{:S(2)}) copy-start(f32[1920]{0:T(1024)} %param.23) | copy-start | bytes 23044
  25.7 6.6 %copy-start.6 = (s32[64]{0:T(128)S(1)}, s32[64]{0:T(128)}, u32[]{:S(2)}) copy-start(s32[64]{0:T(128)} %param.33) | copy-start | bytes 772
  25.7 6.6 %copy-start.11 = (s32[64]{0:T(128)S(1)}, s32[64]{0:T(128)}, u32[]{:S(2)}) copy-start(s32[64]{0:T(128)} %param.32) | copy-start | bytes 772
  25.7 35.6 %copy-start.1 = (bf16[2,5,1024,128]{3,2,1,0:T(8,128)(2,1)S(1)}, bf16[2,5,1024,128]{3,2,1,0:T(8,128)(2,1)}, u32[]{:S(2)}) copy-start(bf16[2,5,1024,128]{3,2,1,0:T(8,128)(2,1)} %param.30) | copy-start | bytes 7864324
  27.6 32.0 %all-to-all-start.1 = ((f32[32,2,4480]{2,1,0:T(2,128)}), f32[32,2,4480]{2,1,0:T(2,128)}, u32[]{:S(2)}, u32[]{:S(2)}) async-start(f32[32,2,4480]{2,1,0:T(2,128)} %copy.68), calls=%async_computation.1 | async-start | bytes 2293760 | tf_op jit(solution)/shard_map/all_to_all | solution.py:121
  32.3 31.4 %copy-start.4 = (f32[2560]{0:T(1024)S(1)}, f32[2560]{0:T(1024)}, u32[]{:S(2)}) copy-start(f32[2560]{0:T(1024)} %param.27) | copy-start | bytes 30724
  60.8 3.0 %copy-start.2 = (bf16[2,5,1024,128]{3,2,1,0:T(8,128)(2,1)S(1)}, bf16[2,5,1024,128]{3,2,1,0:T(8,128)(2,1)}, u32[]{:S(2)}) copy-start(bf16[2,5,1024,128]{3,2,1,0:T(8,128)(2,1)} %param.31) | copy-start | bytes 7864324
  62.1 21.3 %copy-start.9 = (bf16[2560,160]{0,1:T(8,128)(2,1)S(1)}, bf16[2560,160]{0,1:T(8,128)(2,1)}, u32[]{:S(2)}) copy-start(bf16[2560,160]{0,1:T(8,128)(2,1)} %param.28) | copy-start | bytes 2457604
  62.1 21.3 %copy-start.10 = (bf16[640,160]{0,1:T(8,128)(2,1)S(1)}, bf16[640,160]{0,1:T(8,128)(2,1)}, u32[]{:S(2)}) copy-start(bf16[640,160]{0,1:T(8,128)(2,1)} %param.24) | copy-start | bytes 614404
  85.4 5.4 %collective-permute-start = (f32[64,160]{1,0:T(8,128)S(1)}, f32[64,160]{1,0:T(8,128)S(1)}, u32[]{:S(2)}, u32[]{:S(2)}) collective-permute-start(f32[64,160]{1,0:T(8,128)S(1)} %reshape.233), channel_id=1, source_target_pairs={{0,1},{1,0},{2,3},{3,2},{4,5},{5,4},{6,7},{7,6},{8,9},{9,8},{10,11... | collective-permute-start | bytes 122888 | tf_op jit(solution)/shard_map/ppermute | solution.py:53
  90.8 3.2 %collective-permute-start.1 = (f32[64,160]{1,0:T(8,128)S(1)}, f32[64,160]{1,0:T(8,128)S(1)}, u32[]{:S(2)}, u32[]{:S(2)}) collective-permute-start(f32[64,160]{1,0:T(8,128)S(1)} %add.101), channel_id=1, source_target_pairs={{0,2},{1,3},{2,0},{3,1},{4,6},{5,7},{6,4},{7,5},{8,10},{9,11},{10,... | collective-permute-start | bytes 122888 | tf_op jit(solution)/shard_map/ppermute | solution.py:53
  94.0 6.8 %copy-start.3 = (bf16[64,160]{1,0:T(8,128)(2,1)S(1)}, bf16[64,160]{1,0:T(8,128)(2,1)}, u32[]{:S(2)}) copy-start(bf16[64,160]{1,0:T(8,128)(2,1)} %param.17) | copy-start | bytes 61444
  94.0 6.8 %copy-start.7 = (f32[160]{0:T(256)S(1)}, f32[160]{0:T(256)}, u32[]{:S(2)}) copy-start(f32[160]{0:T(256)} %param.29) | copy-start | bytes 1924
  94.0 6.8 %copy-start.8 = (f32[160]{0:T(256)S(1)}, f32[160]{0:T(256)}, u32[]{:S(2)}) copy-start(f32[160]{0:T(256)} %param.25) | copy-start | bytes 1924
  94.1 6.8 %collective-permute-start.2 = (f32[64,160]{1,0:T(8,128)S(1)}, f32[64,160]{1,0:T(8,128)S(1)}, u32[]{:S(2)}, u32[]{:S(2)}) collective-permute-start(f32[64,160]{1,0:T(8,128)S(1)} %add.102), channel_id=1, source_target_pairs={{0,6},{1,7},{2,4},{3,5},{4,2},{5,3},{6,0},{7,1},{8,14},{9,15},{10,... | collective-permute-start | bytes 122888 | tf_op jit(solution)/shard_map/ppermute | solution.py:53

commit v12 on v8

--- a/solution.py
+++ b/solution.py
@@ -43,11 +43,6 @@
     return [(i, i ^ (1 << bit)) for i in range(size)]
 
 
-def exchange_sum(x, axis, size):
-    spread = jnp.broadcast_to(x[None], (size,) + x.shape)
-    return jnp.sum(lax.all_to_all(spread, axis, 0, 0, tiled=False), axis=0)
-
-
 def pair_sum(x, axis, rounds):
     for pairs in rounds:
         x = x + lax.ppermute(x, axis, pairs)
@@ -86,11 +81,13 @@
     rows_dev = key_cache.shape[0]
     heads_dev = key_cache.shape[1]
     wide_in = hidden_in.astype(jnp.float32)
-    stats = exchange_sum(
-        jnp.stack([jnp.sum(wide_in, axis=1), jnp.sum(wide_in * wide_in, axis=1)]),
-        "gx",
-        gx_size,
+    spread = jnp.broadcast_to(
+        jnp.concatenate([wide_in, wide_in * wide_in], axis=0)[None],
+        (gx_size, 2 * requests, wide_in.shape[1]),
     )
+    stats = jnp.sum(
+        lax.all_to_all(jnp.sum(spread, axis=2), "gx", 0, 0, tiled=False), axis=0
+    ).reshape(2, requests)
     slot_ids = lax.iota(jnp.int32, requests)
     matches = assignment[:, None] == slot_ids[None, :]
     to_request = matches.astype(jnp.float32)

time: 103 us -> 102 us (level)
  no operation moved by 1% of the time
where the time goes in v12:
time: 102 us
  waiting for transfers between devices  37.4 us (37%)
  starting transfers between devices  25.2 us (25%)
  blocking collectives  18.7 us (18%)
  other arithmetic  9.49 us (9%)
  matrix products  5.1 us (5%)
  local copies, waits for them, and re-layouts  4.74 us (5%)
    all_to_all x1, waiting for transfers between devices, layer(): reduced = jnp.sum(lax.all_to_all(partial, 'gx', 0, 0, tiled=False), axis=0)  26.9 us
    all_to_all x1, blocking collectives, layer(): lax.all_to_all(jnp.broadcast_to(both[None], (gx_size,) + both.shape), 'gx...  18.7 us
    all_to_all x1, starting transfers between devices, layer(): lax.all_to_all(jnp.sum(spread, axis=2), 'gx', 0, 0, tiled=False)  11.9 us
    ppermute x3, starting transfers between devices, pair_sum(): x = x + lax.ppermute(x, axis, pairs)  8.68 us
    all_to_all x1, waiting for transfers between devices, layer(): lax.all_to_all(jnp.sum(spread, axis=2), 'gx', 0, 0, tiled=False)  7.8 us
    all_to_all x1, starting transfers between devices, layer(): reduced = jnp.sum(lax.all_to_all(partial, 'gx', 0, 0, tiled=False), axis=0)  4.66 us
    select_n x1, other arithmetic, layer(): new_values = jnp.where(at_row, new_value[:, :, None, :], value_cache)  3.96 us
    ppermute x3, waiting for transfers between devices, pair_sum(): x = x + lax.ppermute(x, axis, pairs)  2.72 us
  transfers between devices with their start and end apart: 5, of which 4 were waited for; matrix products, arithmetic and copies ran while one was open for 5% of the time, Pallas kernels for 0%

profile of v12, /device:TPU:1, one launch (start us, length us, event | category | flops | bytes accessed | tf_op | source)
XLA Modules:
  0.0 101.7 jit_solution(3141045520289232203)
XLA Ops:
  0.6 0.8 convert_multiply_fusion
  1.5 0.8 convert_element_type.47
  2.2 0.1 maximum_reduce_fusion
  2.4 0.6 reduce_sum.67
  3.0 11.9 %all-to-all-start = ((f32[32,1,128]{2,1,0:T(1,128)}), f32[32,1,128]{2,1,0:T(1,128)S(1)}, u32[]{:S(2)}, u32[]{:S(2)}) async-start(f32[32,1,128]{2,1,0:T(1,128)} %reduce_sum.67), calls=%async_computation | async-start | bytes 32768 | tf_op jit(solution)/shard_map/all_to_all | solution.py:89
  14.9 0.7 iota_compare_fusion
  15.6 7.8 %all-to-all-done = f32[32,1,128]{2,1,0:T(1,128)S(1)} async-done(((f32[32,1,128]{2,1,0:T(1,128)}), f32[32,1,128]{2,1,0:T(1,128)S(1)}, u32[]{:S(2)}, u32[]{:S(2)}) %all-to-all-start) | async-done | bytes 16416 | tf_op jit(solution)/shard_map/all_to_all | solution.py:89
  23.6 1.0 %add_convert_fusion.1 = (bf16[64,160]{1,0:T(8,128)(2,1)S(1)}, bf16[64,160]{1,0:T(8,128)(2,1)S(1)}) fusion(f32[160]{0:T(256)} %param.19, f32[160]{0:T(256)} %param.18, f32[160]{0:T(256)} %param.21, f32[160]{0:T(256)} %param.20, f32[64]{0:T(128)S(1)} %fusion.38, f32[64]{0:T(128)S(1)} %multiply_bitcast_fusion, bf16[64,160]{1,0:T(8,128)(2,1)} %param.17, ...), kind=kOutput, calls=%fused_computation.25 | convolution fusion | flops 1396736 | bytes 64768 | tf_op jit(solution)/shard_map/dot_general | solution.py:94
  24.7 1.3 %fusion.13 = f32[32,2,1920]{2,0,1:T(8,128)S(1)} fusion(bf16[160,1920]{1,0:T(8,128)(2,1)} %param.22, bf16[32,2,160]{2,1,0:T(2,128)(2,1)S(1)} %reshape.224), kind=kOutput, calls=%fused_computation.19 | convolution fusion | flops 39321600 | bytes 1126400 | tf_op jit(solution)/shard_map/sbk,kn->sbn/dot_general | solution.py:109
  26.0 0.2 fusion.11
  26.4 1.9 %copy.71 = f32[32,2,4480]{2,1,0:T(2,128)} copy(f32[32,2,4480]{2,0,1:T(8,128)S(1)} %pad_maximum_fusion) | data formatting | bytes 2293760 | tf_op jit(solution)/shard_map/concatenate | solution.py:107
  28.3 4.7 %all-to-all-start.1 = ((f32[32,2,4480]{2,1,0:T(2,128)}), f32[32,2,4480]{2,1,0:T(2,128)}, u32[]{:S(2)}, u32[]{:S(2)}) async-start(f32[32,2,4480]{2,1,0:T(2,128)} %copy.71), calls=%async_computation.1 | async-start | bytes 2293760 | tf_op jit(solution)/shard_map/all_to_all | solution.py:118
  33.2 0.1 multiply_cosine_fusion
  33.4 26.9 %all-to-all-done.1 = f32[32,2,4480]{2,1,0:T(2,128)} async-done(((f32[32,2,4480]{2,1,0:T(2,128)}), f32[32,2,4480]{2,1,0:T(2,128)}, u32[]{:S(2)}, u32[]{:S(2)}) %all-to-all-start.1) | async-done | bytes 1146912 | tf_op jit(solution)/shard_map/all_to_all | solution.py:118
  60.3 1.6 %reduce_sum.70 = f32[2,4480]{1,0:T(2,128)S(1)} reduce(f32[32,2,4480]{2,1,0:T(2,128)} %all-to-all-done.1, f32[]{:T(128)} %constant.11.clone.1), dimensions={0}, to_apply=%region_4.5 | reduce | flops 277760 | bytes 1182724 | tf_op jit(solution)/shard_map/reduce_sum | solution.py:118
  62.1 0.2 fusion.26
  62.5 0.2 fusion.32
  62.7 0.8 fusion.33
  63.5 0.3 convert_reduce_fusion
  63.8 0.4 fusion.19
  64.4 0.2 broadcast_in_dim.155
  64.6 18.7 %all_to_all.16 = bf16[32,2,3200]{2,1,0:T(2,128)(2,1)S(1)} all-to-all(bf16[32,2,3200]{2,1,0:T(2,128)(2,1)S(1)} %broadcast_in_dim.155), channel_id=1, replica_groups=mesh['gx'=32,'gy'=8] {'gx'}, dimensions={0} | all-to-all | bytes 819200 | tf_op jit(solution)/shard_map/all_to_all | solution.py:153
  83.3 0.4 fusion.8
  83.8 0.7 copy.76
  84.5 0.9 reshape.228
  85.3 4.5 %collective-permute-start = (f32[64,160]{1,0:T(8,128)S(1)}, f32[64,160]{1,0:T(8,128)S(1)}, u32[]{:S(2)}, u32[]{:S(2)}) collective-permute-start(f32[64,160]{1,0:T(8,128)S(1)} %reshape.228), channel_id=1, source_target_pairs={{0,1},{1,0},{2,3},{3,2},{4,5},{5,4},{6,7},{7,6},{8,9},{9,8},{10,11... | collective-permute-start | bytes 122888 | tf_op jit(solution)/shard_map/ppermute | solution.py:48
  89.8 0.9 collective-permute-done
  90.7 1.4 %collective-permute-start.1 = (f32[64,160]{1,0:T(8,128)S(1)}, f32[64,160]{1,0:T(8,128)S(1)}, u32[]{:S(2)}, u32[]{:S(2)}) collective-permute-start(f32[64,160]{1,0:T(8,128)S(1)} %add.97), channel_id=1, source_target_pairs={{0,2},{1,3},{2,0},{3,1},{4,6},{5,7},{6,4},{7,5},{8,10},{9,11},{10,... | collective-permute-start | bytes 122888 | tf_op jit(solution)/shard_map/ppermute | solution.py:48
  92.1 1.8 %collective-permute-done.1 = f32[64,160]{1,0:T(8,128)S(1)} collective-permute-done((f32[64,160]{1,0:T(8,128)S(1)}, f32[64,160]{1,0:T(8,128)S(1)}, u32[]{:S(2)}, u32[]{:S(2)}) %collective-permute-start.1) | collective-permute-done | bytes 40992 | tf_op jit(solution)/shard_map/ppermute | solution.py:48
  94.0 2.8 %collective-permute-start.2 = (f32[64,160]{1,0:T(8,128)S(1)}, f32[64,160]{1,0:T(8,128)S(1)}, u32[]{:S(2)}, u32[]{:S(2)}) collective-permute-start(f32[64,160]{1,0:T(8,128)S(1)} %add.98), channel_id=1, source_target_pairs={{0,6},{1,7},{2,4},{3,5},{4,2},{5,3},{6,0},{7,1},{8,14},{9,15},{10,... | collective-permute-start | bytes 122888 | tf_op jit(solution)/shard_map/ppermute | solution.py:48
  96.8 4.0 %broadcast_select_fusion = (bf16[2,5,1024,128]{3,2,1,0:T(8,128)(2,1)}, bf16[2,5,1024,128]{3,2,1,0:T(8,128)(2,1)}) fusion(bf16[2,5,1024,128]{3,2,1,0:T(8,128)(2,1)} %param.31, pred[2,1024]{1,0:T(4,128)(4,1)S(1)} %get-tuple-element.30, bf16[2,5,128]{2,1,0:T(8,128)(2,1)S(1)} %copy.78, bf16[2,5,1024,128]{3,2,1,0:T(8,128)(2,1)S(1)} %copy-done.1, ...), kind=kLoop, calls=%fused_computation.1 | loop fusion | flops 2621440 | bytes 10492928 | tf_op jit(solution)/shard_map/jit(_where)/select_n | solution.py:151
  100.8 0.8 fusion.5
  (54 shorter events, 1.1 us)
Async XLA Ops:
  0.6 25.4 %copy-start = (bf16[160,2560]{1,0:T(8,128)(2,1)S(1)}, bf16[160,2560]{1,0:T(8,128)(2,1)}, u32[]{:S(2)}) copy-start(bf16[160,2560]{1,0:T(8,128)(2,1)} %param.26) | copy-start | bytes 2457604
  3.0 20.4 %all-to-all-start = ((f32[32,1,128]{2,1,0:T(1,128)}), f32[32,1,128]{2,1,0:T(1,128)S(1)}, u32[]{:S(2)}, u32[]{:S(2)}) async-start(f32[32,1,128]{2,1,0:T(1,128)} %reduce_sum.67), calls=%async_computation | async-start | bytes 32768 | tf_op jit(solution)/shard_map/all_to_all | solution.py:89
  26.4 6.6 %copy-start.6 = (s32[64]{0:T(128)S(1)}, s32[64]{0:T(128)}, u32[]{:S(2)}) copy-start(s32[64]{0:T(128)} %param.33) | copy-start | bytes 772
  26.4 6.6 %copy-start.11 = (s32[64]{0:T(128)S(1)}, s32[64]{0:T(128)}, u32[]{:S(2)}) copy-start(s32[64]{0:T(128)} %param.32) | copy-start | bytes 772
  26.4 35.5 %copy-start.5 = (f32[1920]{0:T(1024)S(1)}, f32[1920]{0:T(1024)}, u32[]{:S(2)}) copy-start(f32[1920]{0:T(1024)} %param.23) | copy-start | bytes 23044
  26.4 35.6 %copy-start.4 = (f32[2560]{0:T(1024)S(1)}, f32[2560]{0:T(1024)}, u32[]{:S(2)}) copy-start(f32[2560]{0:T(1024)} %param.27) | copy-start | bytes 30724
  26.4 36.3 %copy-start.1 = (bf16[2,5,1024,128]{3,2,1,0:T(8,128)(2,1)S(1)}, bf16[2,5,1024,128]{3,2,1,0:T(8,128)(2,1)}, u32[]{:S(2)}) copy-start(bf16[2,5,1024,128]{3,2,1,0:T(8,128)(2,1)} %param.30) | copy-start | bytes 7864324
  28.3 32.0 %all-to-all-start.1 = ((f32[32,2,4480]{2,1,0:T(2,128)}), f32[32,2,4480]{2,1,0:T(2,128)}, u32[]{:S(2)}, u32[]{:S(2)}) async-start(f32[32,2,4480]{2,1,0:T(2,128)} %copy.71), calls=%async_computation.1 | async-start | bytes 2293760 | tf_op jit(solution)/shard_map/all_to_all | solution.py:118
  62.0 1.8 %copy-start.2 = (bf16[2,5,1024,128]{3,2,1,0:T(8,128)(2,1)S(1)}, bf16[2,5,1024,128]{3,2,1,0:T(8,128)(2,1)}, u32[]{:S(2)}) copy-start(bf16[2,5,1024,128]{3,2,1,0:T(8,128)(2,1)} %param.31) | copy-start | bytes 7864324
  63.5 19.8 %copy-start.9 = (bf16[2560,160]{0,1:T(8,128)(2,1)S(1)}, bf16[2560,160]{0,1:T(8,128)(2,1)}, u32[]{:S(2)}) copy-start(bf16[2560,160]{0,1:T(8,128)(2,1)} %param.28) | copy-start | bytes 2457604
  63.5 19.8 %copy-start.10 = (bf16[640,160]{0,1:T(8,128)(2,1)S(1)}, bf16[640,160]{0,1:T(8,128)(2,1)}, u32[]{:S(2)}) copy-start(bf16[640,160]{0,1:T(8,128)(2,1)} %param.24) | copy-start | bytes 614404
  85.3 5.4 %collective-permute-start = (f32[64,160]{1,0:T(8,128)S(1)}, f32[64,160]{1,0:T(8,128)S(1)}, u32[]{:S(2)}, u32[]{:S(2)}) collective-permute-start(f32[64,160]{1,0:T(8,128)S(1)} %reshape.228), channel_id=1, source_target_pairs={{0,1},{1,0},{2,3},{3,2},{4,5},{5,4},{6,7},{7,6},{8,9},{9,8},{10,11... | collective-permute-start | bytes 122888 | tf_op jit(solution)/shard_map/ppermute | solution.py:48
  90.7 3.2 %collective-permute-start.1 = (f32[64,160]{1,0:T(8,128)S(1)}, f32[64,160]{1,0:T(8,128)S(1)}, u32[]{:S(2)}, u32[]{:S(2)}) collective-permute-start(f32[64,160]{1,0:T(8,128)S(1)} %add.97), channel_id=1, source_target_pairs={{0,2},{1,3},{2,0},{3,1},{4,6},{5,7},{6,4},{7,5},{8,10},{9,11},{10,... | collective-permute-start | bytes 122888 | tf_op jit(solution)/shard_map/ppermute | solution.py:48
  94.0 6.8 %copy-start.3 = (bf16[64,160]{1,0:T(8,128)(2,1)S(1)}, bf16[64,160]{1,0:T(8,128)(2,1)}, u32[]{:S(2)}) copy-start(bf16[64,160]{1,0:T(8,128)(2,1)} %param.17) | copy-start | bytes 61444
  94.0 6.8 %copy-start.7 = (f32[160]{0:T(256)S(1)}, f32[160]{0:T(256)}, u32[]{:S(2)}) copy-start(f32[160]{0:T(256)} %param.29) | copy-start | bytes 1924
  94.0 6.8 %copy-start.8 = (f32[160]{0:T(256)S(1)}, f32[160]{0:T(256)}, u32[]{:S(2)}) copy-start(f32[160]{0:T(256)} %param.25) | copy-start | bytes 1924
  94.0 6.8 %collective-permute-start.2 = (f32[64,160]{1,0:T(8,128)S(1)}, f32[64,160]{1,0:T(8,128)S(1)}, u32[]{:S(2)}, u32[]{:S(2)}) collective-permute-start(f32[64,160]{1,0:T(8,128)S(1)} %add.98), channel_id=1, source_target_pairs={{0,6},{1,7},{2,4},{3,5},{4,2},{5,3},{6,0},{7,1},{8,14},{9,15},{10,... | collective-permute-start | bytes 122888 | tf_op jit(solution)/shard_map/ppermute | solution.py:48

commit v13 on v10

--- a/solution.py
+++ b/solution.py
@@ -95,7 +95,7 @@
     matches = assignment[:, None] == slot_ids[None, :]
     to_request = matches.astype(jnp.float32)
     x_slot = jnp.dot(matches.T.astype(jnp.bfloat16), hidden_in, preferred_element_type=jnp.float32)
-    w_both = lax.optimization_barrier(jnp.concatenate([w_out, w_down], axis=0))
+    w_both = jnp.concatenate([w_out, w_down], axis=0)
     stats = jnp.sum(jnp.where(matches[None], stats[:, :, None], 0.0), axis=1)
     sum_rows, sum_squares = stats[0], stats[1]
     row_mean = sum_rows / D
@@ -156,11 +156,13 @@
     gathered = lax.all_to_all(
         jnp.broadcast_to(both[None], (gx_size,) + both.shape), "gx", 0, 0, tiled=False
     )
-    slot_part = jnp.einsum(
-        "sbk,kn->sbn", gathered, w_both, preferred_element_type=jnp.float32
-    ).reshape(requests, w_out.shape[1])
+    request_rows = jnp.dot(
+        matches.astype(jnp.bfloat16),
+        gathered.reshape(requests, gathered.shape[2]),
+        preferred_element_type=jnp.float32,
+    ).astype(jnp.bfloat16)
+    slot_part = jnp.dot(request_rows, w_both, preferred_element_type=jnp.float32)
     branches = pair_sum(slot_part, "gy", gy_pairs(gy_size))
-    branches = jnp.dot(to_request, branches, precision=lax.Precision.HIGHEST)
     hidden_out = (wide_in + branches + b_out + b_down).astype(jnp.bfloat16)
     return (hidden_out, new_keys, new_values)
 

time: 104 us -> 103 us (level)
  blocking collectives: 0 us -> 18.8 us
  waiting for transfers between devices: 47.3 us -> 37.4 us
  starting transfers between devices: 32.1 us -> 25.2 us
  other arithmetic: 11 us -> 9.43 us
    all_to_all x0 -> x1, blocking collectives: none -> 18.8 us  [layer(): lax.all_to_all(jnp.broadcast_to(both[None], (gx_size,) + both.shape), 'gx...]
    all_to_all x1 -> x0, waiting for transfers between devices: 9.91 us -> none  [layer(): lax.all_to_all(jnp.broadcast_to(both[None], (gx_size,) + both.shape), 'gx...]
    all_to_all x1 -> x0, starting transfers between devices: 6.88 us -> none  [layer(): lax.all_to_all(jnp.broadcast_to(both[None], (gx_size,) + both.shape), 'gx...]
    concatenate x1 -> x0, other arithmetic: 2.21 us -> none  [layer(): w_both = lax.optimization_barrier(jnp.concatenate([w_out, w_down], axis=0))]
    dot_general x2 -> x1, matrix products: 2.64 us -> 1.96 us  [layer(): jnp.dot(request_rows, w_both, preferred_element_type=jnp.float32)]
  transfers between devices with their start and end apart: 6 -> 5, of which waited for: 5 -> 4; matrix products, arithmetic and copies ran while one was open for 7% -> 5% of each run, Pallas kernels for 0% -> 0%
where the time goes in v13:
time: 103 us
  waiting for transfers between devices  37.4 us (36%)
  starting transfers between devices  25.2 us (24%)
  blocking collectives  18.8 us (18%)
  other arithmetic  9.43 us (9%)
  matrix products  5.77 us (6%)
  local copies, waits for them, and re-layouts  5.04 us (5%)
    all_to_all x1, waiting for transfers between devices, layer(): reduced = jnp.sum(lax.all_to_all(partial, 'gx', 0, 0, tiled=False), axis=0)  26.9 us
    all_to_all x1, blocking collectives, layer(): lax.all_to_all(jnp.broadcast_to(both[None], (gx_size,) + both.shape), 'gx...  18.8 us
    all_to_all x1, starting transfers between devices, exchange_sum(): return jnp.sum(lax.all_to_all(spread, axis, 0, 0, tiled=False), axis=0)  11.9 us
    ppermute x3, starting transfers between devices, pair_sum(): x = x + lax.ppermute(x, axis, pairs)  8.68 us
    all_to_all x1, waiting for transfers between devices, exchange_sum(): return jnp.sum(lax.all_to_all(spread, axis, 0, 0, tiled=False), axis=0)  7.8 us
    all_to_all x1, starting transfers between devices, layer(): reduced = jnp.sum(lax.all_to_all(partial, 'gx', 0, 0, tiled=False), axis=0)  4.66 us
    select_n x1, other arithmetic, layer(): new_values = jnp.where(at_row, new_value[:, :, None, :], value_cache)  3.96 us
    ppermute x3, waiting for transfers between devices, pair_sum(): x = x + lax.ppermute(x, axis, pairs)  2.72 us
  transfers between devices with their start and end apart: 5, of which 4 were waited for; matrix products, arithmetic and copies ran while one was open for 5% of the time, Pallas kernels for 0%

profile of v13, /device:TPU:1, one launch (start us, length us, event | category | flops | bytes accessed | tf_op | source)
XLA Modules:
  0.0 102.7 jit_solution(13090566630320053572)
XLA Ops:
  0.6 0.9 convert_reduce_fusion
  1.7 0.6 broadcast_in_dim.151
  2.3 11.9 %all-to-all-start = ((f32[32,1,128]{2,1,0:T(1,128)}), f32[32,1,128]{2,1,0:T(1,128)S(1)}, u32[]{:S(2)}, u32[]{:S(2)}) async-start(f32[32,1,128]{2,1,0:T(1,128)} %broadcast_in_dim.151), calls=%async_computation | async-start | bytes 32768 | tf_op jit(solution)/shard_map/all_to_all | solution.py:48
  14.2 0.7 iota_compare_fusion
  14.9 7.8 %all-to-all-done = f32[32,1,128]{2,1,0:T(1,128)S(1)} async-done(((f32[32,1,128]{2,1,0:T(1,128)}), f32[32,1,128]{2,1,0:T(1,128)S(1)}, u32[]{:S(2)}, u32[]{:S(2)}) %all-to-all-start) | async-done | bytes 16416 | tf_op jit(solution)/shard_map/all_to_all | solution.py:48
  22.8 0.1 select_reduce_fusion
  22.9 1.0 %add_convert_fusion.1 = (bf16[64,160]{1,0:T(8,128)(2,1)S(1)}, bf16[64,160]{1,0:T(8,128)(2,1)S(1)}) fusion(f32[160]{0:T(256)} %param.19, f32[160]{0:T(256)} %param.18, f32[160]{0:T(256)} %param.21, f32[160]{0:T(256)} %param.20, f32[64]{0:T(128)S(1)} %fusion.39, f32[64]{0:T(128)S(1)} %multiply_bitcast_fusion, bf16[64,160]{1,0:T(8,128)(2,1)} %param.17, ...), kind=kOutput, calls=%fused_computation.26 | convolution fusion | flops 1396736 | bytes 64768 | tf_op jit(solution)/shard_map/dot_general | solution.py:97
  24.0 1.3 %fusion.11 = f32[32,2,1920]{2,0,1:T(8,128)S(1)} fusion(bf16[160,1920]{1,0:T(8,128)(2,1)} %param.22, bf16[32,2,160]{2,1,0:T(2,128)(2,1)S(1)} %reshape.226), kind=kOutput, calls=%fused_computation.16 | convolution fusion | flops 39321600 | bytes 1126400 | tf_op jit(solution)/shard_map/sbk,kn->sbn/dot_general | solution.py:112
  25.3 0.3 fusion.9
  25.8 1.9 %copy.61 = f32[32,2,4480]{2,1,0:T(2,128)} copy(f32[32,2,4480]{2,0,1:T(8,128)S(1)} %pad_maximum_fusion) | data formatting | bytes 2293760 | tf_op jit(solution)/shard_map/concatenate | solution.py:110
  27.6 4.7 %all-to-all-start.1 = ((f32[32,2,4480]{2,1,0:T(2,128)}), f32[32,2,4480]{2,1,0:T(2,128)}, u32[]{:S(2)}, u32[]{:S(2)}) async-start(f32[32,2,4480]{2,1,0:T(2,128)} %copy.61), calls=%async_computation.1 | async-start | bytes 2293760 | tf_op jit(solution)/shard_map/all_to_all | solution.py:121
  32.3 0.1 select_reduce_fusion.1
  32.5 0.1 multiply_cosine_fusion
  32.7 26.9 %all-to-all-done.1 = f32[32,2,4480]{2,1,0:T(2,128)} async-done(((f32[32,2,4480]{2,1,0:T(2,128)}), f32[32,2,4480]{2,1,0:T(2,128)}, u32[]{:S(2)}, u32[]{:S(2)}) %all-to-all-start.1) | async-done | bytes 1146912 | tf_op jit(solution)/shard_map/all_to_all | solution.py:121
  59.6 1.6 %reduce_sum.77 = f32[2,4480]{1,0:T(2,128)S(1)} reduce(f32[32,2,4480]{2,1,0:T(2,128)} %all-to-all-done.1, f32[]{:T(128)} %constant.11.clone.1), dimensions={0}, to_apply=%region_5.6 | reduce | flops 277760 | bytes 1182724 | tf_op jit(solution)/shard_map/reduce_sum | solution.py:121
  61.4 0.2 fusion.26
  61.8 0.2 fusion.33
  62.0 0.8 fusion.34
  62.8 0.3 convert_reduce_fusion.1
  63.1 0.4 fusion.19
  63.6 0.1 fusion.37
  63.7 0.2 broadcast_in_dim.158
  63.9 18.8 %all_to_all.16 = bf16[32,2,3200]{2,1,0:T(2,128)(2,1)} all-to-all(bf16[32,2,3200]{2,1,0:T(2,128)(2,1)S(1)} %broadcast_in_dim.158), channel_id=1, replica_groups=mesh['gx'=32,'gy'=8] {'gx'}, dimensions={0} | all-to-all | bytes 819200 | tf_op jit(solution)/shard_map/all_to_all | solution.py:156
  82.7 1.9 %reshape.230 = bf16[64,3200]{1,0:T(8,128)(2,1)} reshape(bf16[32,2,3200]{2,1,0:T(2,128)(2,1)} %all_to_all.16) | data formatting | bytes 819200 | tf_op jit(solution)/shard_map/reshape | solution.py:161
  84.6 2.0 %fusion.1 = f32[64,160]{1,0:T(8,128)S(1)} fusion(bf16[64,3200]{1,0:T(8,128)(2,1)} %reshape.230, bf16[2560,160]{0,1:T(8,128)(2,1)} %param.28, bf16[640,160]{0,1:T(8,128)(2,1)} %param.24, s32[64]{0:T(128)S(1)} %copy-done.8), kind=kOutput, calls=%fused_computation.4 | convolution fusion | flops 94007296 | bytes 1474816 | tf_op jit(solution)/shard_map/dot_general | solution.py:164
  86.6 4.5 %collective-permute-start = (f32[64,160]{1,0:T(8,128)S(1)}, f32[64,160]{1,0:T(8,128)S(1)}, u32[]{:S(2)}, u32[]{:S(2)}) collective-permute-start(f32[64,160]{1,0:T(8,128)S(1)} %fusion.1), channel_id=1, source_target_pairs={{0,1},{1,0},{2,3},{3,2},{4,5},{5,4},{6,7},{7,6},{8,9},{9,8},{10,11... | collective-permute-start | bytes 122888 | tf_op jit(solution)/shard_map/ppermute | solution.py:53
  91.1 0.9 collective-permute-done
  92.0 1.4 %collective-permute-start.1 = (f32[64,160]{1,0:T(8,128)S(1)}, f32[64,160]{1,0:T(8,128)S(1)}, u32[]{:S(2)}, u32[]{:S(2)}) collective-permute-start(f32[64,160]{1,0:T(8,128)S(1)} %add.97), channel_id=1, source_target_pairs={{0,2},{1,3},{2,0},{3,1},{4,6},{5,7},{6,4},{7,5},{8,10},{9,11},{10,... | collective-permute-start | bytes 122888 | tf_op jit(solution)/shard_map/ppermute | solution.py:53
  93.4 1.8 %collective-permute-done.1 = f32[64,160]{1,0:T(8,128)S(1)} collective-permute-done((f32[64,160]{1,0:T(8,128)S(1)}, f32[64,160]{1,0:T(8,128)S(1)}, u32[]{:S(2)}, u32[]{:S(2)}) %collective-permute-start.1) | collective-permute-done | bytes 40992 | tf_op jit(solution)/shard_map/ppermute | solution.py:53
  95.2 2.8 %collective-permute-start.2 = (f32[64,160]{1,0:T(8,128)S(1)}, f32[64,160]{1,0:T(8,128)S(1)}, u32[]{:S(2)}, u32[]{:S(2)}) collective-permute-start(f32[64,160]{1,0:T(8,128)S(1)} %add.98), channel_id=1, source_target_pairs={{0,6},{1,7},{2,4},{3,5},{4,2},{5,3},{6,0},{7,1},{8,14},{9,15},{10,... | collective-permute-start | bytes 122888 | tf_op jit(solution)/shard_map/ppermute | solution.py:53
  98.0 4.0 %broadcast_select_fusion = (bf16[2,5,1024,128]{3,2,1,0:T(8,128)(2,1)}, bf16[2,5,1024,128]{3,2,1,0:T(8,128)(2,1)}) fusion(bf16[2,5,1024,128]{3,2,1,0:T(8,128)(2,1)} %param.31, pred[2,1024]{1,0:T(4,128)(4,1)S(1)} %get-tuple-element.32, bf16[2,5,128]{2,1,0:T(8,128)(2,1)S(1)} %copy.66, bf16[2,5,1024,128]{3,2,1,0:T(8,128)(2,1)S(1)} %copy-done.1, ...), kind=kLoop, calls=%fused_computation.2 | loop fusion | flops 2621440 | bytes 10492928 | tf_op jit(solution)/shard_map/jit(_where)/select_n | solution.py:154
  102.0 0.6 fusion.16
  (48 shorter events, 0.9 us)
Async XLA Ops:
  0.6 24.7 %copy-start = (bf16[160,2560]{1,0:T(8,128)(2,1)S(1)}, bf16[160,2560]{1,0:T(8,128)(2,1)}, u32[]{:S(2)}) copy-start(bf16[160,2560]{1,0:T(8,128)(2,1)} %param.26) | copy-start | bytes 2457604
  2.3 20.4 %all-to-all-start = ((f32[32,1,128]{2,1,0:T(1,128)}), f32[32,1,128]{2,1,0:T(1,128)S(1)}, u32[]{:S(2)}, u32[]{:S(2)}) async-start(f32[32,1,128]{2,1,0:T(1,128)} %broadcast_in_dim.151), calls=%async_computation | async-start | bytes 32768 | tf_op jit(solution)/shard_map/all_to_all | solution.py:48
  25.7 6.6 %copy-start.8 = (s32[64]{0:T(128)S(1)}, s32[64]{0:T(128)}, u32[]{:S(2)}) copy-start(s32[64]{0:T(128)} %param.33) | copy-start | bytes 772
  25.7 6.6 %copy-start.9 = (s32[64]{0:T(128)S(1)}, s32[64]{0:T(128)}, u32[]{:S(2)}) copy-start(s32[64]{0:T(128)} %param.32) | copy-start | bytes 772
  25.7 35.5 %copy-start.5 = (f32[1920]{0:T(1024)S(1)}, f32[1920]{0:T(1024)}, u32[]{:S(2)}) copy-start(f32[1920]{0:T(1024)} %param.23) | copy-start | bytes 23044
  25.7 35.6 %copy-start.4 = (f32[2560]{0:T(1024)S(1)}, f32[2560]{0:T(1024)}, u32[]{:S(2)}) copy-start(f32[2560]{0:T(1024)} %param.27) | copy-start | bytes 30724
  25.7 36.2 %copy-start.1 = (bf16[2,5,1024,128]{3,2,1,0:T(8,128)(2,1)S(1)}, bf16[2,5,1024,128]{3,2,1,0:T(8,128)(2,1)}, u32[]{:S(2)}) copy-start(bf16[2,5,1024,128]{3,2,1,0:T(8,128)(2,1)} %param.30) | copy-start | bytes 7864324
  27.6 32.0 %all-to-all-start.1 = ((f32[32,2,4480]{2,1,0:T(2,128)}), f32[32,2,4480]{2,1,0:T(2,128)}, u32[]{:S(2)}, u32[]{:S(2)}) async-start(f32[32,2,4480]{2,1,0:T(2,128)} %copy.61), calls=%async_computation.1 | async-start | bytes 2293760 | tf_op jit(solution)/shard_map/all_to_all | solution.py:121
  61.3 1.8 %copy-start.2 = (bf16[2,5,1024,128]{3,2,1,0:T(8,128)(2,1)S(1)}, bf16[2,5,1024,128]{3,2,1,0:T(8,128)(2,1)}, u32[]{:S(2)}) copy-start(bf16[2,5,1024,128]{3,2,1,0:T(8,128)(2,1)} %param.31) | copy-start | bytes 7864324
  86.6 5.4 %collective-permute-start = (f32[64,160]{1,0:T(8,128)S(1)}, f32[64,160]{1,0:T(8,128)S(1)}, u32[]{:S(2)}, u32[]{:S(2)}) collective-permute-start(f32[64,160]{1,0:T(8,128)S(1)} %fusion.1), channel_id=1, source_target_pairs={{0,1},{1,0},{2,3},{3,2},{4,5},{5,4},{6,7},{7,6},{8,9},{9,8},{10,11... | collective-permute-start | bytes 122888 | tf_op jit(solution)/shard_map/ppermute | solution.py:53
  92.0 3.2 %collective-permute-start.1 = (f32[64,160]{1,0:T(8,128)S(1)}, f32[64,160]{1,0:T(8,128)S(1)}, u32[]{:S(2)}, u32[]{:S(2)}) collective-permute-start(f32[64,160]{1,0:T(8,128)S(1)} %add.97), channel_id=1, source_target_pairs={{0,2},{1,3},{2,0},{3,1},{4,6},{5,7},{6,4},{7,5},{8,10},{9,11},{10,... | collective-permute-start | bytes 122888 | tf_op jit(solution)/shard_map/ppermute | solution.py:53
  95.2 6.8 %copy-start.3 = (bf16[64,160]{1,0:T(8,128)(2,1)S(1)}, bf16[64,160]{1,0:T(8,128)(2,1)}, u32[]{:S(2)}) copy-start(bf16[64,160]{1,0:T(8,128)(2,1)} %param.17) | copy-start | bytes 61444
  95.2 6.8 %copy-start.6 = (f32[160]{0:T(256)S(1)}, f32[160]{0:T(256)}, u32[]{:S(2)}) copy-start(f32[160]{0:T(256)} %param.29) | copy-start | bytes 1924
  95.2 6.8 %copy-start.7 = (f32[160]{0:T(256)S(1)}, f32[160]{0:T(256)}, u32[]{:S(2)}) copy-start(f32[160]{0:T(256)} %param.25) | copy-start | bytes 1924
  95.2 6.8 %collective-permute-start.2 = (f32[64,160]{1,0:T(8,128)S(1)}, f32[64,160]{1,0:T(8,128)S(1)}, u32[]{:S(2)}, u32[]{:S(2)}) collective-permute-start(f32[64,160]{1,0:T(8,128)S(1)} %add.98), channel_id=1, source_target_pairs={{0,6},{1,7},{2,4},{3,5},{4,2},{5,3},{6,0},{7,1},{8,14},{9,15},{10,... | collective-permute-start | bytes 122888 | tf_op jit(solution)/shard_map/ppermute | solution.py:53
